TPU v7x, 32 devices: a whole 2x2x4 slice. The times are simulated.
32 devices in a mesh: grp: 2 (over y), tm: 4 (over z), col: 4 (over x, core).
Axes of the slice: x: 2, y: 2, z: 4, core: 2. Of those that a mesh axis runs over, the one named last changes fastest.
Arguments:
- amplitudes: float32 [8, 8], P('grp', 'tm'), parts along dimension 0, may hold values from -1 to 1
- drift: float32 [2, 256, 256], replicated, may hold values from -0.1875 to 0.1875
- controls: float32 [4, 2, 256, 256], replicated, may hold values from -0.1875 to 0.1875
- target: float32 [4, 256, 256], P('grp'), parts along dimension 0, may hold values from -0.25 to 0.25
Outputs:
- gradient: float32 [8, 8], P('grp', 'tm'), parts along dimension 0
- propagators: float32 [16, 2, 256, 256], P(('grp', 'tm'), None, None, 'col'), parts along dimension 0
There are 2 independent parts, one for each index of `grp`. A program takes and returns all parts, laid end to end along the dimension named above; an argument that names none is the same for every part. Nothing has to cross between parts.
All inputs are finite; a program needn't handle non-finite values.
Results may differ from a plain program's by a relative error of at most 0.0003.
Values sent between devices are 32-bit elements; how exact they have to be, the bound alone decides.
No kernel may reach another device: no remote copies, remote signals or barrier semaphores. Data moves between devices by JAX's collectives and lax.ppermute only.
A program may use at most 64 MiB of HBM per device.

v0:
```python
import jax
import jax.numpy as jnp
from jax import lax
from jax.sharding import PartitionSpec as P

TAYLOR = 8

fast_mode = lax.Precision.HIGHEST


def mm(left, right):
    return jnp.matmul(left, right, precision=fast_mode)


def mm_nt(left, right):
    return jnp.einsum("...ij,...kj->...ik", left, right, precision=fast_mode)


def mm_tn(left, right):
    return jnp.einsum("...ji,...jk->...ik", left, right, precision=fast_mode)


def cmul(a, b):
    size = a.shape[-2]
    stacked = a.reshape(a.shape[:-3] + (2 * size, a.shape[-1]))
    with_real = mm(stacked, b[..., 0, :, :])
    with_imag = mm(stacked, b[..., 1, :, :])
    real = with_real[..., :size, :] - with_imag[..., size:, :]
    imag = with_imag[..., :size, :] + with_real[..., size:, :]
    return jnp.stack([real, imag], -3)


def cmul_adjoint_right(a, b):
    size = a.shape[-2]
    stacked = a.reshape(a.shape[:-3] + (2 * size, a.shape[-1]))
    with_real = mm_nt(stacked, b[..., 0, :, :])
    with_imag = mm_nt(stacked, b[..., 1, :, :])
    real = with_real[..., :size, :] + with_imag[..., size:, :]
    imag = with_real[..., size:, :] - with_imag[..., :size, :]
    return jnp.stack([real, imag], -3)


def cmul_adjoint_left(a, b):
    ar, ai = a[..., 0, :, :], a[..., 1, :, :]
    br, bi = b[..., 0, :, :], b[..., 1, :, :]
    return jnp.stack([mm_tn(ar, br) + mm_tn(ai, bi), mm_tn(ar, bi) - mm_tn(ai, br)], -3)


def taylor_propagators(ham):
    size = ham.shape[-1]
    eye = jnp.eye(size, dtype=jnp.float32)
    gen = jnp.stack([ham[:, 1], -ham[:, 0]], 1)
    gen2 = cmul(gen, gen)
    both = cmul(jnp.stack([gen, gen2], 0), gen2[None])
    gen3, gen4 = both[0], both[1]
    coef = [1.0]
    for order in range(1, TAYLOR + 1):
        coef.append(coef[-1] / order)
    low = coef[1] * gen + coef[2] * gen2 + coef[3] * gen3
    low = low.at[:, 0].add(coef[0] * eye)
    high = coef[5] * gen + coef[6] * gen2 + coef[7] * gen3 + coef[8] * gen4
    high = high.at[:, 0].add(coef[4] * eye)
    return low + cmul(gen4, high)


def shards(amplitudes, drift, controls, target):
    size = drift.shape[-1]
    tm_count = lax.axis_size("tm")
    tm_index = lax.axis_index("tm")
    col_count = lax.axis_size("col")
    col_width = size // col_count
    col_start = lax.axis_index("col") * col_width
    local_count = amplitudes.shape[1]
    exact = lax.Precision.HIGHEST

    raw = drift[None] + jnp.sum(amplitudes[:, :, None, None, None] * controls[:, None], axis=0)
    ham = jnp.stack(
        [0.5 * (raw[:, 0] + jnp.swapaxes(raw[:, 0], 1, 2)), 0.5 * (raw[:, 1] - jnp.swapaxes(raw[:, 1], 1, 2))], 1
    )
    steps = taylor_propagators(ham)

    running = [steps[0]]
    for position in range(1, local_count):
        running.append(cmul(steps[position][None], running[-1][None])[0])
    block_total = running[-1]
    split = 2 if col_count % 2 == 0 else 1
    if split == 2:
        half = size // 2
        col_index = lax.axis_index("col")
        part = col_index % 2
        mine = lax.all_gather(lax.dynamic_slice_in_dim(block_total, part * half, half, 1), "tm")
        theirs = lax.ppermute(mine, "col", [(i, i ^ 1) for i in range(col_count)])
        upper = jnp.where(part == 0, mine, theirs)
        lower = jnp.where(part == 0, theirs, mine)
        pieces = jnp.concatenate([upper, lower], 2)
    else:
        pieces = lax.all_gather(block_total, "tm")

    eye = jnp.eye(size, dtype=jnp.float32)
    start_full = jnp.stack([eye, jnp.zeros_like(eye)])
    if tm_count <= 8:
        scan = pieces
        shift = 1
        while shift < tm_count:
            later = cmul(scan[shift:], scan[:-shift])
            scan = jnp.concatenate([scan[:shift], later], 0)
            shift *= 2
        final_state = scan[-1]
        earlier = lax.dynamic_index_in_dim(scan, jnp.maximum(tm_index - 1, 0), 0, keepdims=False)
        prefix = jnp.where(tm_index == 0, start_full, earlier)
    else:

        def lap(carry, piece):
            total, prefix, position = carry
            prefix = jnp.where(position == tm_index, total, prefix)
            total = cmul(piece[None], total[None])[0]
            return (total, prefix, position + 1), None

        (final_state, prefix, _), _ = lax.scan(lap, (start_full, start_full, 0), pieces)
    states = cmul(jnp.stack(running, 0), prefix[None])

    correlation_real = jnp.sum(target[0] * final_state[0] + target[1] * final_state[1])
    correlation_imag = jnp.sum(target[0] * final_state[1] - target[1] * final_state[0])
    overlap = cmul_adjoint_left(target, final_state)
    weighted = cmul_adjoint_right(cmul(states, overlap[None]), states)
    control_real = (0.5 * (controls[:, 0] + jnp.swapaxes(controls[:, 0], 1, 2)))[:, None]
    control_imag = (0.5 * (controls[:, 1] - jnp.swapaxes(controls[:, 1], 1, 2)))[:, None]
    trace_real = jnp.sum(control_real * weighted[None, :, 0] + control_imag * weighted[None, :, 1], axis=(2, 3))
    trace_imag = jnp.sum(control_real * weighted[None, :, 1] - control_imag * weighted[None, :, 0], axis=(2, 3))
    gradient = correlation_real * trace_imag - correlation_imag * trace_real
    propagators = lax.dynamic_slice_in_dim(states, col_start, col_width, 3)
    return (gradient, propagators)


def solution(mesh):
    in_specs = (P("grp", "tm"), P(), P(), P("grp", None, None))
    out_specs = (P("grp", "tm"), P(("grp", "tm"), None, None, "col"))
    return jax.shard_map(shards, mesh=mesh, in_specs=in_specs, out_specs=out_specs, check_vma=False)
```

profile of v0, /device:TPU:13, one launch (start us, length us, event | category | flops | bytes accessed | tf_op | source)
XLA Modules:
  0.0 98.8 jit_solution(11340203302989472993)
XLA Ops:
  7.2 0.8 copy.49
  8.0 2.1 %multiply_reduce_fusion = f32[2,2,256,256]{3,2,1,0:T(8,128)S(1)} fusion(f32[4,2,256,256]{3,2,1,0:T(8,128)} %param.10, f32[4,2]{1,0:T(4,128)S(1)} %copy.49), kind=kLoop, calls=%fused_computation | loop fusion | flops 1835008 | bytes 3145760 | tf_op jit(solution)/shard_map/reduce_sum | solution.py:76
  10.1 0.3 copy.50
  10.4 0.2 copy.48
  10.8 0.2 copy.52
  11.1 0.2 copy.53
  11.8 1.1 %fusion.77 = f32[2,512,256]{2,1,0:T(8,128)S(1)} fusion(f32[2,512,256]{2,1,0:T(8,128)S(1)} %bitcast.232, f32[2,256,256]{2,1,0:T(8,128)S(1)} %copy.51, f32[2,2,256,256]{2,3,0,1:T(8,128)S(1)} %broadcast_add_fusion), kind=kOutput, calls=%fused_computation.158 | convolution fusion | flops 805568512 | bytes 3145728 | tf_op jit(solution)/shard_map/dot_general | solution.py:12
  12.9 1.1 %fusion.50 = f32[2,512,256]{2,1,0:T(8,128)S(1)} fusion(f32[2,512,256]{2,1,0:T(8,128)S(1)} %bitcast.233, f32[2,256,256]{2,1,0:T(8,128)S(1)} %copy.53), kind=kOutput, calls=%fused_computation.115 | convolution fusion | flops 805568512 | bytes 2621440 | tf_op jit(solution)/shard_map/dot_general | solution.py:12
  14.4 2.0 %fusion.6 = f32[2,2,512,256]{3,2,1,0:T(8,128)S(1)} fusion(f32[1,2,2,256,256]{4,3,1,2,0:T(8,128)S(1)} %get-tuple-element.65, f32[1,2,512,256]{3,2,0,1:T(8,128)S(1)} %bitcast.248, f32[1,2,512,256]{3,2,0,1:T(8,128)S(1)} %bitcast.234), kind=kOutput, calls=%fused_computation.24 | convolution fusion | flops 1611137024 | bytes 4718592 | tf_op jit(solution)/shard_map/dot_general | solution.py:12
  16.4 2.0 %fusion.9 = f32[2,2,512,256]{3,2,1,0:T(8,128)S(1)} fusion(f32[1,2,2,256,256]{4,3,1,2,0:T(8,128)S(1)} %get-tuple-element.65, f32[1,2,512,256]{3,2,0,1:T(8,128)S(1)} %bitcast.249, f32[1,2,512,256]{3,2,0,1:T(8,128)S(1)} %bitcast.235), kind=kOutput, calls=%fused_computation.25 | convolution fusion | flops 1611137024 | bytes 4718592 | tf_op jit(solution)/shard_map/dot_general | solution.py:12
  18.4 0.3 fusion.17
  18.7 0.4 bitcast_add_fusion.1
  19.3 1.1 %fusion.42 = f32[2,512,256]{2,1,0:T(8,128)S(1)} fusion(f32[2,512,256]{2,1,0:T(8,128)S(1)} %bitcast.246, f32[2,2,256,256]{3,2,0,1:T(8,128)S(1)} %get-tuple-element.36), kind=kOutput, calls=%fused_computation.91 | convolution fusion | flops 805306368 | bytes 2621440 | tf_op jit(solution)/shard_map/dot_general | solution.py:12
  20.4 1.1 %fusion.44 = f32[2,512,256]{2,1,0:T(8,128)S(1)} fusion(f32[2,512,256]{2,1,0:T(8,128)S(1)} %bitcast.247, f32[2,2,256,256]{3,2,0,1:T(8,128)S(1)} %get-tuple-element.36, f32[256,256]{1,0:T(8,128)S(1)} %fusion.70), kind=kOutput, calls=%fused_computation.94 | convolution fusion | flops 805437440 | bytes 2883584 | tf_op jit(solution)/shard_map/dot_general | solution.py:12
  22.0 0.8 convolution_bitcast_fusion.1
  22.7 0.6 convolution_bitcast_fusion
  23.4 0.7 fusion.52
  24.2 28.9 %all-gather.2.cloned.1.call-done = f32[4,2,128,256]{3,2,0,1:T(8,128)} async-done(((f32[1,2,128,256]{3,2,0,1:T(8,128)}), f32[4,2,128,256]{3,2,0,1:T(8,128)}) %all-gather.2.cloned.1.call-update) | async-done | bytes 1048592 | tf_op jit(solution)/shard_map/all_gather | solution.py:91
  53.1 0.9 collective-permute-start
  54.2 1.4 %copy-done = f32[4,2,256,256]{3,2,1,0:T(8,128)S(1)} copy-done((f32[4,2,256,256]{3,2,1,0:T(8,128)S(1)}, f32[4,2,256,256]{3,2,1,0:T(8,128)}, u32[]{:S(2)}) %copy-start) | copy-done | bytes 2097176
  55.6 1.6 %fusion.89 = (f32[4,1,256,256]{3,2,1,0:T(8,128)}, f32[4,256,256]{2,1,0:T(8,128)}) fusion(f32[4,2,256,256]{3,2,1,0:T(8,128)S(1)} %copy-done), kind=kLoop, calls=%fused_computation.170 | loop fusion | bytes 4194304 | tf_op jit(solution)/shard_map/slice | solution.py:126
  57.2 2.5 %copy.73 = f32[4,256,256]{1,2,0:T(8,128)} copy(f32[4,256,256]{2,1,0:T(8,128)} %get-tuple-element.46) | data formatting | bytes 2097152 | tf_op jit(solution)/shard_map/squeeze | solution.py:127
  59.7 2.5 %copy.83 = f32[4,1,256,256]{2,3,0,1:T(8,128)} copy(f32[4,1,256,256]{3,2,1,0:T(8,128)} %get-tuple-element.45) | data formatting | bytes 2097152
  62.3 3.2 %fusion.18 = (f32[4,256,256]{2,1,0:T(8,128)}, f32[4,256,256]{2,1,0:T(8,128)}) fusion(f32[4,1,256,256]{2,3,0,1:T(8,128)} %copy.83, f32[4,2,256,256]{3,2,1,0:T(8,128)S(1)} %copy-done, f32[4,256,256]{1,2,0:T(8,128)} %copy.73), kind=kLoop, calls=%fused_computation.49 | loop fusion | flops 1048576 | bytes 6291456 | tf_op jit(solution)/shard_map/mul | solution.py:126
  65.5 1.4 %broadcast_select_fusion = (f32[4,2,128,256]{3,2,0,1:T(8,128)S(1)}, f32[4,2,128,256]{3,2,0,1:T(8,128)S(1)}) fusion(f32[4,2,128,256]{3,2,0,1:T(8,128)} %collective-permute-done, f32[4,2,128,256]{3,2,0,1:T(8,128)S(1)} %copy-done.5, pred[]{:T(512)S(6)} %eq.24), kind=kLoop, calls=%fused_computation.112 | loop fusion | flops 524288 | bytes 4194305 | tf_op jit(solution)/shard_map/jit(_where)/select_n | solution.py:94
  67.2 1.5 %fusion.26 = f32[3,512,256]{2,1,0:T(8,128)S(1)} fusion(f32[3,512,256]{2,1,0:T(8,128)S(1)} %bitcast.236, f32[4,2,128,256]{3,2,0,1:T(8,128)S(1)} %get-tuple-element.56, f32[4,2,128,256]{3,2,0,1:T(8,128)S(1)} %get-tuple-element.55), kind=kOutput, calls=%fused_computation.61 | convolution fusion | flops 1208156160 | bytes 5242880 | tf_op jit(solution)/shard_map/dot_general | solution.py:12
  68.7 1.5 %fusion.22 = f32[3,512,256]{2,1,0:T(8,128)S(1)} fusion(f32[3,512,256]{2,1,0:T(8,128)S(1)} %bitcast.237, f32[4,2,128,256]{3,2,0,1:T(8,128)S(1)} %get-tuple-element.56, f32[4,2,128,256]{3,2,0,1:T(8,128)S(1)} %get-tuple-element.55), kind=kOutput, calls=%fused_computation.58 | convolution fusion | flops 1208156160 | bytes 5242880 | tf_op jit(solution)/shard_map/dot_general | solution.py:12
  70.3 0.3 fusion.29
  70.9 1.1 %fusion.38 = f32[2,512,256]{2,1,0:T(8,128)S(1)} fusion(f32[2,512,256]{2,1,0:T(8,128)S(1)} %bitcast.244, f32[4,2,256,256]{3,2,0,1:T(8,128)S(1)} %fusion.1), kind=kOutput, calls=%fused_computation.83 | convolution fusion | flops 805306368 | bytes 2621440 | tf_op jit(solution)/shard_map/dot_general | solution.py:12
  71.9 1.1 %fusion.39 = f32[2,512,256]{2,1,0:T(8,128)S(1)} fusion(f32[2,512,256]{2,1,0:T(8,128)S(1)} %bitcast.245, f32[4,2,256,256]{3,2,0,1:T(8,128)S(1)} %fusion.1), kind=kOutput, calls=%fused_computation.85 | convolution fusion | flops 805306368 | bytes 2621440 | tf_op jit(solution)/shard_map/dot_general | solution.py:12
  73.2 1.1 %slice-done = f32[2,2,256,256]{3,2,0,1:T(8,128)S(1)} async-done(((f32[4,2,256,256]{3,2,0,1:T(8,128)}), f32[2,2,256,256]{3,2,0,1:T(8,128)S(1)}, s32[]{:S(2)}) %slice-start) | async-done | bytes 1048600 | tf_op jit(solution)/shard_map/slice | solution.py:105
  74.4 1.0 fusion.56
  75.4 1.0 fusion.55
  76.4 0.7 fusion.62
  77.1 0.6 fusion.67
  77.7 0.6 fusion.65
  78.3 0.8 fusion.14
  79.1 0.6 fusion.13
  80.1 1.0 %fusion.54 = f32[2,512,256]{2,1,0:T(8,128)S(1)} fusion(f32[2,512,256]{2,1,0:T(8,128)S(1)} %bitcast.242, f32[1,2,256,256]{2,3,1,0:T(8,128)S(1)} %maximum_bitcast_fusion), kind=kOutput, calls=%fused_computation.121 | convolution fusion | flops 805306368 | bytes 2359296 | tf_op jit(solution)/shard_map/dot_general | solution.py:12
  81.1 1.0 %fusion.53 = f32[2,512,256]{2,1,0:T(8,128)S(1)} fusion(f32[2,512,256]{2,1,0:T(8,128)S(1)} %bitcast.243, f32[1,2,256,256]{2,3,1,0:T(8,128)S(1)} %maximum_bitcast_fusion), kind=kOutput, calls=%fused_computation.119 | convolution fusion | flops 805306368 | bytes 2359296 | tf_op jit(solution)/shard_map/dot_general | solution.py:12
  82.5 1.1 %fusion.80 = f32[2,512,256]{2,1,0:T(8,128)S(1)} fusion(f32[2,512,256]{2,1,0:T(8,128)S(1)} %bitcast.238, f32[2,512,256]{2,1,0:T(8,128)S(1)} %fusion.55, f32[2,512,256]{2,1,0:T(8,128)S(1)} %fusion.56), kind=kOutput, calls=%fused_computation.160 | convolution fusion | flops 805437440 | bytes 3145728 | tf_op jit(solution)/shard_map/...ij,...kj->...ik/dot_general | solution.py:16
  83.6 1.1 %fusion.82 = f32[2,512,256]{2,1,0:T(8,128)S(1)} fusion(f32[2,512,256]{2,1,0:T(8,128)S(1)} %bitcast.239, f32[2,512,256]{2,1,0:T(8,128)S(1)} %fusion.56, f32[2,512,256]{2,1,0:T(8,128)S(1)} %fusion.55), kind=kOutput, calls=%fused_computation.162 | convolution fusion | flops 805437440 | bytes 3145728 | tf_op jit(solution)/shard_map/...ij,...kj->...ik/dot_general | solution.py:16
  84.7 1.0 %fusion.30 = f32[2,2,256,64]{3,2,0,1:T(8,128)} fusion(s32[]{:T(128)S(6)} %select_n.42, f32[2,1,256,256]{3,2,0,1:T(8,128)S(1)} %get-tuple-element.51, f32[2,1,256,256]{3,2,0,1:T(8,128)S(1)} %get-tuple-element.52), kind=kLoop, calls=%fused_computation.66 | loop fusion | flops 65536 | bytes 1310724 | tf_op jit(solution)/shard_map/stack | solution.py:30
  85.7 2.0 %copy.75 = f32[2,2,256,64]{2,3,1,0:T(8,128)} copy(f32[2,2,256,64]{3,2,0,1:T(8,128)} %fusion.30) | data formatting | bytes 524288
  87.8 1.1 %copy-done.4 = f32[4,256,256]{2,1,0:T(8,128)S(1)} copy-done((f32[4,256,256]{2,1,0:T(8,128)S(1)}, f32[4,256,256]{2,1,0:T(8,128)}, u32[]{:S(2)}) %copy-start.4) | copy-done | bytes 1048600
  88.9 1.1 %subtract_reduce_fusion = (f32[4,2]{1,0:T(4,128)S(1)}, f32[4,2]{1,0:T(4,128)S(1)}) fusion(f32[2,256,256]{2,1,0:T(8,128)S(1)} %get-tuple-element.48, f32[4,256,256]{2,1,0:T(8,128)S(1)} %copy-done.4, f32[2,256,256]{2,1,0:T(8,128)S(1)} %get-tuple-element.47, f32[4,256,256]{2,1,0:T(8,128)S(1)} %copy-done.3), kind=kLoop, calls=%fused_computation.19 | loop fusion | flops 4194288 | bytes 3145792 | tf_op jit(solution)/shard_map/reduce_sum | solution.py:129
  90.0 1.3 %multiply_subtract_fusion = f32[4,2]{1,0:T(4,128)S(1)} fusion(f32[4,2]{1,0:T(4,128)S(1)} %get-tuple-element.33, f32[4,2]{1,0:T(4,128)S(1)} %get-tuple-element.32, f32[]{:T(128)} %get-tuple-element.35, f32[]{:T(128)} %get-tuple-element.34), kind=kLoop, calls=%fused_computation.164 | loop fusion | flops 24 | bytes 104 | tf_op jit(solution)/shard_map/sub | solution.py:130
  91.3 0.6 copy.74
  (52 shorter events, 3.5 us)
Async XLA Ops:
  7.2 45.9 %all-gather.2.cloned.1.call-start = ((), (), s32[]{:S(2)}) async-start(), calls=%async_computation | async-start | bytes 1310720 | tf_op jit(solution)/shard_map/all_gather | solution.py:91
  8.0 2.4 %copy-start.6 = (f32[2,256,256]{2,1,0:T(8,128)S(1)}, f32[2,256,256]{2,1,0:T(8,128)}, u32[]{:S(2)}) copy-start(f32[2,256,256]{2,1,0:T(8,128)} %param.9) | copy-start | bytes 1572868
  53.1 12.4 %collective-permute-start = (f32[4,2,128,256]{3,2,0,1:T(8,128)}, f32[4,2,128,256]{3,2,0,1:T(8,128)}, u32[]{:S(2)}, u32[]{:S(2)}) collective-permute-start(f32[4,2,128,256]{3,2,0,1:T(8,128)} %all-gather.2.cloned.1.call-done), channel_id=1, source_target_pairs={{0,1},{1,0},{2,3},{3,2},{4,5},{5,4},{6,7},{7,6},{8,9},{9,8},{10,11... | collective-permute-start | bytes 3145736 | tf_op jit(solution)/shard_map/ppermute | solution.py:92
  54.0 1.6 %copy-start = (f32[4,2,256,256]{3,2,1,0:T(8,128)S(1)}, f32[4,2,256,256]{3,2,1,0:T(8,128)}, u32[]{:S(2)}) copy-start(f32[4,2,256,256]{3,2,1,0:T(8,128)} %param.10) | copy-start | bytes 6291460
  62.3 3.2 %copy-start.5 = (f32[4,2,128,256]{3,2,0,1:T(8,128)S(1)}, f32[4,2,128,256]{3,2,0,1:T(8,128)}, u32[]{:S(2)}) copy-start(f32[4,2,128,256]{3,2,0,1:T(8,128)} %all-gather.2.cloned.1.call-done) | copy-start | bytes 3145732
  70.8 2.3 %copy-start.1 = (f32[4,2,256,256]{3,2,0,1:T(8,128)}, f32[4,2,256,256]{3,2,0,1:T(8,128)S(1)}, u32[]{:S(2)}) copy-start(f32[4,2,256,256]{3,2,0,1:T(8,128)S(1)} %fusion.1) | copy-start | bytes 6291460
  73.0 1.2 %slice-start = ((f32[4,2,256,256]{3,2,0,1:T(8,128)}), f32[2,2,256,256]{3,2,0,1:T(8,128)S(1)}, s32[]{:S(2)}) async-start(f32[4,2,256,256]{3,2,0,1:T(8,128)} %copy-done.1), calls=%async_computation.1 | async-start | bytes 2097152 | tf_op jit(solution)/shard_map/slice | solution.py:105
  74.4 2.0 %copy-start.2 = (f32[2,256,256]{2,1,0:T(8,128)S(1)}, f32[2,256,256]{2,1,0:T(8,128)}, u32[]{:S(2)}) copy-start(f32[2,256,256]{2,1,0:T(8,128)} %param.11) | copy-start | bytes 1572868
  85.7 2.2 %copy-start.3 = (f32[4,256,256]{2,1,0:T(8,128)S(1)}, f32[4,256,256]{2,1,0:T(8,128)}, u32[]{:S(2)}) copy-start(f32[4,256,256]{2,1,0:T(8,128)} %get-tuple-element.43) | copy-start | bytes 3145732
  87.7 1.2 %copy-start.4 = (f32[4,256,256]{2,1,0:T(8,128)S(1)}, f32[4,256,256]{2,1,0:T(8,128)}, u32[]{:S(2)}) copy-start(f32[4,256,256]{2,1,0:T(8,128)} %get-tuple-element.44) | copy-start | bytes 3145732
Sparse Core Ops, SparseCore 0:
  24.3 28.7 all-gather.1
where the time goes:
time: 100 us; the launch traced here: 98.8 us
  waiting for transfers between devices  29 us (29%)
  matrix products  23.7 us (24%)
  local copies, waits for them, and re-layouts  15.6 us (16%)
  other arithmetic  15 us (15%)
  between operations  14.6 us (15%)
    all_gather x1, waiting for transfers between devices, shards(): lax.all_gather(lax.dynamic_slice_in_dim(block_total, part * half, half, 1...  28.9 us
    dot_general x16, matrix products, mm(): return jnp.matmul(left, right, precision=fast_mode)  18.9 us
    unnamed x19, local copies, waits for them, and re-layouts  8.69 us
    mul x1, other arithmetic, shards(): 0.5 * (controls[:, 0] + jnp.swapaxes(controls[:, 0], 1, 2))  3.21 us
    another operation x12, other arithmetic, cmul(): return jnp.stack([real, imag], -3)  3.17 us
    dot_general x4, matrix products, mm_tn(): return jnp.einsum('...ji,...jk->...ik', left, right, precision=fast_mode)  2.61 us
    squeeze x1, local copies, waits for them, and re-layouts, shards(): controls[:, 1] - jnp.swapaxes(controls[:, 1], 1, 2)  2.52 us
    dot_general x2, matrix products, mm_nt(): return jnp.einsum('...ij,...kj->...ik', left, right, precision=fast_mode)  2.2 us
  transfers between devices with their start and end apart: 2, of which 1 were waited for; matrix products, arithmetic and copies ran while one was open for 10% of the time, Pallas kernels for 0%

commit v1 on v0

--- a/solution.py
+++ b/solution.py
@@ -84,17 +84,26 @@
         running.append(cmul(steps[position][None], running[-1][None])[0])
     block_total = running[-1]
     split = 2 if col_count % 2 == 0 else 1
+    part = lax.axis_index("col") % split
+    rows = size // split
+    mine = lax.dynamic_slice_in_dim(block_total, part * rows, rows, 1)
+    if tm_count <= 8:
+        slots = jnp.arange(tm_count)[:, None, None, None]
+        gathered = jnp.where(slots == tm_index, mine[None], jnp.zeros_like(mine)[None])
+        for shift in range(1, tm_count):
+            for sign in (1, -1):
+                pairs = [(i, i + sign * shift) for i in range(tm_count) if 0 <= i + sign * shift < tm_count]
+                moved = lax.ppermute(mine, "tm", pairs)
+                gathered = jnp.where(slots == tm_index - sign * shift, moved[None], gathered)
+    else:
+        gathered = lax.all_gather(mine, "tm")
     if split == 2:
-        half = size // 2
-        col_index = lax.axis_index("col")
-        part = col_index % 2
-        mine = lax.all_gather(lax.dynamic_slice_in_dim(block_total, part * half, half, 1), "tm")
-        theirs = lax.ppermute(mine, "col", [(i, i ^ 1) for i in range(col_count)])
-        upper = jnp.where(part == 0, mine, theirs)
-        lower = jnp.where(part == 0, theirs, mine)
+        theirs = lax.ppermute(gathered, "col", [(i, i ^ 1) for i in range(col_count)])
+        upper = jnp.where(part == 0, gathered, theirs)
+        lower = jnp.where(part == 0, theirs, gathered)
         pieces = jnp.concatenate([upper, lower], 2)
     else:
-        pieces = lax.all_gather(block_total, "tm")
+        pieces = gathered
 
     eye = jnp.eye(size, dtype=jnp.float32)
     start_full = jnp.stack([eye, jnp.zeros_like(eye)])

time: 100 us -> 88.6 us (0.89)
  starting transfers between devices: 0.93 us -> 17.8 us
  waiting for transfers between devices: 29 us -> 12.4 us
  between operations: 14.6 us -> 1.48 us
  other arithmetic: 15 us -> 16 us
    all_gather x1 -> x0, waiting for transfers between devices: 28.9 us -> none  [shards(): lax.all_gather(lax.dynamic_slice_in_dim(block_total, part * half, half, 1...]
    ppermute x1 -> x7, starting transfers between devices: 0.89 us -> 17.8 us  [the longest x6 17.3 us: shards(): moved = lax.ppermute(mine, 'tm', pairs)]
    ppermute x1 -> x7, waiting for transfers between devices: 0.01 us -> 12.4 us  [the longest x6 12.4 us: shards(): moved = lax.ppermute(mine, 'tm', pairs)]
    select_n x1 -> x2, other arithmetic: 1.38 us -> 3.09 us  [the longest x1 1.73 us: shards(): lower = jnp.where(part == 0, theirs, gathered)]
    another operation x12 -> x11, other arithmetic: 3.17 us -> 2.45 us  [cmul(): return jnp.stack([real, imag], -3)]
    unnamed x19 -> x41, local copies, waits for them, and re-layouts: 8.69 us -> 8.79 us
  transfers between devices with their start and end apart: 2 -> 7, of which waited for: 1 -> 3; matrix products, arithmetic and copies ran while one was open for 10% -> 12% of each run, Pallas kernels for 0% -> 0%
where the time goes in v1:
time: 88.6 us; the launch traced here: 87.1 us
  matrix products  23.7 us (27%)
  starting transfers between devices  17.8 us (20%)
  other arithmetic  16 us (18%)
  local copies, waits for them, and re-layouts  15.7 us (18%)
  waiting for transfers between devices  12.4 us (14%)
  between operations  1.48 us (2%)
    dot_general x16, matrix products, mm(): return jnp.matmul(left, right, precision=fast_mode)  18.9 us
    ppermute x6, starting transfers between devices, shards(): moved = lax.ppermute(mine, 'tm', pairs)  17.3 us
    ppermute x6, waiting for transfers between devices, shards(): moved = lax.ppermute(mine, 'tm', pairs)  12.4 us
    unnamed x41, local copies, waits for them, and re-layouts  8.79 us
    mul x1, other arithmetic, shards(): 0.5 * (controls[:, 0] + jnp.swapaxes(controls[:, 0], 1, 2))  3.31 us
    dot_general x4, matrix products, mm_tn(): return jnp.einsum('...ji,...jk->...ik', left, right, precision=fast_mode)  2.59 us
    squeeze x1, local copies, waits for them, and re-layouts, shards(): controls[:, 1] - jnp.swapaxes(controls[:, 1], 1, 2)  2.56 us
    another operation x11, other arithmetic, cmul(): return jnp.stack([real, imag], -3)  2.45 us
  transfers between devices with their start and end apart: 7, of which 3 were waited for; matrix products, arithmetic and copies ran while one was open for 12% of the time, Pallas kernels for 0%

profile of v1, /device:TPU:13, one launch (start us, length us, event | category | flops | bytes accessed | tf_op | source)
XLA Modules:
  0.0 87.1 jit_solution(12091536438495875339)
XLA Ops:
  0.6 0.8 copy.49
  1.4 2.1 %multiply_reduce_fusion = f32[2,2,256,256]{3,2,1,0:T(8,128)S(1)} fusion(f32[4,2,256,256]{3,2,1,0:T(8,128)} %param.10, f32[4,2]{1,0:T(4,128)S(1)} %copy.49), kind=kLoop, calls=%fused_computation | loop fusion | flops 1835008 | bytes 3145760 | tf_op jit(solution)/shard_map/reduce_sum | solution.py:76
  5.2 1.1 %fusion.78 = f32[2,512,256]{2,1,0:T(8,128)S(1)} fusion(f32[2,512,256]{2,1,0:T(8,128)S(1)} %bitcast.234, f32[2,256,256]{2,1,0:T(8,128)S(1)} %copy.51, f32[2,2,256,256]{2,3,0,1:T(8,128)S(1)} %broadcast_add_fusion), kind=kOutput, calls=%fused_computation.160 | convolution fusion | flops 805568512 | bytes 3145728 | tf_op jit(solution)/shard_map/dot_general | solution.py:12
  6.4 1.1 %fusion.50 = f32[2,512,256]{2,1,0:T(8,128)S(1)} fusion(f32[2,512,256]{2,1,0:T(8,128)S(1)} %bitcast.235, f32[2,256,256]{2,1,0:T(8,128)S(1)} %copy.53), kind=kOutput, calls=%fused_computation.116 | convolution fusion | flops 805568512 | bytes 2621440 | tf_op jit(solution)/shard_map/dot_general | solution.py:12
  7.8 2.0 %fusion.6 = f32[2,2,512,256]{3,2,1,0:T(8,128)S(1)} fusion(f32[1,2,2,256,256]{4,3,1,2,0:T(8,128)S(1)} %get-tuple-element.65, f32[1,2,512,256]{3,2,0,1:T(8,128)S(1)} %bitcast.250, f32[1,2,512,256]{3,2,0,1:T(8,128)S(1)} %bitcast.236), kind=kOutput, calls=%fused_computation.24 | convolution fusion | flops 1611137024 | bytes 4718592 | tf_op jit(solution)/shard_map/dot_general | solution.py:12
  9.8 2.0 %fusion.9 = f32[2,2,512,256]{3,2,1,0:T(8,128)S(1)} fusion(f32[1,2,2,256,256]{4,3,1,2,0:T(8,128)S(1)} %get-tuple-element.65, f32[1,2,512,256]{3,2,0,1:T(8,128)S(1)} %bitcast.251, f32[1,2,512,256]{3,2,0,1:T(8,128)S(1)} %bitcast.237), kind=kOutput, calls=%fused_computation.25 | convolution fusion | flops 1611137024 | bytes 4718592 | tf_op jit(solution)/shard_map/dot_general | solution.py:12
  12.7 1.1 %fusion.42 = f32[2,512,256]{2,1,0:T(8,128)S(1)} fusion(f32[2,512,256]{2,1,0:T(8,128)S(1)} %bitcast.248, f32[2,2,256,256]{3,2,0,1:T(8,128)S(1)} %get-tuple-element.36), kind=kOutput, calls=%fused_computation.92 | convolution fusion | flops 805306368 | bytes 2621440 | tf_op jit(solution)/shard_map/dot_general | solution.py:12
  13.8 1.1 %fusion.44 = f32[2,512,256]{2,1,0:T(8,128)S(1)} fusion(f32[2,512,256]{2,1,0:T(8,128)S(1)} %bitcast.249, f32[2,2,256,256]{3,2,0,1:T(8,128)S(1)} %get-tuple-element.36, f32[256,256]{1,0:T(8,128)S(1)} %fusion.71), kind=kOutput, calls=%fused_computation.95 | convolution fusion | flops 805437440 | bytes 2883584 | tf_op jit(solution)/shard_map/dot_general | solution.py:12
  15.4 0.8 convolution_bitcast_fusion.1
  16.2 0.6 convolution_bitcast_fusion
  16.9 0.7 collective-permute-start
  17.6 0.7 collective-permute-start.1
  18.2 1.3 %collective-permute-start.2 = (f32[2,128,256]{2,1,0:T(8,128)S(1)}, f32[2,128,256]{2,1,0:T(8,128)S(1)}, u32[]{:S(2)}, u32[]{:S(2)}) collective-permute-start(f32[2,128,256]{2,1,0:T(8,128)S(1)} %fusion.53), channel_id=1, source_target_pairs={{8,0},{12,4},{9,1},{13,5},{10,2},{14,6},{11,3},{15,7},{24,16},{28,... | collective-permute-start | bytes 786440 | tf_op jit(solution)/shard_map/ppermute | solution.py:96
  19.5 6.0 %collective-permute-start.3 = (f32[2,128,256]{2,1,0:T(8,128)S(1)}, f32[2,128,256]{2,1,0:T(8,128)S(1)}, u32[]{:S(2)}, u32[]{:S(2)}) collective-permute-start(f32[2,128,256]{2,1,0:T(8,128)S(1)} %fusion.53), channel_id=1, source_target_pairs={{0,8},{4,12},{1,9},{5,13},{2,10},{6,14},{3,11},{7,15},{16,24},{20,... | collective-permute-start | bytes 786440 | tf_op jit(solution)/shard_map/ppermute | solution.py:96
  25.6 6.7 %collective-permute-start.4 = (f32[2,128,256]{2,1,0:T(8,128)S(1)}, f32[2,128,256]{2,1,0:T(8,128)S(1)}, u32[]{:S(2)}, u32[]{:S(2)}) collective-permute-start(f32[2,128,256]{2,1,0:T(8,128)S(1)} %fusion.53), channel_id=1, source_target_pairs={{4,0},{8,4},{12,8},{5,1},{9,5},{13,9},{6,2},{10,6},{14,10},{7,3},{... | collective-permute-start | bytes 786440 | tf_op jit(solution)/shard_map/ppermute | solution.py:96
  32.3 1.9 %collective-permute-start.5 = (f32[2,128,256]{2,1,0:T(8,128)S(1)}, f32[2,128,256]{2,1,0:T(8,128)S(1)}, u32[]{:S(2)}, u32[]{:S(2)}) collective-permute-start(f32[2,128,256]{2,1,0:T(8,128)S(1)} %fusion.53), channel_id=1, source_target_pairs={{0,4},{4,8},{8,12},{1,5},{5,9},{9,13},{2,6},{6,10},{10,14},{3,7},{... | collective-permute-start | bytes 786440 | tf_op jit(solution)/shard_map/ppermute | solution.py:96
  34.4 6.8 %collective-permute-done.3 = f32[2,128,256]{2,1,0:T(8,128)S(1)} collective-permute-done((f32[2,128,256]{2,1,0:T(8,128)S(1)}, f32[2,128,256]{2,1,0:T(8,128)S(1)}, u32[]{:S(2)}, u32[]{:S(2)}) %collective-permute-start.3) | collective-permute-done | bytes 262176 | tf_op jit(solution)/shard_map/ppermute | solution.py:96
  41.1 3.5 %collective-permute-done.4 = f32[2,128,256]{2,1,0:T(8,128)S(1)} collective-permute-done((f32[2,128,256]{2,1,0:T(8,128)S(1)}, f32[2,128,256]{2,1,0:T(8,128)S(1)}, u32[]{:S(2)}, u32[]{:S(2)}) %collective-permute-start.4) | collective-permute-done | bytes 262176 | tf_op jit(solution)/shard_map/ppermute | solution.py:96
  44.7 2.1 %collective-permute-done.5 = f32[2,128,256]{2,1,0:T(8,128)S(1)} collective-permute-done((f32[2,128,256]{2,1,0:T(8,128)S(1)}, f32[2,128,256]{2,1,0:T(8,128)S(1)}, u32[]{:S(2)}, u32[]{:S(2)}) %collective-permute-start.5) | collective-permute-done | bytes 262176 | tf_op jit(solution)/shard_map/ppermute | solution.py:96
  46.8 1.4 %select_select_fusion = f32[4,2,128,256]{3,2,0,1:T(8,128)} fusion(f32[2,128,256]{2,1,0:T(8,128)S(1)} %fusion.53, f32[2,128,256]{2,1,0:T(8,128)S(1)} %collective-permute-done.5, f32[2,128,256]{2,1,0:T(8,128)S(1)} %collective-permute-done.4, f32[2,128,256]{2,1,0:T(8,128)S(1)} %collective-permute-done.3, f32[2,128,256]{2,1,0:T(8,128)S(1)} %collective-permute-done.2, ...), kind=kLoop, calls=%fused_computation.56 | loop fusion | flops 1835008 | bytes 2883612 | tf_op jit(solution)/shard_map/jit(_where)/select_n | solution.py:97
  48.8 1.4 %copy-done = f32[4,2,256,256]{3,2,1,0:T(8,128)S(1)} copy-done((f32[4,2,256,256]{3,2,1,0:T(8,128)S(1)}, f32[4,2,256,256]{3,2,1,0:T(8,128)}, u32[]{:S(2)}) %copy-start) | copy-done | bytes 2097176
  50.2 1.6 %fusion.90 = (f32[4,1,256,256]{3,2,1,0:T(8,128)}, f32[4,256,256]{2,1,0:T(8,128)}) fusion(f32[4,2,256,256]{3,2,1,0:T(8,128)S(1)} %copy-done), kind=kLoop, calls=%fused_computation.179 | loop fusion | bytes 4194304 | tf_op jit(solution)/shard_map/slice | solution.py:135
  51.8 2.6 %copy.73 = f32[4,256,256]{1,2,0:T(8,128)} copy(f32[4,256,256]{2,1,0:T(8,128)} %get-tuple-element.46) | data formatting | bytes 2097152 | tf_op jit(solution)/shard_map/squeeze | solution.py:136
  54.4 2.6 %copy.83 = f32[4,1,256,256]{2,3,0,1:T(8,128)} copy(f32[4,1,256,256]{3,2,1,0:T(8,128)} %get-tuple-element.45) | data formatting | bytes 2097152
  57.1 3.3 %fusion.18 = (f32[4,256,256]{2,1,0:T(8,128)}, f32[4,256,256]{2,1,0:T(8,128)}) fusion(f32[4,1,256,256]{2,3,0,1:T(8,128)} %copy.83, f32[4,2,256,256]{3,2,1,0:T(8,128)S(1)} %copy-done, f32[4,256,256]{1,2,0:T(8,128)} %copy.73), kind=kLoop, calls=%fused_computation.49 | loop fusion | flops 1048576 | bytes 6291456 | tf_op jit(solution)/shard_map/mul | solution.py:135
  60.4 1.7 %broadcast_select_fusion = (f32[4,2,128,256]{3,2,0,1:T(8,128)S(1)}, f32[4,2,128,256]{3,2,0,1:T(8,128)S(1)}) fusion(f32[4,2,128,256]{3,2,0,1:T(8,128)} %collective-permute-done.6, pred[]{:T(512)S(6)} %eq.101, f32[2,128,256]{2,1,0:T(8,128)S(1)} %fusion.53, pred[4]{0:T(512)(128)(4,1)S(1)} %get-tuple-element.71, f32[2,128,256]{2,1,0:T(8,128)S(1)} %copy-done.16, ...), kind=kLoop, calls=%fused_computation.113 | loop fusion | flops 2359296 | bytes 4980765 | tf_op jit(solution)/shard_map/jit(_where)/select_n | solution.py:103
  62.5 1.5 %fusion.26 = f32[3,512,256]{2,1,0:T(8,128)S(1)} fusion(f32[3,512,256]{2,1,0:T(8,128)S(1)} %bitcast.238, f32[4,2,128,256]{3,2,0,1:T(8,128)S(1)} %get-tuple-element.56, f32[4,2,128,256]{3,2,0,1:T(8,128)S(1)} %get-tuple-element.55), kind=kOutput, calls=%fused_computation.62 | convolution fusion | flops 1208156160 | bytes 5242880 | tf_op jit(solution)/shard_map/dot_general | solution.py:12
  64.0 1.5 %fusion.22 = f32[3,512,256]{2,1,0:T(8,128)S(1)} fusion(f32[3,512,256]{2,1,0:T(8,128)S(1)} %bitcast.239, f32[4,2,128,256]{3,2,0,1:T(8,128)S(1)} %get-tuple-element.56, f32[4,2,128,256]{3,2,0,1:T(8,128)S(1)} %get-tuple-element.55), kind=kOutput, calls=%fused_computation.59 | convolution fusion | flops 1208156160 | bytes 5242880 | tf_op jit(solution)/shard_map/dot_general | solution.py:12
  66.1 1.1 %fusion.38 = f32[2,512,256]{2,1,0:T(8,128)S(1)} fusion(f32[2,512,256]{2,1,0:T(8,128)S(1)} %bitcast.246, f32[4,2,256,256]{3,2,0,1:T(8,128)S(1)} %fusion.1), kind=kOutput, calls=%fused_computation.84 | convolution fusion | flops 805306368 | bytes 2621440 | tf_op jit(solution)/shard_map/dot_general | solution.py:12
  67.2 1.1 %fusion.39 = f32[2,512,256]{2,1,0:T(8,128)S(1)} fusion(f32[2,512,256]{2,1,0:T(8,128)S(1)} %bitcast.247, f32[4,2,256,256]{3,2,0,1:T(8,128)S(1)} %fusion.1), kind=kOutput, calls=%fused_computation.86 | convolution fusion | flops 805306368 | bytes 2621440 | tf_op jit(solution)/shard_map/dot_general | solution.py:12
  68.5 1.1 %slice-done = f32[2,2,256,256]{3,2,0,1:T(8,128)S(1)} async-done(((f32[4,2,256,256]{3,2,0,1:T(8,128)}), f32[2,2,256,256]{3,2,0,1:T(8,128)S(1)}, s32[]{:S(2)}) %slice-start) | async-done | bytes 1048600 | tf_op jit(solution)/shard_map/slice | solution.py:114
  69.7 1.0 %fusion.57 = f32[2,512,256]{2,1,0:T(8,128)S(1)} fusion(f32[2,512,256]{2,1,0:T(8,128)S(1)} %bitcast.242, f32[1,2,256,256]{3,2,1,0:T(8,128)S(1)} %fusion.34), kind=kOutput, calls=%fused_computation.127 | convolution fusion | flops 805306368 | bytes 2359296 | tf_op jit(solution)/shard_map/dot_general | solution.py:12
  70.7 1.0 %fusion.56 = f32[2,512,256]{2,1,0:T(8,128)S(1)} fusion(f32[2,512,256]{2,1,0:T(8,128)S(1)} %bitcast.243, f32[1,2,256,256]{3,2,1,0:T(8,128)S(1)} %fusion.34), kind=kOutput, calls=%fused_computation.125 | convolution fusion | flops 805306368 | bytes 2359296 | tf_op jit(solution)/shard_map/dot_general | solution.py:12
  71.7 0.7 fusion.63
  72.4 0.6 fusion.68
  73.0 0.6 fusion.66
  73.6 0.8 fusion.14
  74.4 0.6 fusion.13
  75.3 1.0 %fusion.55 = f32[2,512,256]{2,1,0:T(8,128)S(1)} fusion(f32[2,512,256]{2,1,0:T(8,128)S(1)} %bitcast.244, f32[1,2,256,256]{2,3,1,0:T(8,128)S(1)} %maximum_bitcast_fusion), kind=kOutput, calls=%fused_computation.123 | convolution fusion | flops 805306368 | bytes 2359296 | tf_op jit(solution)/shard_map/dot_general | solution.py:12
  76.4 1.0 %fusion.54 = f32[2,512,256]{2,1,0:T(8,128)S(1)} fusion(f32[2,512,256]{2,1,0:T(8,128)S(1)} %bitcast.245, f32[1,2,256,256]{2,3,1,0:T(8,128)S(1)} %maximum_bitcast_fusion), kind=kOutput, calls=%fused_computation.121 | convolution fusion | flops 805306368 | bytes 2359296 | tf_op jit(solution)/shard_map/dot_general | solution.py:12
  77.7 1.1 %fusion.81 = f32[2,512,256]{2,1,0:T(8,128)S(1)} fusion(f32[2,512,256]{2,1,0:T(8,128)S(1)} %bitcast.240, f32[2,512,256]{2,1,0:T(8,128)S(1)} %fusion.56, f32[2,512,256]{2,1,0:T(8,128)S(1)} %fusion.57), kind=kOutput, calls=%fused_computation.162 | convolution fusion | flops 805437440 | bytes 3145728 | tf_op jit(solution)/shard_map/...ij,...kj->...ik/dot_general | solution.py:16
  78.8 1.1 %fusion.83 = f32[2,512,256]{2,1,0:T(8,128)S(1)} fusion(f32[2,512,256]{2,1,0:T(8,128)S(1)} %bitcast.241, f32[2,512,256]{2,1,0:T(8,128)S(1)} %fusion.57, f32[2,512,256]{2,1,0:T(8,128)S(1)} %fusion.56), kind=kOutput, calls=%fused_computation.164 | convolution fusion | flops 805437440 | bytes 3145728 | tf_op jit(solution)/shard_map/...ij,...kj->...ik/dot_general | solution.py:16
  79.9 1.0 %fusion.30 = f32[2,2,256,64]{3,2,0,1:T(8,128)} fusion(s32[]{:T(128)S(6)} %select_n.72, f32[2,1,256,256]{3,2,0,1:T(8,128)S(1)} %get-tuple-element.51, f32[2,1,256,256]{3,2,0,1:T(8,128)S(1)} %get-tuple-element.52), kind=kLoop, calls=%fused_computation.67 | loop fusion | flops 65536 | bytes 1310724 | tf_op jit(solution)/shard_map/stack | solution.py:30
  80.9 2.0 %copy.75 = f32[2,2,256,64]{2,3,1,0:T(8,128)} copy(f32[2,2,256,64]{3,2,0,1:T(8,128)} %fusion.30) | data formatting | bytes 524288
  83.1 1.1 %copy-done.4 = f32[4,256,256]{2,1,0:T(8,128)S(1)} copy-done((f32[4,256,256]{2,1,0:T(8,128)S(1)}, f32[4,256,256]{2,1,0:T(8,128)}, u32[]{:S(2)}) %copy-start.4) | copy-done | bytes 1048600
  84.2 1.1 %subtract_reduce_fusion = (f32[4,2]{1,0:T(4,128)S(1)}, f32[4,2]{1,0:T(4,128)S(1)}) fusion(f32[2,256,256]{2,1,0:T(8,128)S(1)} %get-tuple-element.48, f32[4,256,256]{2,1,0:T(8,128)S(1)} %copy-done.4, f32[2,256,256]{2,1,0:T(8,128)S(1)} %get-tuple-element.47, f32[4,256,256]{2,1,0:T(8,128)S(1)} %copy-done.3), kind=kLoop, calls=%fused_computation.19 | loop fusion | flops 4194288 | bytes 3145792 | tf_op jit(solution)/shard_map/reduce_sum | solution.py:138
  85.3 1.2 %multiply_subtract_fusion = f32[4,2]{1,0:T(4,128)S(1)} fusion(f32[4,2]{1,0:T(4,128)S(1)} %get-tuple-element.33, f32[4,2]{1,0:T(4,128)S(1)} %get-tuple-element.32, f32[]{:T(128)} %get-tuple-element.35, f32[]{:T(128)} %get-tuple-element.34), kind=kLoop, calls=%fused_computation.166 | loop fusion | flops 24 | bytes 104 | tf_op jit(solution)/shard_map/sub | solution.py:139
  86.5 0.6 copy.74
  (88 shorter events, 6.0 us)
Async XLA Ops:
  1.4 2.4 %copy-start.17 = (f32[2,256,256]{2,1,0:T(8,128)S(1)}, f32[2,256,256]{2,1,0:T(8,128)}, u32[]{:S(2)}) copy-start(f32[2,256,256]{2,1,0:T(8,128)} %param.9) | copy-start | bytes 1572868
  16.9 15.4 %collective-permute-start = (f32[2,128,256]{2,1,0:T(8,128)S(1)}, f32[2,128,256]{2,1,0:T(8,128)S(1)}, u32[]{:S(2)}, u32[]{:S(2)}) collective-permute-start(f32[2,128,256]{2,1,0:T(8,128)S(1)} %fusion.53), channel_id=1, source_target_pairs={{12,0},{13,1},{14,2},{15,3},{28,16},{29,17},{30,18},{31,19}} | collective-permute-start | bytes 786440 | tf_op jit(solution)/shard_map/ppermute | solution.py:96
  17.6 16.8 %collective-permute-start.1 = (f32[2,128,256]{2,1,0:T(8,128)S(1)}, f32[2,128,256]{2,1,0:T(8,128)S(1)}, u32[]{:S(2)}, u32[]{:S(2)}) collective-permute-start(f32[2,128,256]{2,1,0:T(8,128)S(1)} %fusion.53), channel_id=1, source_target_pairs={{0,12},{1,13},{2,14},{3,15},{16,28},{17,29},{18,30},{19,31}} | collective-permute-start | bytes 786440 | tf_op jit(solution)/shard_map/ppermute | solution.py:96
  18.2 16.1 %collective-permute-start.2 = (f32[2,128,256]{2,1,0:T(8,128)S(1)}, f32[2,128,256]{2,1,0:T(8,128)S(1)}, u32[]{:S(2)}, u32[]{:S(2)}) collective-permute-start(f32[2,128,256]{2,1,0:T(8,128)S(1)} %fusion.53), channel_id=1, source_target_pairs={{8,0},{12,4},{9,1},{13,5},{10,2},{14,6},{11,3},{15,7},{24,16},{28,... | collective-permute-start | bytes 786440 | tf_op jit(solution)/shard_map/ppermute | solution.py:96
  19.5 21.6 %collective-permute-start.3 = (f32[2,128,256]{2,1,0:T(8,128)S(1)}, f32[2,128,256]{2,1,0:T(8,128)S(1)}, u32[]{:S(2)}, u32[]{:S(2)}) collective-permute-start(f32[2,128,256]{2,1,0:T(8,128)S(1)} %fusion.53), channel_id=1, source_target_pairs={{0,8},{4,12},{1,9},{5,13},{2,10},{6,14},{3,11},{7,15},{16,24},{20,... | collective-permute-start | bytes 786440 | tf_op jit(solution)/shard_map/ppermute | solution.py:96
  25.6 19.1 %collective-permute-start.4 = (f32[2,128,256]{2,1,0:T(8,128)S(1)}, f32[2,128,256]{2,1,0:T(8,128)S(1)}, u32[]{:S(2)}, u32[]{:S(2)}) collective-permute-start(f32[2,128,256]{2,1,0:T(8,128)S(1)} %fusion.53), channel_id=1, source_target_pairs={{4,0},{8,4},{12,8},{5,1},{9,5},{13,9},{6,2},{10,6},{14,10},{7,3},{... | collective-permute-start | bytes 786440 | tf_op jit(solution)/shard_map/ppermute | solution.py:96
  32.3 16.3 %copy-start.5 = (f32[2,128,256]{2,1,0:T(8,128)}, f32[2,128,256]{2,1,0:T(8,128)S(1)}, u32[]{:S(2)}) copy-start(f32[2,128,256]{2,1,0:T(8,128)S(1)} %collective-permute-done) | copy-start | bytes 786436
  32.3 14.4 %collective-permute-start.5 = (f32[2,128,256]{2,1,0:T(8,128)S(1)}, f32[2,128,256]{2,1,0:T(8,128)S(1)}, u32[]{:S(2)}, u32[]{:S(2)}) collective-permute-start(f32[2,128,256]{2,1,0:T(8,128)S(1)} %fusion.53), channel_id=1, source_target_pairs={{0,4},{4,8},{8,12},{1,5},{5,9},{9,13},{2,6},{6,10},{10,14},{3,7},{... | collective-permute-start | bytes 786440 | tf_op jit(solution)/shard_map/ppermute | solution.py:96
  34.3 14.3 %copy-start.7 = (f32[2,128,256]{2,1,0:T(8,128)}, f32[2,128,256]{2,1,0:T(8,128)S(1)}, u32[]{:S(2)}) copy-start(f32[2,128,256]{2,1,0:T(8,128)S(1)} %collective-permute-done.1) | copy-start | bytes 786436
  34.3 14.3 %copy-start.9 = (f32[2,128,256]{2,1,0:T(8,128)}, f32[2,128,256]{2,1,0:T(8,128)S(1)}, u32[]{:S(2)}) copy-start(f32[2,128,256]{2,1,0:T(8,128)S(1)} %collective-permute-done.2) | copy-start | bytes 786436
  41.1 7.5 %copy-start.11 = (f32[2,128,256]{2,1,0:T(8,128)}, f32[2,128,256]{2,1,0:T(8,128)S(1)}, u32[]{:S(2)}) copy-start(f32[2,128,256]{2,1,0:T(8,128)S(1)} %collective-permute-done.3) | copy-start | bytes 786436
  44.7 4.0 %copy-start.13 = (f32[2,128,256]{2,1,0:T(8,128)}, f32[2,128,256]{2,1,0:T(8,128)S(1)}, u32[]{:S(2)}) copy-start(f32[2,128,256]{2,1,0:T(8,128)S(1)} %collective-permute-done.4) | copy-start | bytes 786436
  46.8 1.9 %copy-start.15 = (f32[2,128,256]{2,1,0:T(8,128)}, f32[2,128,256]{2,1,0:T(8,128)S(1)}, u32[]{:S(2)}) copy-start(f32[2,128,256]{2,1,0:T(8,128)S(1)} %collective-permute-done.5) | copy-start | bytes 786436
  48.1 12.3 %collective-permute-start.6 = (f32[4,2,128,256]{3,2,0,1:T(8,128)}, f32[4,2,128,256]{3,2,0,1:T(8,128)}, u32[]{:S(2)}, u32[]{:S(2)}) collective-permute-start(f32[4,2,128,256]{3,2,0,1:T(8,128)} %select_select_fusion), channel_id=1, source_target_pairs={{0,1},{1,0},{2,3},{3,2},{4,5},{5,4},{6,7},{7,6},{8,9},{9,8},{10,11... | collective-permute-start | bytes 3145736 | tf_op jit(solution)/shard_map/ppermute | solution.py:101
  48.6 1.6 %copy-start = (f32[4,2,256,256]{3,2,1,0:T(8,128)S(1)}, f32[4,2,256,256]{3,2,1,0:T(8,128)}, u32[]{:S(2)}) copy-start(f32[4,2,256,256]{3,2,1,0:T(8,128)} %param.10) | copy-start | bytes 6291460
  57.0 3.4 %copy-start.6 = (f32[2,128,256]{2,1,0:T(8,128)S(1)}, f32[2,128,256]{2,1,0:T(8,128)}, u32[]{:S(2)}) copy-start(f32[2,128,256]{2,1,0:T(8,128)} %copy-done.5) | copy-start | bytes 786436
  57.0 3.4 %copy-start.8 = (f32[2,128,256]{2,1,0:T(8,128)S(1)}, f32[2,128,256]{2,1,0:T(8,128)}, u32[]{:S(2)}) copy-start(f32[2,128,256]{2,1,0:T(8,128)} %copy-done.7) | copy-start | bytes 786436
  57.0 3.4 %copy-start.10 = (f32[2,128,256]{2,1,0:T(8,128)S(1)}, f32[2,128,256]{2,1,0:T(8,128)}, u32[]{:S(2)}) copy-start(f32[2,128,256]{2,1,0:T(8,128)} %copy-done.9) | copy-start | bytes 786436
  57.0 3.4 %copy-start.12 = (f32[2,128,256]{2,1,0:T(8,128)S(1)}, f32[2,128,256]{2,1,0:T(8,128)}, u32[]{:S(2)}) copy-start(f32[2,128,256]{2,1,0:T(8,128)} %copy-done.11) | copy-start | bytes 786436
  57.1 3.4 %copy-start.14 = (f32[2,128,256]{2,1,0:T(8,128)S(1)}, f32[2,128,256]{2,1,0:T(8,128)}, u32[]{:S(2)}) copy-start(f32[2,128,256]{2,1,0:T(8,128)} %copy-done.13) | copy-start | bytes 786436
  57.1 3.4 %copy-start.16 = (f32[2,128,256]{2,1,0:T(8,128)S(1)}, f32[2,128,256]{2,1,0:T(8,128)}, u32[]{:S(2)}) copy-start(f32[2,128,256]{2,1,0:T(8,128)} %copy-done.15) | copy-start | bytes 786436
  66.1 2.3 %copy-start.1 = (f32[4,2,256,256]{3,2,0,1:T(8,128)}, f32[4,2,256,256]{3,2,0,1:T(8,128)S(1)}, u32[]{:S(2)}) copy-start(f32[4,2,256,256]{3,2,0,1:T(8,128)S(1)} %fusion.1) | copy-start | bytes 6291460
  68.3 1.2 %slice-start = ((f32[4,2,256,256]{3,2,0,1:T(8,128)}), f32[2,2,256,256]{3,2,0,1:T(8,128)S(1)}, s32[]{:S(2)}) async-start(f32[4,2,256,256]{3,2,0,1:T(8,128)} %copy-done.1), calls=%async_computation | async-start | bytes 2097152 | tf_op jit(solution)/shard_map/slice | solution.py:114
  69.6 2.0 %copy-start.2 = (f32[2,256,256]{2,1,0:T(8,128)S(1)}, f32[2,256,256]{2,1,0:T(8,128)}, u32[]{:S(2)}) copy-start(f32[2,256,256]{2,1,0:T(8,128)} %param.11) | copy-start | bytes 1572868
  80.9 2.2 %copy-start.3 = (f32[4,256,256]{2,1,0:T(8,128)S(1)}, f32[4,256,256]{2,1,0:T(8,128)}, u32[]{:S(2)}) copy-start(f32[4,256,256]{2,1,0:T(8,128)} %get-tuple-element.43) | copy-start | bytes 3145732
  83.0 1.2 %copy-start.4 = (f32[4,256,256]{2,1,0:T(8,128)S(1)}, f32[4,256,256]{2,1,0:T(8,128)}, u32[]{:S(2)}) copy-start(f32[4,256,256]{2,1,0:T(8,128)} %get-tuple-element.44) | copy-start | bytes 3145732

commit v2 on v1

--- a/solution.py
+++ b/solution.py
@@ -6,10 +6,11 @@
 TAYLOR = 8
 
 fast_mode = lax.Precision.HIGHEST
+taylor_mode = lax.Precision.HIGHEST
 
 
-def mm(left, right):
-    return jnp.matmul(left, right, precision=fast_mode)
+def mm(left, right, mode=fast_mode):
+    return jnp.matmul(left, right, precision=mode)
 
 
 def mm_nt(left, right):
@@ -20,11 +21,11 @@
     return jnp.einsum("...ji,...jk->...ik", left, right, precision=fast_mode)
 
 
-def cmul(a, b):
+def cmul(a, b, mode=fast_mode):
     size = a.shape[-2]
     stacked = a.reshape(a.shape[:-3] + (2 * size, a.shape[-1]))
-    with_real = mm(stacked, b[..., 0, :, :])
-    with_imag = mm(stacked, b[..., 1, :, :])
+    with_real = mm(stacked, b[..., 0, :, :], mode)
+    with_imag = mm(stacked, b[..., 1, :, :], mode)
     real = with_real[..., :size, :] - with_imag[..., size:, :]
     imag = with_imag[..., :size, :] + with_real[..., size:, :]
     return jnp.stack([real, imag], -3)
@@ -50,8 +51,8 @@
     size = ham.shape[-1]
     eye = jnp.eye(size, dtype=jnp.float32)
     gen = jnp.stack([ham[:, 1], -ham[:, 0]], 1)
-    gen2 = cmul(gen, gen)
-    both = cmul(jnp.stack([gen, gen2], 0), gen2[None])
+    gen2 = cmul(gen, gen, taylor_mode)
+    both = cmul(jnp.stack([gen, gen2], 0), gen2[None], taylor_mode)
     gen3, gen4 = both[0], both[1]
     coef = [1.0]
     for order in range(1, TAYLOR + 1):
@@ -60,7 +61,7 @@
     low = low.at[:, 0].add(coef[0] * eye)
     high = coef[5] * gen + coef[6] * gen2 + coef[7] * gen3 + coef[8] * gen4
     high = high.at[:, 0].add(coef[4] * eye)
-    return low + cmul(gen4, high)
+    return low + cmul(gen4, high, taylor_mode)
 
 
 def shards(amplitudes, drift, controls, target):
@@ -88,22 +89,32 @@
     rows = size // split
     mine = lax.dynamic_slice_in_dim(block_total, part * rows, rows, 1)
     if tm_count <= 8:
+        received = []
+        for shift in range(1, tm_count):
+            pairs = [(i, (i + shift) % tm_count) for i in range(tm_count)]
+            received.append(lax.ppermute(mine, "tm", pairs))
+        received = jnp.stack(received, 0)
+        if split == 2:
+            theirs = lax.ppermute(received, "col", [(i, i ^ 1) for i in range(col_count)])
+            own_block = block_total
+            received = jnp.where(
+                part == 0, jnp.concatenate([received, theirs], 2), jnp.concatenate([theirs, received], 2)
+            )
+        else:
+            own_block = block_total
         slots = jnp.arange(tm_count)[:, None, None, None]
-        gathered = jnp.where(slots == tm_index, mine[None], jnp.zeros_like(mine)[None])
+        pieces = jnp.where(slots == tm_index, own_block[None], jnp.zeros_like(own_block)[None])
         for shift in range(1, tm_count):
-            for sign in (1, -1):
-                pairs = [(i, i + sign * shift) for i in range(tm_count) if 0 <= i + sign * shift < tm_count]
-                moved = lax.ppermute(mine, "tm", pairs)
-                gathered = jnp.where(slots == tm_index - sign * shift, moved[None], gathered)
+            pieces = jnp.where(slots == (tm_index - shift) % tm_count, received[shift - 1][None], pieces)
     else:
         gathered = lax.all_gather(mine, "tm")
-    if split == 2:
-        theirs = lax.ppermute(gathered, "col", [(i, i ^ 1) for i in range(col_count)])
-        upper = jnp.where(part == 0, gathered, theirs)
-        lower = jnp.where(part == 0, theirs, gathered)
-        pieces = jnp.concatenate([upper, lower], 2)
-    else:
-        pieces = gathered
+        if split == 2:
+            theirs = lax.ppermute(gathered, "col", [(i, i ^ 1) for i in range(col_count)])
+            upper = jnp.where(part == 0, gathered, theirs)
+            lower = jnp.where(part == 0, theirs, gathered)
+            pieces = jnp.concatenate([upper, lower], 2)
+        else:
+            pieces = gathered
 
     eye = jnp.eye(size, dtype=jnp.float32)
     start_full = jnp.stack([eye, jnp.zeros_like(eye)])

time: 88.6 us -> 75.7 us (0.85); the launches traced: 87.1 us -> 75.3 us
  starting transfers between devices: 17.8 us -> 4.33 us
  waiting for transfers between devices: 12.4 us -> 14.1 us
  other arithmetic: 16 us -> 17.2 us
  local copies, waits for them, and re-layouts: 15.7 us -> 14.6 us
    ppermute x7 -> x4, starting transfers between devices: 17.8 us -> 4.33 us  [the longest x3 3.77 us: shards(): received.append(lax.ppermute(mine, 'tm', pairs))]
    ppermute x7 -> x4, waiting for transfers between devices: 12.4 us -> 14.1 us  [the longest x3 14.1 us: shards(): received.append(lax.ppermute(mine, 'tm', pairs))]
    mul x1, other arithmetic: 3.31 us -> 1.77 us  [shards(): 0.5 * (controls[:, 0] + jnp.swapaxes(controls[:, 0], 1, 2))]
    another operation x1, other arithmetic: 0.07 us -> 1.28 us  [shards(): states = cmul(jnp.stack(running, 0), prefix[None])]
    another operation x1 -> x2, other arithmetic: 0.14 us -> 1.32 us  [the longest x1 1.18 us: shards(): received = jnp.stack(received, 0)]
    select_n x2, other arithmetic: 3.09 us -> 1.93 us  [the longest x1 1.58 us: shards(): jnp.where(part == 0, jnp.concatenate([received, theirs], 2), jnp.concaten...]
    unnamed x41 -> x21, local copies, waits for them, and re-layouts: 8.79 us -> 7.64 us
    broadcast_in_dim x0 -> x1, other arithmetic: none -> 0.99 us  [shards(): jnp.where(slots == tm_index, own_block[None], jnp.zeros_like(own_block)[N...]
  transfers between devices with their start and end apart: 7 -> 4, of which waited for: 3 -> 2; matrix products, arithmetic and copies ran while one was open for 12% -> 14% of each run, Pallas kernels for 0% -> 0%
where the time goes in v2:
time: 75.7 us; the launch traced here: 75.3 us
  matrix products  23.7 us (31%)
  other arithmetic  17.2 us (23%)
  local copies, waits for them, and re-layouts  14.6 us (19%)
  waiting for transfers between devices  14.1 us (19%)
  starting transfers between devices  4.33 us (6%)
  between operations  1.26 us (2%)
    dot_general x16, matrix products, mm(): return jnp.matmul(left, right, precision=mode)  18.9 us
    ppermute x3, waiting for transfers between devices, shards(): received.append(lax.ppermute(mine, 'tm', pairs))  14.1 us
    unnamed x21, local copies, waits for them, and re-layouts  7.64 us
    ppermute x3, starting transfers between devices, shards(): received.append(lax.ppermute(mine, 'tm', pairs))  3.77 us
    dot_general x4, matrix products, mm_tn(): return jnp.einsum('...ji,...jk->...ik', left, right, precision=fast_mode)  2.6 us
    squeeze x1, local copies, waits for them, and re-layouts, shards(): controls[:, 1] - jnp.swapaxes(controls[:, 1], 1, 2)  2.54 us
    another operation x11, other arithmetic, cmul(): return jnp.stack([real, imag], -3)  2.4 us
    dot_general x2, matrix products, mm_nt(): return jnp.einsum('...ij,...kj->...ik', left, right, precision=fast_mode)  2.2 us
  transfers between devices with their start and end apart: 4, of which 2 were waited for; matrix products, arithmetic and copies ran while one was open for 14% of the time, Pallas kernels for 0%

profile of v2, /device:TPU:13, one launch (start us, length us, event | category | flops | bytes accessed | tf_op | source)
XLA Modules:
  0.0 75.3 jit_solution(9597106462979777537)
XLA Ops:
  0.6 0.8 %copy.49 = f32[4,2]{1,0:T(4,128)S(1)} copy(f32[4,2]{0,1:T(2,128)} %param.8) | data formatting | bytes 64 | tf_op args[0]
  1.4 2.1 %multiply_reduce_fusion = f32[2,2,256,256]{3,2,1,0:T(8,128)S(1)} fusion(f32[4,2,256,256]{3,2,1,0:T(8,128)} %param.10, f32[4,2]{1,0:T(4,128)S(1)} %copy.49), kind=kLoop, calls=%fused_computation | loop fusion | flops 1835008 | bytes 3145760 | tf_op jit(solution)/shard_map/reduce_sum | solution.py:77
  5.2 1.1 %fusion.82 = f32[2,512,256]{2,1,0:T(8,128)S(1)} fusion(f32[2,512,256]{2,1,0:T(8,128)S(1)} %bitcast.245, f32[2,256,256]{2,1,0:T(8,128)S(1)} %copy.51, f32[2,2,256,256]{2,3,0,1:T(8,128)S(1)} %broadcast_add_fusion), kind=kOutput, calls=%fused_computation.166 | convolution fusion | flops 805568512 | bytes 3145728 | tf_op jit(solution)/shard_map/dot_general | solution.py:13
  6.4 1.1 %fusion.54 = f32[2,512,256]{2,1,0:T(8,128)S(1)} fusion(f32[2,512,256]{2,1,0:T(8,128)S(1)} %bitcast.246, f32[2,256,256]{2,1,0:T(8,128)S(1)} %copy.53), kind=kOutput, calls=%fused_computation.122 | convolution fusion | flops 805568512 | bytes 2621440 | tf_op jit(solution)/shard_map/dot_general | solution.py:13
  7.8 2.0 %fusion.4 = f32[2,2,512,256]{3,2,1,0:T(8,128)S(1)} fusion(f32[1,2,2,256,256]{4,3,1,2,0:T(8,128)S(1)} %get-tuple-element.66, f32[1,2,512,256]{3,2,0,1:T(8,128)S(1)} %bitcast.259, f32[1,2,512,256]{3,2,0,1:T(8,128)S(1)} %bitcast.247), kind=kOutput, calls=%fused_computation.16 | convolution fusion | flops 1611137024 | bytes 4718592 | tf_op jit(solution)/shard_map/dot_general | solution.py:13
  9.8 2.0 %fusion.7 = f32[2,2,512,256]{3,2,1,0:T(8,128)S(1)} fusion(f32[1,2,2,256,256]{4,3,1,2,0:T(8,128)S(1)} %get-tuple-element.66, f32[1,2,512,256]{3,2,0,1:T(8,128)S(1)} %bitcast.260, f32[1,2,512,256]{3,2,0,1:T(8,128)S(1)} %bitcast.248), kind=kOutput, calls=%fused_computation.17 | convolution fusion | flops 1611137024 | bytes 4718592 | tf_op jit(solution)/shard_map/dot_general | solution.py:13
  12.2 0.4 bitcast_add_fusion.1
  12.7 1.1 %fusion.46 = f32[2,512,256]{2,1,0:T(8,128)S(1)} fusion(f32[2,512,256]{2,1,0:T(8,128)S(1)} %bitcast.257, f32[2,2,256,256]{3,2,0,1:T(8,128)S(1)} %get-tuple-element.36), kind=kOutput, calls=%fused_computation.102 | convolution fusion | flops 805306368 | bytes 2621440 | tf_op jit(solution)/shard_map/dot_general | solution.py:13
  13.8 1.1 %fusion.48 = f32[2,512,256]{2,1,0:T(8,128)S(1)} fusion(f32[2,512,256]{2,1,0:T(8,128)S(1)} %bitcast.258, f32[2,2,256,256]{3,2,0,1:T(8,128)S(1)} %get-tuple-element.36, f32[256,256]{1,0:T(8,128)S(1)} %fusion.75), kind=kOutput, calls=%fused_computation.105 | convolution fusion | flops 805437440 | bytes 2883584 | tf_op jit(solution)/shard_map/dot_general | solution.py:13
  15.3 0.9 %fusion.95 = (f32[1,2,256,256]{3,2,0,1:T(8,128)}, f32[1,2,256,256]{3,2,0,1:T(8,128)S(1)}) fusion(f32[2,2,256,256]{3,2,0,1:T(8,128)S(1)} %maximum_add_fusion), kind=kLoop, calls=%fused_computation.183 | loop fusion | bytes 2097152 | tf_op jit(solution)/shard_map/slice | solution.py:83
  16.2 0.8 %convolution_bitcast_fusion.1 = f32[1,512,256]{2,1,0:T(8,128)S(1)} fusion(f32[512,256]{1,0:T(8,128)S(1)} %bitcast.265, f32[2,2,256,256]{3,2,0,1:T(8,128)S(1)} %maximum_add_fusion), kind=kOutput, calls=%fused_computation.23 | convolution fusion | flops 402653184 | bytes 1310720 | tf_op jit(solution)/shard_map/dot_general | solution.py:13
  16.9 0.6 convolution_bitcast_fusion
  17.6 0.8 %fusion.57 = f32[2,128,256]{2,1,0:T(8,128)} fusion(s32[]{:T(128)S(6)} %select_n.60, f32[1,1,256,256]{3,2,0,1:T(8,128)S(1)} %get-tuple-element.64, f32[1,1,256,256]{3,2,0,1:T(8,128)S(1)} %get-tuple-element.65), kind=kLoop, calls=%fused_computation.125 | loop fusion | flops 65536 | bytes 786436 | tf_op jit(solution)/shard_map/dynamic_slice | solution.py:90
  18.4 1.3 %collective-permute-start = (f32[2,128,256]{2,1,0:T(8,128)}, f32[2,128,256]{2,1,0:T(8,128)}, u32[]{:S(2)}, u32[]{:S(2)}) collective-permute-start(f32[2,128,256]{2,1,0:T(8,128)} %fusion.57), channel_id=1, source_target_pairs={{0,4},{4,8},{8,12},{12,0},{1,5},{5,9},{9,13},{13,1},{2,6},{6,10},{... | collective-permute-start | bytes 786440 | tf_op jit(solution)/shard_map/ppermute | solution.py:95
  19.7 1.0 %collective-permute-start.1 = (f32[2,128,256]{2,1,0:T(8,128)}, f32[2,128,256]{2,1,0:T(8,128)}, u32[]{:S(2)}, u32[]{:S(2)}) collective-permute-start(f32[2,128,256]{2,1,0:T(8,128)} %fusion.57), channel_id=1, source_target_pairs={{0,8},{4,12},{8,0},{12,4},{1,9},{5,13},{9,1},{13,5},{2,10},{6,14},... | collective-permute-start | bytes 786440 | tf_op jit(solution)/shard_map/ppermute | solution.py:95
  20.7 1.5 %collective-permute-start.2 = (f32[2,128,256]{2,1,0:T(8,128)}, f32[2,128,256]{2,1,0:T(8,128)}, u32[]{:S(2)}, u32[]{:S(2)}) collective-permute-start(f32[2,128,256]{2,1,0:T(8,128)} %fusion.57), channel_id=1, source_target_pairs={{0,12},{4,0},{8,4},{12,8},{1,13},{5,1},{9,5},{13,9},{2,14},{6,2},{... | collective-permute-start | bytes 786440 | tf_op jit(solution)/shard_map/ppermute | solution.py:95
  22.2 1.3 %maximum_maximum_fusion = f32[2,2,256,256]{3,2,0,1:T(8,128)S(1)} fusion(f32[1,1,256,256]{3,2,0,1:T(8,128)S(1)} %get-tuple-element.65, f32[1,1,256,256]{3,2,0,1:T(8,128)S(1)} %get-tuple-element.64, f32[1,2,256,256]{3,2,0,1:T(8,128)} %get-tuple-element.62), kind=kLoop, calls=%fused_computation.38 | loop fusion | flops 524288 | bytes 2097152 | tf_op jit(solution)/shard_map/stack | solution.py:140
  23.9 1.5 %fusion.94 = (f32[4,1,256,256]{3,2,1,0:T(8,128)}, f32[4,256,256]{2,1,0:T(8,128)}) fusion(f32[4,2,256,256]{3,2,1,0:T(8,128)S(1)} %copy-done), kind=kLoop, calls=%fused_computation.182 | loop fusion | bytes 4194304 | tf_op jit(solution)/shard_map/slice | solution.py:146
  25.4 2.5 %copy.73 = f32[4,256,256]{1,2,0:T(8,128)} copy(f32[4,256,256]{2,1,0:T(8,128)} %get-tuple-element.46) | data formatting | bytes 2097152 | tf_op jit(solution)/shard_map/squeeze | solution.py:147
  28.0 2.5 %copy.83 = f32[4,1,256,256]{2,3,0,1:T(8,128)} copy(f32[4,1,256,256]{3,2,1,0:T(8,128)} %get-tuple-element.45) | data formatting | bytes 2097152
  30.5 11.3 %collective-permute-done.1 = f32[2,128,256]{2,1,0:T(8,128)} collective-permute-done((f32[2,128,256]{2,1,0:T(8,128)}, f32[2,128,256]{2,1,0:T(8,128)}, u32[]{:S(2)}, u32[]{:S(2)}) %collective-permute-start.1) | collective-permute-done | bytes 262176 | tf_op jit(solution)/shard_map/ppermute | solution.py:95
  41.8 2.9 %collective-permute-done.2 = f32[2,128,256]{2,1,0:T(8,128)} collective-permute-done((f32[2,128,256]{2,1,0:T(8,128)}, f32[2,128,256]{2,1,0:T(8,128)}, u32[]{:S(2)}, u32[]{:S(2)}) %collective-permute-start.2) | collective-permute-done | bytes 262176 | tf_op jit(solution)/shard_map/ppermute | solution.py:95
  44.7 1.2 %pad_maximum_fusion.7 = f32[3,2,128,256]{3,2,1,0:T(8,128)S(1)} fusion(f32[1,2,128,256]{3,2,1,0:T(8,128)} %bitcast.43, f32[1,2,128,256]{3,2,1,0:T(8,128)} %bitcast.42, f32[1,2,128,256]{3,2,1,0:T(8,128)} %bitcast.41), kind=kLoop, calls=%fused_computation.56 | loop fusion | flops 393216 | bytes 1572864 | tf_op jit(solution)/shard_map/stack | solution.py:96
  45.9 0.6 collective-permute-start.3
  46.5 1.0 %fusion.21 = f32[2,256,256]{2,1,0:T(8,128)S(1)} fusion(f32[1,1,256,256]{3,2,0,1:T(8,128)} %copy-done.6, f32[1,1,256,256]{3,2,0,1:T(8,128)S(1)} %get-tuple-element.64), kind=kLoop, calls=%fused_computation.60 | loop fusion | flops 131072 | bytes 1048576 | tf_op jit(solution)/shard_map/jit(_where)/broadcast_in_dim | solution.py:106
  47.5 1.8 %fusion.15 = (f32[4,256,256]{2,1,0:T(8,128)}, f32[4,256,256]{2,1,0:T(8,128)}) fusion(f32[4,1,256,256]{2,3,0,1:T(8,128)S(1)} %copy-done.5, f32[4,2,256,256]{3,2,1,0:T(8,128)S(1)} %copy-done, f32[4,256,256]{1,2,0:T(8,128)S(1)} %copy-done.4), kind=kLoop, calls=%fused_computation.41 | loop fusion | flops 1048576 | bytes 6291456 | tf_op jit(solution)/shard_map/mul | solution.py:146
  49.2 1.6 %maximum_select_fusion = f32[3,2,256,256]{3,2,1,0:T(8,128)S(1)} fusion(f32[3,2,128,256]{3,2,1,0:T(8,128)S(1)} %collective-permute-done.3, f32[1,2,128,256]{3,2,1,0:T(8,128)} %bitcast.43, f32[1,2,128,256]{3,2,1,0:T(8,128)} %bitcast.42, f32[1,2,128,256]{3,2,1,0:T(8,128)} %bitcast.41, pred[]{:T(512)S(6)} %eq.72), kind=kLoop, calls=%fused_computation.18 | loop fusion | flops 2752512 | bytes 3145729 | tf_op jit(solution)/shard_map/jit(_where)/select_n | solution.py:100
  51.7 1.6 %fusion.20 = f32[3,512,256]{2,1,0:T(8,128)S(1)} fusion(f32[3,512,256]{2,1,0:T(8,128)S(1)} %bitcast.249, f32[4,2,256,256]{3,2,0,1:T(8,128)S(1)} %select_select_fusion), kind=kOutput, calls=%fused_computation.55 | convolution fusion | flops 1207959552 | bytes 3932160 | tf_op jit(solution)/shard_map/dot_general | solution.py:13
  53.2 1.6 %fusion.19 = f32[3,512,256]{2,1,0:T(8,128)S(1)} fusion(f32[3,512,256]{2,1,0:T(8,128)S(1)} %bitcast.250, f32[4,2,256,256]{3,2,0,1:T(8,128)S(1)} %select_select_fusion), kind=kOutput, calls=%fused_computation.53 | convolution fusion | flops 1207959552 | bytes 3932160 | tf_op jit(solution)/shard_map/dot_general | solution.py:13
  55.2 1.1 %fusion.34 = f32[2,512,256]{2,1,0:T(8,128)S(1)} fusion(f32[2,512,256]{2,1,0:T(8,128)S(1)} %bitcast.261, f32[1,2,256,256]{3,2,0,1:T(8,128)S(1)} %slice.396, f32[3,1,256,256]{3,2,0,1:T(8,128)S(1)} %get-tuple-element.42, f32[3,1,256,256]{3,2,0,1:T(8,128)S(1)} %get-tuple-element.41), kind=kOutput, calls=%fused_computation.83 | convolution fusion | flops 805568512 | bytes 4194304 | tf_op jit(solution)/shard_map/dot_general | solution.py:13
  56.3 1.1 %fusion.39 = f32[2,512,256]{2,1,0:T(8,128)S(1)} fusion(f32[2,512,256]{2,1,0:T(8,128)S(1)} %bitcast.262, f32[1,2,256,256]{3,2,0,1:T(8,128)S(1)} %slice.396, f32[3,1,256,256]{3,2,0,1:T(8,128)S(1)} %get-tuple-element.42, f32[3,1,256,256]{3,2,0,1:T(8,128)S(1)} %get-tuple-element.41), kind=kOutput, calls=%fused_computation.89 | convolution fusion | flops 805568512 | bytes 4194304 | tf_op jit(solution)/shard_map/dot_general | solution.py:13
  57.7 1.0 %fusion.61 = f32[2,512,256]{2,1,0:T(8,128)S(1)} fusion(f32[2,512,256]{2,1,0:T(8,128)S(1)} %bitcast.253, f32[1,2,256,256]{3,2,1,0:T(8,128)S(1)} %fusion.27), kind=kOutput, calls=%fused_computation.133 | convolution fusion | flops 805306368 | bytes 2359296 | tf_op jit(solution)/shard_map/dot_general | solution.py:13
  58.7 1.0 %fusion.60 = f32[2,512,256]{2,1,0:T(8,128)S(1)} fusion(f32[2,512,256]{2,1,0:T(8,128)S(1)} %bitcast.254, f32[1,2,256,256]{3,2,1,0:T(8,128)S(1)} %fusion.27), kind=kOutput, calls=%fused_computation.131 | convolution fusion | flops 805306368 | bytes 2359296 | tf_op jit(solution)/shard_map/dot_general | solution.py:13
  59.7 0.7 fusion.67
  60.4 0.6 fusion.72
  61.0 0.6 fusion.70
  61.6 0.8 %fusion.11 = f32[1,256,256]{1,2,0:T(8,128)S(1)} fusion(f32[256,256]{1,0:T(8,128)S(1)} %fusion.72, f32[2,256,256]{2,1,0:T(8,128)S(1)} %get-tuple-element.53, f32[2,256,256]{2,1,0:T(8,128)S(1)} %copy-done.1), kind=kOutput, calls=%fused_computation.27 | convolution fusion | flops 201392128 | bytes 1048576 | tf_op jit(solution)/shard_map/...ji,...jk->...ik/dot_general | solution.py:21
  62.4 0.6 fusion.10
  63.4 1.0 %fusion.59 = f32[2,512,256]{2,1,0:T(8,128)S(1)} fusion(f32[2,512,256]{2,1,0:T(8,128)S(1)} %bitcast.255, f32[1,2,256,256]{2,3,1,0:T(8,128)S(1)} %maximum_bitcast_fusion.4), kind=kOutput, calls=%fused_computation.129 | convolution fusion | flops 805306368 | bytes 2359296 | tf_op jit(solution)/shard_map/dot_general | solution.py:13
  64.4 1.0 %fusion.58 = f32[2,512,256]{2,1,0:T(8,128)S(1)} fusion(f32[2,512,256]{2,1,0:T(8,128)S(1)} %bitcast.256, f32[1,2,256,256]{2,3,1,0:T(8,128)S(1)} %maximum_bitcast_fusion.4), kind=kOutput, calls=%fused_computation.127 | convolution fusion | flops 805306368 | bytes 2359296 | tf_op jit(solution)/shard_map/dot_general | solution.py:13
  65.8 1.1 %fusion.85 = f32[2,512,256]{2,1,0:T(8,128)S(1)} fusion(f32[2,512,256]{2,1,0:T(8,128)S(1)} %bitcast.251, f32[2,512,256]{2,1,0:T(8,128)S(1)} %fusion.60, f32[2,512,256]{2,1,0:T(8,128)S(1)} %fusion.61), kind=kOutput, calls=%fused_computation.168 | convolution fusion | flops 805437440 | bytes 3145728 | tf_op jit(solution)/shard_map/...ij,...kj->...ik/dot_general | solution.py:17
  66.9 1.1 %fusion.87 = f32[2,512,256]{2,1,0:T(8,128)S(1)} fusion(f32[2,512,256]{2,1,0:T(8,128)S(1)} %bitcast.252, f32[2,512,256]{2,1,0:T(8,128)S(1)} %fusion.61, f32[2,512,256]{2,1,0:T(8,128)S(1)} %fusion.60), kind=kOutput, calls=%fused_computation.170 | convolution fusion | flops 805437440 | bytes 3145728 | tf_op jit(solution)/shard_map/...ij,...kj->...ik/dot_general | solution.py:17
  68.0 1.0 %fusion.22 = f32[2,2,256,64]{3,2,0,1:T(8,128)} fusion(s32[]{:T(128)S(6)} %select_n.70, f32[2,1,256,256]{3,2,0,1:T(8,128)S(1)} %get-tuple-element.51, f32[2,1,256,256]{3,2,0,1:T(8,128)S(1)} %get-tuple-element.52), kind=kLoop, calls=%fused_computation.61 | loop fusion | flops 65536 | bytes 1310724 | tf_op jit(solution)/shard_map/stack | solution.py:31
  69.0 2.0 %copy.75 = f32[2,2,256,64]{2,3,1,0:T(8,128)} copy(f32[2,2,256,64]{3,2,0,1:T(8,128)} %fusion.22) | data formatting | bytes 524288
  71.2 1.1 %copy-done.3 = f32[4,256,256]{2,1,0:T(8,128)S(1)} copy-done((f32[4,256,256]{2,1,0:T(8,128)S(1)}, f32[4,256,256]{2,1,0:T(8,128)}, u32[]{:S(2)}) %copy-start.3) | copy-done | bytes 1048600
  72.3 1.1 %subtract_reduce_fusion = (f32[4,2]{1,0:T(4,128)S(1)}, f32[4,2]{1,0:T(4,128)S(1)}) fusion(f32[2,256,256]{2,1,0:T(8,128)S(1)} %get-tuple-element.48, f32[4,256,256]{2,1,0:T(8,128)S(1)} %copy-done.3, f32[2,256,256]{2,1,0:T(8,128)S(1)} %get-tuple-element.47, f32[4,256,256]{2,1,0:T(8,128)S(1)} %copy-done.2), kind=kLoop, calls=%fused_computation.10 | loop fusion | flops 4194288 | bytes 3145792 | tf_op jit(solution)/shard_map/reduce_sum | solution.py:149
  73.3 1.3 %multiply_subtract_fusion = f32[4,2]{1,0:T(4,128)S(1)} fusion(f32[4,2]{1,0:T(4,128)S(1)} %get-tuple-element.33, f32[4,2]{1,0:T(4,128)S(1)} %get-tuple-element.32, f32[]{:T(128)} %get-tuple-element.35, f32[]{:T(128)} %get-tuple-element.34), kind=kLoop, calls=%fused_computation.172 | loop fusion | flops 24 | bytes 104 | tf_op jit(solution)/shard_map/sub | solution.py:150
  74.6 0.6 copy.74
  (61 shorter events, 5.6 us)
Async XLA Ops:
  1.4 2.4 %copy-start.7 = (f32[2,256,256]{2,1,0:T(8,128)S(1)}, f32[2,256,256]{2,1,0:T(8,128)}, u32[]{:S(2)}) copy-start(f32[2,256,256]{2,1,0:T(8,128)} %param.9) | copy-start | bytes 1572868
  17.6 4.6 %copy-start.6 = (f32[1,1,256,256]{3,2,0,1:T(8,128)}, f32[1,1,256,256]{3,2,0,1:T(8,128)S(1)}, u32[]{:S(2)}) copy-start(f32[1,1,256,256]{3,2,0,1:T(8,128)S(1)} %get-tuple-element.65) | copy-start | bytes 786436
  18.4 12.1 %collective-permute-start = (f32[2,128,256]{2,1,0:T(8,128)}, f32[2,128,256]{2,1,0:T(8,128)}, u32[]{:S(2)}, u32[]{:S(2)}) collective-permute-start(f32[2,128,256]{2,1,0:T(8,128)} %fusion.57), channel_id=1, source_target_pairs={{0,4},{4,8},{8,12},{12,0},{1,5},{5,9},{9,13},{13,1},{2,6},{6,10},{... | collective-permute-start | bytes 786440 | tf_op jit(solution)/shard_map/ppermute | solution.py:95
  19.7 22.1 %collective-permute-start.1 = (f32[2,128,256]{2,1,0:T(8,128)}, f32[2,128,256]{2,1,0:T(8,128)}, u32[]{:S(2)}, u32[]{:S(2)}) collective-permute-start(f32[2,128,256]{2,1,0:T(8,128)} %fusion.57), channel_id=1, source_target_pairs={{0,8},{4,12},{8,0},{12,4},{1,9},{5,13},{9,1},{13,5},{2,10},{6,14},... | collective-permute-start | bytes 786440 | tf_op jit(solution)/shard_map/ppermute | solution.py:95
  20.7 24.0 %collective-permute-start.2 = (f32[2,128,256]{2,1,0:T(8,128)}, f32[2,128,256]{2,1,0:T(8,128)}, u32[]{:S(2)}, u32[]{:S(2)}) collective-permute-start(f32[2,128,256]{2,1,0:T(8,128)} %fusion.57), channel_id=1, source_target_pairs={{0,12},{4,0},{8,4},{12,8},{1,13},{5,1},{9,5},{13,9},{2,14},{6,2},{... | collective-permute-start | bytes 786440 | tf_op jit(solution)/shard_map/ppermute | solution.py:95
  22.2 1.7 %copy-start = (f32[4,2,256,256]{3,2,1,0:T(8,128)S(1)}, f32[4,2,256,256]{3,2,1,0:T(8,128)}, u32[]{:S(2)}) copy-start(f32[4,2,256,256]{3,2,1,0:T(8,128)} %param.10) | copy-start | bytes 6291460
  30.5 16.9 %copy-start.4 = (f32[4,256,256]{1,2,0:T(8,128)S(1)}, f32[4,256,256]{1,2,0:T(8,128)}, u32[]{:S(2)}) copy-start(f32[4,256,256]{1,2,0:T(8,128)} %copy.73) | copy-start | bytes 3145732
  30.5 16.9 %copy-start.5 = (f32[4,1,256,256]{2,3,0,1:T(8,128)S(1)}, f32[4,1,256,256]{2,3,0,1:T(8,128)}, u32[]{:S(2)}) copy-start(f32[4,1,256,256]{2,3,0,1:T(8,128)} %copy.83) | copy-start | bytes 3145732
  45.9 3.4 %collective-permute-start.3 = (f32[3,2,128,256]{3,2,1,0:T(8,128)S(1)}, f32[3,2,128,256]{3,2,1,0:T(8,128)S(1)}, u32[]{:S(2)}, u32[]{:S(2)}) collective-permute-start(f32[3,2,128,256]{3,2,1,0:T(8,128)S(1)} %pad_maximum_fusion.7), channel_id=1, source_target_pairs={{0,1},{1,0},{2,3},{3,2},{4,5},{5,4},{6,7},{7,6},{8,9},{9,8},{10,11... | collective-permute-start | bytes 2359304 | tf_op jit(solution)/shard_map/ppermute | solution.py:98
  57.7 2.0 %copy-start.1 = (f32[2,256,256]{2,1,0:T(8,128)S(1)}, f32[2,256,256]{2,1,0:T(8,128)}, u32[]{:S(2)}) copy-start(f32[2,256,256]{2,1,0:T(8,128)} %param.11) | copy-start | bytes 1572868
  69.0 2.2 %copy-start.2 = (f32[4,256,256]{2,1,0:T(8,128)S(1)}, f32[4,256,256]{2,1,0:T(8,128)}, u32[]{:S(2)}) copy-start(f32[4,256,256]{2,1,0:T(8,128)} %get-tuple-element.43) | copy-start | bytes 3145732
  71.0 1.2 %copy-start.3 = (f32[4,256,256]{2,1,0:T(8,128)S(1)}, f32[4,256,256]{2,1,0:T(8,128)}, u32[]{:S(2)}) copy-start(f32[4,256,256]{2,1,0:T(8,128)} %get-tuple-element.44) | copy-start | bytes 3145732

commit v3 on v2

--- a/solution.py
+++ b/solution.py
@@ -118,7 +118,13 @@
 
     eye = jnp.eye(size, dtype=jnp.float32)
     start_full = jnp.stack([eye, jnp.zeros_like(eye)])
-    if tm_count <= 8:
+    if tm_count == 4:
+        pairs = cmul(pieces[1::2], pieces[0::2])
+        ends = cmul(jnp.stack([pairs[1], pieces[2]], 0), pairs[0][None])
+        final_state = ends[0]
+        options = jnp.stack([start_full, pieces[0], pairs[0], ends[1]], 0)
+        prefix = lax.dynamic_index_in_dim(options, tm_index, 0, keepdims=False)
+    elif tm_count <= 8:
         scan = pieces
         shift = 1
         while shift < tm_count:
@@ -138,17 +144,17 @@
 
         (final_state, prefix, _), _ = lax.scan(lap, (start_full, start_full, 0), pieces)
     states = cmul(jnp.stack(running, 0), prefix[None])
+    overlap = cmul_adjoint_left(target, final_state)
 
     correlation_real = jnp.sum(target[0] * final_state[0] + target[1] * final_state[1])
     correlation_imag = jnp.sum(target[0] * final_state[1] - target[1] * final_state[0])
-    overlap = cmul_adjoint_left(target, final_state)
     weighted = cmul_adjoint_right(cmul(states, overlap[None]), states)
     control_real = (0.5 * (controls[:, 0] + jnp.swapaxes(controls[:, 0], 1, 2)))[:, None]
     control_imag = (0.5 * (controls[:, 1] - jnp.swapaxes(controls[:, 1], 1, 2)))[:, None]
     trace_real = jnp.sum(control_real * weighted[None, :, 0] + control_imag * weighted[None, :, 1], axis=(2, 3))
     trace_imag = jnp.sum(control_real * weighted[None, :, 1] - control_imag * weighted[None, :, 0], axis=(2, 3))
     gradient = correlation_real * trace_imag - correlation_imag * trace_real
-    propagators = lax.dynamic_slice_in_dim(states, col_start, col_width, 3)
+    propagators = cmul(jnp.stack(running, 0), lax.dynamic_slice_in_dim(prefix, col_start, col_width, 2)[None])
     return (gradient, propagators)
 
 

time: 75.7 us -> 73.6 us (0.972)
  other arithmetic: 17.2 us -> 14.9 us
  local copies, waits for them, and re-layouts: 14.6 us -> 13.1 us
  matrix products: 23.7 us -> 24.9 us
    mul x1, other arithmetic: 1.77 us -> 0.27 us  [shards(): 0.5 * (controls[:, 0] + jnp.swapaxes(controls[:, 0], 1, 2))]
    unnamed x21 -> x17, local copies, waits for them, and re-layouts: 7.64 us -> 6.15 us
    dot_general x16 -> x18, matrix products: 18.9 us -> 20.4 us  [mm(): return jnp.matmul(left, right, precision=mode)]
    another operation x11, other arithmetic: 2.4 us -> 1.2 us  [cmul(): return jnp.stack([real, imag], -3)]
  transfers between devices with their start and end apart: 4 -> 4, of which waited for: 2 -> 3; matrix products, arithmetic and copies ran while one was open for 14% -> 13% of each run, Pallas kernels for 0% -> 0%
where the time goes in v3:
time: 73.6 us; the launch traced here: 73.2 us
  matrix products  24.9 us (34%)
  other arithmetic  14.9 us (20%)
  waiting for transfers between devices  14.6 us (20%)
  local copies, waits for them, and re-layouts  13.1 us (18%)
  starting transfers between devices  4.33 us (6%)
  between operations  1.28 us (2%)
    dot_general x18, matrix products, mm(): return jnp.matmul(left, right, precision=mode)  20.4 us
    ppermute x3, waiting for transfers between devices, shards(): received.append(lax.ppermute(mine, 'tm', pairs))  14.1 us
    unnamed x17, local copies, waits for them, and re-layouts  6.15 us
    ppermute x3, starting transfers between devices, shards(): received.append(lax.ppermute(mine, 'tm', pairs))  3.77 us
    squeeze x1, local copies, waits for them, and re-layouts, shards(): controls[:, 1] - jnp.swapaxes(controls[:, 1], 1, 2)  2.53 us
    dot_general x4, matrix products, mm_tn(): return jnp.einsum('...ji,...jk->...ik', left, right, precision=fast_mode)  2.38 us
    dot_general x2, matrix products, mm_nt(): return jnp.einsum('...ij,...kj->...ik', left, right, precision=fast_mode)  2.2 us
    reduce_sum x1, other arithmetic, shards(): jnp.sum(amplitudes[:, :, None, None, None] * controls[:, None], axis=0)  2.1 us
  transfers between devices with their start and end apart: 4, of which 3 were waited for; matrix products, arithmetic and copies ran while one was open for 13% of the time, Pallas kernels for 0%

profile of v3, /device:TPU:13, one launch (start us, length us, event | category | flops | bytes accessed | tf_op | source)
XLA Modules:
  0.0 73.2 jit_solution(13101892183040424544)
XLA Ops:
  0.6 0.8 %copy.65 = f32[4,2]{1,0:T(4,128)S(1)} copy(f32[4,2]{0,1:T(2,128)} %param.8) | data formatting | bytes 64 | tf_op args[0]
  1.4 2.1 %multiply_reduce_fusion = f32[2,2,256,256]{3,2,1,0:T(8,128)S(1)} fusion(f32[4,2,256,256]{3,2,1,0:T(8,128)} %param.10, f32[4,2]{1,0:T(4,128)S(1)} %copy.65), kind=kLoop, calls=%fused_computation | loop fusion | flops 1835008 | bytes 3145760 | tf_op jit(solution)/shard_map/reduce_sum | solution.py:77
  5.2 1.1 %fusion.66 = f32[2,512,256]{2,1,0:T(8,128)S(1)} fusion(f32[2,512,256]{2,1,0:T(8,128)S(1)} %bitcast.261, f32[2,256,256]{2,1,0:T(8,128)S(1)} %copy.67, f32[2,2,256,256]{2,3,0,1:T(8,128)S(1)} %broadcast_add_fusion), kind=kOutput, calls=%fused_computation.151 | convolution fusion | flops 805568512 | bytes 3145728 | tf_op jit(solution)/shard_map/dot_general | solution.py:13
  6.4 1.1 %fusion.36 = f32[2,512,256]{2,1,0:T(8,128)S(1)} fusion(f32[2,512,256]{2,1,0:T(8,128)S(1)} %bitcast.262, f32[2,256,256]{2,1,0:T(8,128)S(1)} %copy.69), kind=kOutput, calls=%fused_computation.102 | convolution fusion | flops 805568512 | bytes 2621440 | tf_op jit(solution)/shard_map/dot_general | solution.py:13
  7.8 2.0 %fusion.7 = f32[2,2,512,256]{3,2,1,0:T(8,128)S(1)} fusion(f32[1,2,2,256,256]{4,3,1,2,0:T(8,128)S(1)} %get-tuple-element.70, f32[1,2,512,256]{3,2,0,1:T(8,128)S(1)} %bitcast.275, f32[1,2,512,256]{3,2,0,1:T(8,128)S(1)} %bitcast.263), kind=kOutput, calls=%fused_computation.19 | convolution fusion | flops 1611137024 | bytes 4718592 | tf_op jit(solution)/shard_map/dot_general | solution.py:13
  9.8 2.0 %fusion.10 = f32[2,2,512,256]{3,2,1,0:T(8,128)S(1)} fusion(f32[1,2,2,256,256]{4,3,1,2,0:T(8,128)S(1)} %get-tuple-element.70, f32[1,2,512,256]{3,2,0,1:T(8,128)S(1)} %bitcast.276, f32[1,2,512,256]{3,2,0,1:T(8,128)S(1)} %bitcast.264), kind=kOutput, calls=%fused_computation.20 | convolution fusion | flops 1611137024 | bytes 4718592 | tf_op jit(solution)/shard_map/dot_general | solution.py:13
  12.7 1.1 %fusion.28 = f32[2,512,256]{2,1,0:T(8,128)S(1)} fusion(f32[2,512,256]{2,1,0:T(8,128)S(1)} %bitcast.273, f32[2,2,256,256]{3,2,0,1:T(8,128)S(1)} %get-tuple-element.36), kind=kOutput, calls=%fused_computation.81 | convolution fusion | flops 805306368 | bytes 2621440 | tf_op jit(solution)/shard_map/dot_general | solution.py:13
  13.8 1.1 %fusion.30 = f32[2,512,256]{2,1,0:T(8,128)S(1)} fusion(f32[2,512,256]{2,1,0:T(8,128)S(1)} %bitcast.274, f32[2,2,256,256]{3,2,0,1:T(8,128)S(1)} %get-tuple-element.36, f32[256,256]{1,0:T(8,128)S(1)} %fusion.59), kind=kOutput, calls=%fused_computation.84 | convolution fusion | flops 805437440 | bytes 2883584 | tf_op jit(solution)/shard_map/dot_general | solution.py:13
  15.3 0.9 %fusion.87 = (f32[1,2,256,256]{3,2,0,1:T(8,128)}, f32[1,2,256,256]{3,2,0,1:T(8,128)S(1)}) fusion(f32[2,2,256,256]{3,2,0,1:T(8,128)S(1)} %maximum_add_fusion), kind=kLoop, calls=%fused_computation.180 | loop fusion | bytes 2097152 | tf_op jit(solution)/shard_map/slice | solution.py:83
  16.1 0.8 %convolution_bitcast_fusion.1 = f32[1,512,256]{2,1,0:T(8,128)S(1)} fusion(f32[512,256]{1,0:T(8,128)S(1)} %bitcast.283, f32[2,2,256,256]{3,2,0,1:T(8,128)S(1)} %maximum_add_fusion), kind=kOutput, calls=%fused_computation.23 | convolution fusion | flops 402653184 | bytes 1310720 | tf_op jit(solution)/shard_map/dot_general | solution.py:13
  16.9 0.6 convolution_bitcast_fusion
  17.6 0.8 %fusion.39 = f32[2,128,256]{2,1,0:T(8,128)} fusion(s32[]{:T(128)S(6)} %select_n.58, f32[1,1,256,256]{3,2,0,1:T(8,128)S(1)} %get-tuple-element.68, f32[1,1,256,256]{3,2,0,1:T(8,128)S(1)} %get-tuple-element.69), kind=kLoop, calls=%fused_computation.105 | loop fusion | flops 65536 | bytes 786436 | tf_op jit(solution)/shard_map/dynamic_slice | solution.py:90
  18.4 1.3 %collective-permute-start = (f32[2,128,256]{2,1,0:T(8,128)}, f32[2,128,256]{2,1,0:T(8,128)}, u32[]{:S(2)}, u32[]{:S(2)}) collective-permute-start(f32[2,128,256]{2,1,0:T(8,128)} %fusion.39), channel_id=1, source_target_pairs={{0,4},{4,8},{8,12},{12,0},{1,5},{5,9},{9,13},{13,1},{2,6},{6,10},{... | collective-permute-start | bytes 786440 | tf_op jit(solution)/shard_map/ppermute | solution.py:95
  19.7 1.0 %collective-permute-start.1 = (f32[2,128,256]{2,1,0:T(8,128)}, f32[2,128,256]{2,1,0:T(8,128)}, u32[]{:S(2)}, u32[]{:S(2)}) collective-permute-start(f32[2,128,256]{2,1,0:T(8,128)} %fusion.39), channel_id=1, source_target_pairs={{0,8},{4,12},{8,0},{12,4},{1,9},{5,13},{9,1},{13,5},{2,10},{6,14},... | collective-permute-start | bytes 786440 | tf_op jit(solution)/shard_map/ppermute | solution.py:95
  20.7 1.5 %collective-permute-start.2 = (f32[2,128,256]{2,1,0:T(8,128)}, f32[2,128,256]{2,1,0:T(8,128)}, u32[]{:S(2)}, u32[]{:S(2)}) collective-permute-start(f32[2,128,256]{2,1,0:T(8,128)} %fusion.39), channel_id=1, source_target_pairs={{0,12},{4,0},{8,4},{12,8},{1,13},{5,1},{9,5},{13,9},{2,14},{6,2},{... | collective-permute-start | bytes 786440 | tf_op jit(solution)/shard_map/ppermute | solution.py:95
  22.2 1.3 %maximum_maximum_fusion = f32[2,2,256,256]{3,2,0,1:T(8,128)S(1)} fusion(f32[1,1,256,256]{3,2,0,1:T(8,128)S(1)} %get-tuple-element.69, f32[1,1,256,256]{3,2,0,1:T(8,128)S(1)} %get-tuple-element.68, f32[1,2,256,256]{3,2,0,1:T(8,128)} %get-tuple-element.66), kind=kLoop, calls=%fused_computation.40 | loop fusion | flops 524288 | bytes 2097152 | tf_op jit(solution)/shard_map/stack | solution.py:146
  23.9 1.6 %fusion.84 = (f32[4,1,256,256]{3,2,1,0:T(8,128)}, f32[4,256,256]{2,1,0:T(8,128)}) fusion(f32[4,2,256,256]{3,2,1,0:T(8,128)S(1)} %copy-done), kind=kLoop, calls=%fused_computation.177 | loop fusion | bytes 4194304 | tf_op jit(solution)/shard_map/slice | solution.py:152
  25.5 2.5 %copy.117 = f32[4,1,256,256]{2,3,0,1:T(8,128)} copy(f32[4,1,256,256]{3,2,1,0:T(8,128)} %get-tuple-element.43) | data formatting | bytes 2097152
  28.0 2.5 %copy.95 = f32[4,256,256]{1,2,0:T(8,128)} copy(f32[4,256,256]{2,1,0:T(8,128)} %get-tuple-element.44) | data formatting | bytes 2097152 | tf_op jit(solution)/shard_map/squeeze | solution.py:153
  30.6 11.2 %collective-permute-done.1 = f32[2,128,256]{2,1,0:T(8,128)} collective-permute-done((f32[2,128,256]{2,1,0:T(8,128)}, f32[2,128,256]{2,1,0:T(8,128)}, u32[]{:S(2)}, u32[]{:S(2)}) %collective-permute-start.1) | collective-permute-done | bytes 262176 | tf_op jit(solution)/shard_map/ppermute | solution.py:95
  41.8 2.9 %collective-permute-done.2 = f32[2,128,256]{2,1,0:T(8,128)} collective-permute-done((f32[2,128,256]{2,1,0:T(8,128)}, f32[2,128,256]{2,1,0:T(8,128)}, u32[]{:S(2)}, u32[]{:S(2)}) %collective-permute-start.2) | collective-permute-done | bytes 262176 | tf_op jit(solution)/shard_map/ppermute | solution.py:95
  44.7 1.2 %pad_maximum_fusion.7 = f32[3,2,128,256]{3,2,1,0:T(8,128)S(1)} fusion(f32[1,2,128,256]{3,2,1,0:T(8,128)} %bitcast.43, f32[1,2,128,256]{3,2,1,0:T(8,128)} %bitcast.42, f32[1,2,128,256]{3,2,1,0:T(8,128)} %bitcast.41), kind=kLoop, calls=%fused_computation.51 | loop fusion | flops 393216 | bytes 1572864 | tf_op jit(solution)/shard_map/stack | solution.py:96
  45.8 0.6 collective-permute-start.3
  46.4 1.0 %fusion.20 = f32[2,256,256]{2,1,0:T(8,128)S(1)} fusion(f32[1,1,256,256]{3,2,0,1:T(8,128)} %copy-done.4, f32[1,1,256,256]{3,2,0,1:T(8,128)S(1)} %get-tuple-element.68), kind=kLoop, calls=%fused_computation.55 | loop fusion | flops 131072 | bytes 1048576 | tf_op jit(solution)/shard_map/jit(_where)/broadcast_in_dim | solution.py:106
  47.8 0.5 collective-permute-done.3
  48.3 1.5 %maximum_select_fusion = f32[3,2,256,256]{3,2,1,0:T(8,128)S(1)} fusion(f32[3,2,128,256]{3,2,1,0:T(8,128)S(1)} %collective-permute-done.3, f32[1,2,128,256]{3,2,1,0:T(8,128)} %bitcast.43, f32[1,2,128,256]{3,2,1,0:T(8,128)} %bitcast.42, f32[1,2,128,256]{3,2,1,0:T(8,128)} %bitcast.41, pred[]{:T(512)S(6)} %eq.69), kind=kLoop, calls=%fused_computation.21 | loop fusion | flops 2752512 | bytes 3145729 | tf_op jit(solution)/shard_map/jit(_where)/select_n | solution.py:100
  50.6 1.1 %fusion.24 = f32[2,512,256]{2,1,0:T(8,128)S(1)} fusion(f32[2,512,256]{2,1,0:T(8,128)S(1)} %bitcast.269, f32[2,2,256,256]{3,2,0,1:T(8,128)S(1)} %get-tuple-element.57), kind=kOutput, calls=%fused_computation.70 | convolution fusion | flops 805306368 | bytes 2621440 | tf_op jit(solution)/shard_map/dot_general | solution.py:13
  51.6 1.1 %fusion.25 = f32[2,512,256]{2,1,0:T(8,128)S(1)} fusion(f32[2,512,256]{2,1,0:T(8,128)S(1)} %bitcast.270, f32[2,2,256,256]{3,2,0,1:T(8,128)S(1)} %get-tuple-element.57), kind=kOutput, calls=%fused_computation.72 | convolution fusion | flops 805306368 | bytes 2621440 | tf_op jit(solution)/shard_map/dot_general | solution.py:13
  53.2 1.0 %fusion.45 = f32[2,512,256]{2,1,0:T(8,128)S(1)} fusion(f32[2,512,256]{2,1,0:T(8,128)S(1)} %bitcast.271, f32[2,256,256]{2,1,0:T(8,128)S(1)} %get-tuple-element.56), kind=kOutput, calls=%fused_computation.119 | convolution fusion | flops 805306368 | bytes 2359296 | tf_op jit(solution)/shard_map/dot_general | solution.py:13
  54.2 1.0 %fusion.44 = f32[2,512,256]{2,1,0:T(8,128)S(1)} fusion(f32[2,512,256]{2,1,0:T(8,128)S(1)} %bitcast.272, f32[2,256,256]{2,1,0:T(8,128)S(1)} %get-tuple-element.55), kind=kOutput, calls=%fused_computation.117 | convolution fusion | flops 805306368 | bytes 2359296 | tf_op jit(solution)/shard_map/dot_general | solution.py:13
  55.4 0.9 %copy-done.1 = f32[2,256,256]{2,1,0:T(8,128)S(1)} copy-done((f32[2,256,256]{2,1,0:T(8,128)S(1)}, f32[2,256,256]{2,1,0:T(8,128)}, u32[]{:S(2)}) %copy-start.1) | copy-done | bytes 524312
  56.3 0.6 fusion.56
  56.9 0.8 %fusion.51 = (f32[]{:T(128)}, f32[]{:T(128)}) fusion(f32[2,256,256]{2,1,0:T(8,128)S(1)} %get-tuple-element.53, f32[2,256,256]{2,1,0:T(8,128)S(1)} %get-tuple-element.54, f32[2,256,256]{2,1,0:T(8,128)S(1)} %copy-done.1), kind=kLoop, calls=%fused_computation.132 | loop fusion | flops 524286 | bytes 1048584 | tf_op jit(solution)/shard_map/reduce_sum | solution.py:149
  57.7 0.6 fusion.54
  58.4 1.0 %fusion.43 = f32[2,512,256]{2,1,0:T(8,128)S(1)} fusion(f32[2,512,256]{2,1,0:T(8,128)S(1)} %bitcast.257, f32[4,2,256,256]{3,2,0,1:T(8,128)S(1)} %fusion, s32[]{:T(128)S(6)} %select_n.66), kind=kOutput, calls=%fused_computation.113 | convolution fusion | flops 805306368 | bytes 2359300 | tf_op jit(solution)/shard_map/dot_general | solution.py:13
  59.4 1.2 %fusion.76 = f32[2,512,64]{1,2,0:T(8,128)S(1)} fusion(f32[2,512,256]{2,1,0:T(8,128)S(1)} %bitcast.258, f32[4,2,256,256]{3,2,0,1:T(8,128)S(1)} %fusion, s32[]{:T(128)S(6)} %select_n.67, s32[]{:T(128)S(6)} %select_n.69), kind=kOutput, calls=%fused_computation.164 | convolution fusion | flops 201326592 | bytes 1441800 | tf_op jit(solution)/shard_map/dot_general | solution.py:13
  60.6 1.2 %fusion.75 = f32[2,512,64]{1,2,0:T(8,128)S(1)} fusion(f32[2,512,256]{2,1,0:T(8,128)S(1)} %bitcast.259, f32[4,2,256,256]{3,2,0,1:T(8,128)S(1)} %fusion, s32[]{:T(128)S(6)} %select_n.67, s32[]{:T(128)S(6)} %add.151, s32[]{:T(128)S(6)} %select_n.69), kind=kOutput, calls=%fused_computation.162 | convolution fusion | flops 201326592 | bytes 1441804 | tf_op jit(solution)/shard_map/dot_general | solution.py:13
  61.7 1.2 %fusion.42 = f32[2,512,256]{2,1,0:T(8,128)S(1)} fusion(f32[2,512,256]{2,1,0:T(8,128)S(1)} %bitcast.260, f32[4,2,256,256]{3,2,0,1:T(8,128)S(1)} %fusion, s32[]{:T(128)S(6)} %select_n.66, s32[]{:T(128)S(6)} %add.151), kind=kOutput, calls=%fused_computation.111 | convolution fusion | flops 805306368 | bytes 2359304 | tf_op jit(solution)/shard_map/dot_general | solution.py:13
  63.0 0.6 fusion.14
  63.6 0.6 fusion.13
  64.6 1.0 %fusion.41 = f32[2,512,256]{2,1,0:T(8,128)S(1)} fusion(f32[2,512,256]{2,1,0:T(8,128)S(1)} %bitcast.267, f32[1,2,256,256]{2,3,1,0:T(8,128)S(1)} %maximum_bitcast_fusion), kind=kOutput, calls=%fused_computation.109 | convolution fusion | flops 805306368 | bytes 2359296 | tf_op jit(solution)/shard_map/dot_general | solution.py:13
  65.6 1.0 %fusion.40 = f32[2,512,256]{2,1,0:T(8,128)S(1)} fusion(f32[2,512,256]{2,1,0:T(8,128)S(1)} %bitcast.268, f32[1,2,256,256]{2,3,1,0:T(8,128)S(1)} %maximum_bitcast_fusion), kind=kOutput, calls=%fused_computation.107 | convolution fusion | flops 805306368 | bytes 2359296 | tf_op jit(solution)/shard_map/dot_general | solution.py:13
  66.9 1.1 %fusion.69 = f32[2,512,256]{2,1,0:T(8,128)S(1)} fusion(f32[2,512,256]{2,1,0:T(8,128)S(1)} %bitcast.265, f32[2,512,256]{2,1,0:T(8,128)S(1)} %fusion.42, f32[2,512,256]{2,1,0:T(8,128)S(1)} %fusion.43), kind=kOutput, calls=%fused_computation.153 | convolution fusion | flops 805437440 | bytes 3145728 | tf_op jit(solution)/shard_map/...ij,...kj->...ik/dot_general | solution.py:17
  68.0 1.1 %fusion.71 = f32[2,512,256]{2,1,0:T(8,128)S(1)} fusion(f32[2,512,256]{2,1,0:T(8,128)S(1)} %bitcast.266, f32[2,512,256]{2,1,0:T(8,128)S(1)} %fusion.43, f32[2,512,256]{2,1,0:T(8,128)S(1)} %fusion.42), kind=kOutput, calls=%fused_computation.155 | convolution fusion | flops 805437440 | bytes 3145728 | tf_op jit(solution)/shard_map/...ij,...kj->...ik/dot_general | solution.py:17
  69.2 0.7 copy.99
  70.1 1.1 %subtract_reduce_fusion = (f32[4,2]{1,0:T(4,128)S(1)}, f32[4,2]{1,0:T(4,128)S(1)}) fusion(f32[2,256,256]{2,1,0:T(8,128)S(1)} %get-tuple-element.46, f32[4,256,256]{2,1,0:T(8,128)S(1)} %get-tuple-element.42, f32[2,256,256]{2,1,0:T(8,128)S(1)} %get-tuple-element.45, f32[4,256,256]{2,1,0:T(8,128)S(1)} %get-tuple-element.41), kind=kLoop, calls=%fused_computation.12 | loop fusion | flops 4194288 | bytes 3145792 | tf_op jit(solution)/shard_map/reduce_sum | solution.py:155
  71.2 1.3 %multiply_subtract_fusion = f32[4,2]{1,0:T(4,128)S(1)} fusion(f32[4,2]{1,0:T(4,128)S(1)} %get-tuple-element.33, f32[4,2]{1,0:T(4,128)S(1)} %get-tuple-element.32, f32[]{:T(128)} %get-tuple-element.35, f32[]{:T(128)} %get-tuple-element.34), kind=kLoop, calls=%fused_computation.165 | loop fusion | flops 24 | bytes 104 | tf_op jit(solution)/shard_map/sub | solution.py:156
  72.5 0.6 copy.98
  (62 shorter events, 6.4 us)
Async XLA Ops:
  1.4 2.4 %copy-start.5 = (f32[2,256,256]{2,1,0:T(8,128)S(1)}, f32[2,256,256]{2,1,0:T(8,128)}, u32[]{:S(2)}) copy-start(f32[2,256,256]{2,1,0:T(8,128)} %param.9) | copy-start | bytes 1572868
  17.6 4.6 %copy-start.4 = (f32[1,1,256,256]{3,2,0,1:T(8,128)}, f32[1,1,256,256]{3,2,0,1:T(8,128)S(1)}, u32[]{:S(2)}) copy-start(f32[1,1,256,256]{3,2,0,1:T(8,128)S(1)} %get-tuple-element.69) | copy-start | bytes 786436
  18.4 12.2 %collective-permute-start = (f32[2,128,256]{2,1,0:T(8,128)}, f32[2,128,256]{2,1,0:T(8,128)}, u32[]{:S(2)}, u32[]{:S(2)}) collective-permute-start(f32[2,128,256]{2,1,0:T(8,128)} %fusion.39), channel_id=1, source_target_pairs={{0,4},{4,8},{8,12},{12,0},{1,5},{5,9},{9,13},{13,1},{2,6},{6,10},{... | collective-permute-start | bytes 786440 | tf_op jit(solution)/shard_map/ppermute | solution.py:95
  19.7 22.1 %collective-permute-start.1 = (f32[2,128,256]{2,1,0:T(8,128)}, f32[2,128,256]{2,1,0:T(8,128)}, u32[]{:S(2)}, u32[]{:S(2)}) collective-permute-start(f32[2,128,256]{2,1,0:T(8,128)} %fusion.39), channel_id=1, source_target_pairs={{0,8},{4,12},{8,0},{12,4},{1,9},{5,13},{9,1},{13,5},{2,10},{6,14},... | collective-permute-start | bytes 786440 | tf_op jit(solution)/shard_map/ppermute | solution.py:95
  20.7 24.0 %collective-permute-start.2 = (f32[2,128,256]{2,1,0:T(8,128)}, f32[2,128,256]{2,1,0:T(8,128)}, u32[]{:S(2)}, u32[]{:S(2)}) collective-permute-start(f32[2,128,256]{2,1,0:T(8,128)} %fusion.39), channel_id=1, source_target_pairs={{0,12},{4,0},{8,4},{12,8},{1,13},{5,1},{9,5},{13,9},{2,14},{6,2},{... | collective-permute-start | bytes 786440 | tf_op jit(solution)/shard_map/ppermute | solution.py:95
  22.2 1.7 %copy-start = (f32[4,2,256,256]{3,2,1,0:T(8,128)S(1)}, f32[4,2,256,256]{3,2,1,0:T(8,128)}, u32[]{:S(2)}) copy-start(f32[4,2,256,256]{3,2,1,0:T(8,128)} %param.10) | copy-start | bytes 6291460
  30.6 16.9 %copy-start.2 = (f32[4,1,256,256]{2,3,0,1:T(8,128)S(1)}, f32[4,1,256,256]{2,3,0,1:T(8,128)}, u32[]{:S(2)}) copy-start(f32[4,1,256,256]{2,3,0,1:T(8,128)} %copy.117) | copy-start | bytes 3145732
  30.6 16.9 %copy-start.3 = (f32[4,256,256]{1,2,0:T(8,128)S(1)}, f32[4,256,256]{1,2,0:T(8,128)}, u32[]{:S(2)}) copy-start(f32[4,256,256]{1,2,0:T(8,128)} %copy.95) | copy-start | bytes 3145732
  45.8 2.5 %collective-permute-start.3 = (f32[3,2,128,256]{3,2,1,0:T(8,128)S(1)}, f32[3,2,128,256]{3,2,1,0:T(8,128)S(1)}, u32[]{:S(2)}, u32[]{:S(2)}) collective-permute-start(f32[3,2,128,256]{3,2,1,0:T(8,128)S(1)} %pad_maximum_fusion.7), channel_id=1, source_target_pairs={{0,1},{1,0},{2,3},{3,2},{4,5},{5,4},{6,7},{7,6},{8,9},{9,8},{10,11... | collective-permute-start | bytes 2359304 | tf_op jit(solution)/shard_map/ppermute | solution.py:98
  55.2 1.0 %copy-start.1 = (f32[2,256,256]{2,1,0:T(8,128)S(1)}, f32[2,256,256]{2,1,0:T(8,128)}, u32[]{:S(2)}) copy-start(f32[2,256,256]{2,1,0:T(8,128)} %param.11) | copy-start | bytes 1572868

commit v4 on v3

--- a/solution.py
+++ b/solution.py
@@ -42,9 +42,12 @@
 
 
 def cmul_adjoint_left(a, b):
-    ar, ai = a[..., 0, :, :], a[..., 1, :, :]
-    br, bi = b[..., 0, :, :], b[..., 1, :, :]
-    return jnp.stack([mm_tn(ar, br) + mm_tn(ai, bi), mm_tn(ar, bi) - mm_tn(ai, br)], -3)
+    size = a.shape[-2]
+    stacked = a.reshape(a.shape[:-3] + (2 * size, a.shape[-1]))
+    real = mm_tn(stacked, b.reshape(b.shape[:-3] + (2 * size, b.shape[-1])))
+    swapped = jnp.stack([b[..., 1, :, :], -b[..., 0, :, :]], -3)
+    imag = mm_tn(stacked, swapped.reshape(b.shape[:-3] + (2 * size, b.shape[-1])))
+    return jnp.stack([real, imag], -3)
 
 
 def taylor_propagators(ham):

time: 73.6 us -> 72.1 us (0.980)
  local copies, waits for them, and re-layouts: 13.1 us -> 12.2 us
    unnamed x17, local copies, waits for them, and re-layouts: 6.15 us -> 5.27 us
    dot_general x4 -> x2, matrix products: 2.38 us -> 2.27 us  [mm_tn(): return jnp.einsum('...ji,...jk->...ik', left, right, precision=fast_mode)]
where the time goes in v4:
time: 72.1 us; the launch traced here: 71.7 us
  matrix products  24.6 us (34%)
  other arithmetic  14.7 us (20%)
  waiting for transfers between devices  14.6 us (20%)
  local copies, waits for them, and re-layouts  12.2 us (17%)
  starting transfers between devices  4.33 us (6%)
  between operations  1.28 us (2%)
    dot_general x18, matrix products, mm(): return jnp.matmul(left, right, precision=mode)  20.1 us
    ppermute x3, waiting for transfers between devices, shards(): received.append(lax.ppermute(mine, 'tm', pairs))  14.1 us
    unnamed x17, local copies, waits for them, and re-layouts  5.27 us
    ppermute x3, starting transfers between devices, shards(): received.append(lax.ppermute(mine, 'tm', pairs))  3.77 us
    squeeze x1, local copies, waits for them, and re-layouts, shards(): controls[:, 1] - jnp.swapaxes(controls[:, 1], 1, 2)  2.55 us
    dot_general x2, matrix products, mm_tn(): return jnp.einsum('...ji,...jk->...ik', left, right, precision=fast_mode)  2.27 us
    dot_general x2, matrix products, mm_nt(): return jnp.einsum('...ij,...kj->...ik', left, right, precision=fast_mode)  2.2 us
    reduce_sum x1, other arithmetic, shards(): jnp.sum(amplitudes[:, :, None, None, None] * controls[:, None], axis=0)  2.1 us
  transfers between devices with their start and end apart: 4, of which 3 were waited for; matrix products, arithmetic and copies ran while one was open for 13% of the time, Pallas kernels for 0%

profile of v4, /device:TPU:13, one launch (start us, length us, event | category | flops | bytes accessed | tf_op | source)
XLA Modules:
  0.0 71.7 jit_solution(6405826113819585327)
XLA Ops:
  0.6 0.8 %copy.55 = f32[4,2]{1,0:T(4,128)S(1)} copy(f32[4,2]{0,1:T(2,128)} %param.8) | data formatting | bytes 64 | tf_op args[0]
  1.4 2.1 %multiply_reduce_fusion = f32[2,2,256,256]{3,2,1,0:T(8,128)S(1)} fusion(f32[4,2,256,256]{3,2,1,0:T(8,128)} %param.10, f32[4,2]{1,0:T(4,128)S(1)} %copy.55), kind=kLoop, calls=%fused_computation | loop fusion | flops 1835008 | bytes 3145760 | tf_op jit(solution)/shard_map/reduce_sum | solution.py:80
  5.2 1.1 %fusion.54 = f32[2,512,256]{2,1,0:T(8,128)S(1)} fusion(f32[2,512,256]{2,1,0:T(8,128)S(1)} %bitcast.224, f32[2,256,256]{2,1,0:T(8,128)S(1)} %copy.57, f32[2,2,256,256]{2,3,0,1:T(8,128)S(1)} %broadcast_add_fusion), kind=kOutput, calls=%fused_computation.137 | convolution fusion | flops 805568512 | bytes 3145728 | tf_op jit(solution)/shard_map/dot_general | solution.py:13
  6.4 1.1 %fusion.38 = f32[2,512,256]{2,1,0:T(8,128)S(1)} fusion(f32[2,512,256]{2,1,0:T(8,128)S(1)} %bitcast.225, f32[2,256,256]{2,1,0:T(8,128)S(1)} %copy.59), kind=kOutput, calls=%fused_computation.105 | convolution fusion | flops 805568512 | bytes 2621440 | tf_op jit(solution)/shard_map/dot_general | solution.py:13
  7.8 2.0 %fusion.7 = f32[2,2,512,256]{3,2,1,0:T(8,128)S(1)} fusion(f32[1,2,2,256,256]{4,3,1,2,0:T(8,128)S(1)} %get-tuple-element.72, f32[1,2,512,256]{3,2,0,1:T(8,128)S(1)} %bitcast.238, f32[1,2,512,256]{3,2,0,1:T(8,128)S(1)} %bitcast.226), kind=kOutput, calls=%fused_computation.17 | convolution fusion | flops 1611137024 | bytes 4718592 | tf_op jit(solution)/shard_map/dot_general | solution.py:13
  9.8 2.0 %fusion.10 = f32[2,2,512,256]{3,2,1,0:T(8,128)S(1)} fusion(f32[1,2,2,256,256]{4,3,1,2,0:T(8,128)S(1)} %get-tuple-element.72, f32[1,2,512,256]{3,2,0,1:T(8,128)S(1)} %bitcast.239, f32[1,2,512,256]{3,2,0,1:T(8,128)S(1)} %bitcast.227), kind=kOutput, calls=%fused_computation.18 | convolution fusion | flops 1611137024 | bytes 4718592 | tf_op jit(solution)/shard_map/dot_general | solution.py:13
  12.2 0.4 bitcast_add_fusion.1
  12.7 1.1 %fusion.27 = f32[2,512,256]{2,1,0:T(8,128)S(1)} fusion(f32[2,512,256]{2,1,0:T(8,128)S(1)} %bitcast.236, f32[2,2,256,256]{3,2,0,1:T(8,128)S(1)} %get-tuple-element.36), kind=kOutput, calls=%fused_computation.81 | convolution fusion | flops 805306368 | bytes 2621440 | tf_op jit(solution)/shard_map/dot_general | solution.py:13
  13.8 1.1 %fusion.29 = f32[2,512,256]{2,1,0:T(8,128)S(1)} fusion(f32[2,512,256]{2,1,0:T(8,128)S(1)} %bitcast.237, f32[2,2,256,256]{3,2,0,1:T(8,128)S(1)} %get-tuple-element.36, f32[256,256]{1,0:T(8,128)S(1)} %fusion.51), kind=kOutput, calls=%fused_computation.84 | convolution fusion | flops 805437440 | bytes 2883584 | tf_op jit(solution)/shard_map/dot_general | solution.py:13
  15.3 0.9 %fusion.76 = (f32[1,2,256,256]{3,2,0,1:T(8,128)}, f32[1,2,256,256]{3,2,0,1:T(8,128)S(1)}) fusion(f32[2,2,256,256]{3,2,0,1:T(8,128)S(1)} %maximum_add_fusion), kind=kLoop, calls=%fused_computation.167 | loop fusion | bytes 2097152 | tf_op jit(solution)/shard_map/slice | solution.py:86
  16.1 0.8 %convolution_bitcast_fusion.1 = f32[1,512,256]{2,1,0:T(8,128)S(1)} fusion(f32[512,256]{1,0:T(8,128)S(1)} %bitcast.245, f32[2,2,256,256]{3,2,0,1:T(8,128)S(1)} %maximum_add_fusion), kind=kOutput, calls=%fused_computation.21 | convolution fusion | flops 402653184 | bytes 1310720 | tf_op jit(solution)/shard_map/dot_general | solution.py:13
  16.9 0.6 convolution_bitcast_fusion
  17.6 0.8 %fusion.41 = f32[2,128,256]{2,1,0:T(8,128)} fusion(s32[]{:T(128)S(6)} %select_n.58, f32[1,1,256,256]{3,2,0,1:T(8,128)S(1)} %get-tuple-element.70, f32[1,1,256,256]{3,2,0,1:T(8,128)S(1)} %get-tuple-element.71), kind=kLoop, calls=%fused_computation.108 | loop fusion | flops 65536 | bytes 786436 | tf_op jit(solution)/shard_map/dynamic_slice | solution.py:93
  18.4 1.3 %collective-permute-start = (f32[2,128,256]{2,1,0:T(8,128)}, f32[2,128,256]{2,1,0:T(8,128)}, u32[]{:S(2)}, u32[]{:S(2)}) collective-permute-start(f32[2,128,256]{2,1,0:T(8,128)} %fusion.41), channel_id=1, source_target_pairs={{0,4},{4,8},{8,12},{12,0},{1,5},{5,9},{9,13},{13,1},{2,6},{6,10},{... | collective-permute-start | bytes 786440 | tf_op jit(solution)/shard_map/ppermute | solution.py:98
  19.7 1.0 %collective-permute-start.1 = (f32[2,128,256]{2,1,0:T(8,128)}, f32[2,128,256]{2,1,0:T(8,128)}, u32[]{:S(2)}, u32[]{:S(2)}) collective-permute-start(f32[2,128,256]{2,1,0:T(8,128)} %fusion.41), channel_id=1, source_target_pairs={{0,8},{4,12},{8,0},{12,4},{1,9},{5,13},{9,1},{13,5},{2,10},{6,14},... | collective-permute-start | bytes 786440 | tf_op jit(solution)/shard_map/ppermute | solution.py:98
  20.7 1.5 %collective-permute-start.2 = (f32[2,128,256]{2,1,0:T(8,128)}, f32[2,128,256]{2,1,0:T(8,128)}, u32[]{:S(2)}, u32[]{:S(2)}) collective-permute-start(f32[2,128,256]{2,1,0:T(8,128)} %fusion.41), channel_id=1, source_target_pairs={{0,12},{4,0},{8,4},{12,8},{1,13},{5,1},{9,5},{13,9},{2,14},{6,2},{... | collective-permute-start | bytes 786440 | tf_op jit(solution)/shard_map/ppermute | solution.py:98
  22.2 1.3 %maximum_maximum_fusion = f32[2,2,256,256]{3,2,0,1:T(8,128)S(1)} fusion(f32[1,1,256,256]{3,2,0,1:T(8,128)S(1)} %get-tuple-element.71, f32[1,1,256,256]{3,2,0,1:T(8,128)S(1)} %get-tuple-element.70, f32[1,2,256,256]{3,2,0,1:T(8,128)} %get-tuple-element.68), kind=kLoop, calls=%fused_computation.36 | loop fusion | flops 524288 | bytes 2097152 | tf_op jit(solution)/shard_map/stack | solution.py:149
  23.5 0.4 copy-done
  23.9 1.5 %fusion.73 = (f32[4,1,256,256]{3,2,1,0:T(8,128)}, f32[4,256,256]{2,1,0:T(8,128)}) fusion(f32[4,2,256,256]{3,2,1,0:T(8,128)S(1)} %copy-done), kind=kLoop, calls=%fused_computation.164 | loop fusion | bytes 4194304 | tf_op jit(solution)/shard_map/slice | solution.py:155
  25.4 2.6 %copy.80 = f32[4,256,256]{1,2,0:T(8,128)} copy(f32[4,256,256]{2,1,0:T(8,128)} %get-tuple-element.44) | data formatting | bytes 2097152 | tf_op jit(solution)/shard_map/squeeze | solution.py:156
  28.0 2.5 %copy.97 = f32[4,1,256,256]{2,3,0,1:T(8,128)} copy(f32[4,1,256,256]{3,2,1,0:T(8,128)} %get-tuple-element.43) | data formatting | bytes 2097152
  30.6 11.2 %collective-permute-done.1 = f32[2,128,256]{2,1,0:T(8,128)} collective-permute-done((f32[2,128,256]{2,1,0:T(8,128)}, f32[2,128,256]{2,1,0:T(8,128)}, u32[]{:S(2)}, u32[]{:S(2)}) %collective-permute-start.1) | collective-permute-done | bytes 262176 | tf_op jit(solution)/shard_map/ppermute | solution.py:98
  41.8 2.9 %collective-permute-done.2 = f32[2,128,256]{2,1,0:T(8,128)} collective-permute-done((f32[2,128,256]{2,1,0:T(8,128)}, f32[2,128,256]{2,1,0:T(8,128)}, u32[]{:S(2)}, u32[]{:S(2)}) %collective-permute-start.2) | collective-permute-done | bytes 262176 | tf_op jit(solution)/shard_map/ppermute | solution.py:98
  44.7 1.2 %pad_maximum_fusion.7 = f32[3,2,128,256]{3,2,1,0:T(8,128)S(1)} fusion(f32[1,2,128,256]{3,2,1,0:T(8,128)} %bitcast.42, f32[1,2,128,256]{3,2,1,0:T(8,128)} %bitcast.41, f32[1,2,128,256]{3,2,1,0:T(8,128)} %bitcast.40), kind=kLoop, calls=%fused_computation.49 | loop fusion | flops 393216 | bytes 1572864 | tf_op jit(solution)/shard_map/stack | solution.py:99
  45.9 0.6 collective-permute-start.3
  46.4 1.0 %fusion.18 = f32[2,256,256]{2,1,0:T(8,128)S(1)} fusion(f32[1,1,256,256]{3,2,0,1:T(8,128)} %copy-done.4, f32[1,1,256,256]{3,2,0,1:T(8,128)S(1)} %get-tuple-element.70), kind=kLoop, calls=%fused_computation.53 | loop fusion | flops 131072 | bytes 1048576 | tf_op jit(solution)/shard_map/jit(_where)/broadcast_in_dim | solution.py:109
  47.8 0.5 collective-permute-done.3
  48.3 1.6 %maximum_select_fusion = f32[3,2,256,256]{3,2,1,0:T(8,128)S(1)} fusion(f32[3,2,128,256]{3,2,1,0:T(8,128)S(1)} %collective-permute-done.3, f32[1,2,128,256]{3,2,1,0:T(8,128)} %bitcast.42, f32[1,2,128,256]{3,2,1,0:T(8,128)} %bitcast.41, f32[1,2,128,256]{3,2,1,0:T(8,128)} %bitcast.40, pred[]{:T(512)S(6)} %eq.69), kind=kLoop, calls=%fused_computation.19 | loop fusion | flops 2752512 | bytes 3145729 | tf_op jit(solution)/shard_map/jit(_where)/select_n | solution.py:103
  50.0 0.3 select_select_fusion
  50.6 1.1 %fusion.24 = f32[2,512,256]{2,1,0:T(8,128)S(1)} fusion(f32[2,512,256]{2,1,0:T(8,128)S(1)} %bitcast.232, f32[2,2,256,256]{3,2,0,1:T(8,128)S(1)} %get-tuple-element.57), kind=kOutput, calls=%fused_computation.72 | convolution fusion | flops 805306368 | bytes 2621440 | tf_op jit(solution)/shard_map/dot_general | solution.py:13
  51.7 1.1 %fusion.23 = f32[2,512,256]{2,1,0:T(8,128)S(1)} fusion(f32[2,512,256]{2,1,0:T(8,128)S(1)} %bitcast.233, f32[2,2,256,256]{3,2,0,1:T(8,128)S(1)} %get-tuple-element.57), kind=kOutput, calls=%fused_computation.70 | convolution fusion | flops 805306368 | bytes 2621440 | tf_op jit(solution)/shard_map/dot_general | solution.py:13
  53.3 1.0 %fusion.46 = f32[2,512,256]{2,1,0:T(8,128)S(1)} fusion(f32[2,512,256]{2,1,0:T(8,128)S(1)} %bitcast.234, f32[2,256,256]{2,1,0:T(8,128)S(1)} %get-tuple-element.56), kind=kOutput, calls=%fused_computation.118 | convolution fusion | flops 805306368 | bytes 2359296 | tf_op jit(solution)/shard_map/dot_general | solution.py:13
  54.3 1.0 %fusion.47 = f32[2,512,256]{2,1,0:T(8,128)S(1)} fusion(f32[2,512,256]{2,1,0:T(8,128)S(1)} %bitcast.235, f32[2,256,256]{2,1,0:T(8,128)S(1)} %get-tuple-element.55), kind=kOutput, calls=%fused_computation.120 | convolution fusion | flops 805306368 | bytes 2359296 | tf_op jit(solution)/shard_map/dot_general | solution.py:13
  55.7 1.0 %fusion.45 = f32[2,512,256]{2,1,0:T(8,128)S(1)} fusion(f32[2,512,256]{2,1,0:T(8,128)S(1)} %bitcast.220, f32[4,2,256,256]{3,2,0,1:T(8,128)S(1)} %fusion.1, s32[]{:T(128)S(6)} %select_n.66), kind=kOutput, calls=%fused_computation.116 | convolution fusion | flops 805306368 | bytes 2359300 | tf_op jit(solution)/shard_map/dot_general | solution.py:13
  56.7 1.2 %fusion.64 = f32[2,512,64]{1,2,0:T(8,128)S(1)} fusion(f32[2,512,256]{2,1,0:T(8,128)S(1)} %bitcast.221, f32[4,2,256,256]{3,2,0,1:T(8,128)S(1)} %fusion.1, s32[]{:T(128)S(6)} %select_n.67, s32[]{:T(128)S(6)} %select_n.69), kind=kOutput, calls=%fused_computation.150 | convolution fusion | flops 201326592 | bytes 1441800 | tf_op jit(solution)/shard_map/dot_general | solution.py:13
  57.8 1.2 %fusion.63 = f32[2,512,64]{1,2,0:T(8,128)S(1)} fusion(f32[2,512,256]{2,1,0:T(8,128)S(1)} %bitcast.222, f32[4,2,256,256]{3,2,0,1:T(8,128)S(1)} %fusion.1, s32[]{:T(128)S(6)} %select_n.67, s32[]{:T(128)S(6)} %add.144, s32[]{:T(128)S(6)} %select_n.69), kind=kOutput, calls=%fused_computation.148 | convolution fusion | flops 201326592 | bytes 1441804 | tf_op jit(solution)/shard_map/dot_general | solution.py:13
  59.0 1.0 %fusion.44 = f32[2,512,256]{2,1,0:T(8,128)S(1)} fusion(f32[2,512,256]{2,1,0:T(8,128)S(1)} %bitcast.223, f32[4,2,256,256]{3,2,0,1:T(8,128)S(1)} %fusion.1, s32[]{:T(128)S(6)} %select_n.66, s32[]{:T(128)S(6)} %add.144), kind=kOutput, calls=%fused_computation.114 | convolution fusion | flops 805306368 | bytes 2359304 | tf_op jit(solution)/shard_map/dot_general | solution.py:13
  60.0 0.7 add_reduce_fusion.1
  61.1 1.2 %convolution_bitcast_fusion.2 = f32[1,256,256]{1,2,0:T(8,128)S(1)} fusion(f32[2,256,256]{2,1,0:T(8,128)S(1)} %copy-done.1, f32[1,256,256]{2,1,0:T(8,128)S(1)} %get-tuple-element.79, f32[1,256,256]{2,1,0:T(8,128)S(1)} %get-tuple-element.78), kind=kOutput, calls=%fused_computation.22 | convolution fusion | flops 402784256 | bytes 1310720 | tf_op jit(solution)/shard_map/...ji,...jk->...ik/dot_general | solution.py:21
  62.3 1.0 %convolution_bitcast_fusion.3 = f32[1,256,256]{1,2,0:T(8,128)S(1)} fusion(f32[512,256]{1,0:T(8,128)S(1)} %bitcast.249, f32[512,256]{1,0:T(8,128)S(1)} %bitcast.244), kind=kOutput, calls=%fused_computation.23 | convolution fusion | flops 402653184 | bytes 1310720 | tf_op jit(solution)/shard_map/...ji,...jk->...ik/dot_general | solution.py:21
  63.4 1.0 %fusion.43 = f32[2,512,256]{2,1,0:T(8,128)S(1)} fusion(f32[2,512,256]{2,1,0:T(8,128)S(1)} %bitcast.230, f32[1,2,256,256]{2,3,1,0:T(8,128)S(1)} %maximum_bitcast_fusion), kind=kOutput, calls=%fused_computation.112 | convolution fusion | flops 805306368 | bytes 2359296 | tf_op jit(solution)/shard_map/dot_general | solution.py:13
  64.4 1.0 %fusion.42 = f32[2,512,256]{2,1,0:T(8,128)S(1)} fusion(f32[2,512,256]{2,1,0:T(8,128)S(1)} %bitcast.231, f32[1,2,256,256]{2,3,1,0:T(8,128)S(1)} %maximum_bitcast_fusion), kind=kOutput, calls=%fused_computation.110 | convolution fusion | flops 805306368 | bytes 2359296 | tf_op jit(solution)/shard_map/dot_general | solution.py:13
  65.8 1.1 %fusion.57 = f32[2,512,256]{2,1,0:T(8,128)S(1)} fusion(f32[2,512,256]{2,1,0:T(8,128)S(1)} %bitcast.228, f32[2,512,256]{2,1,0:T(8,128)S(1)} %fusion.44, f32[2,512,256]{2,1,0:T(8,128)S(1)} %fusion.45), kind=kOutput, calls=%fused_computation.139 | convolution fusion | flops 805437440 | bytes 3145728 | tf_op jit(solution)/shard_map/...ij,...kj->...ik/dot_general | solution.py:17
  66.9 1.1 %fusion.59 = f32[2,512,256]{2,1,0:T(8,128)S(1)} fusion(f32[2,512,256]{2,1,0:T(8,128)S(1)} %bitcast.229, f32[2,512,256]{2,1,0:T(8,128)S(1)} %fusion.45, f32[2,512,256]{2,1,0:T(8,128)S(1)} %fusion.44), kind=kOutput, calls=%fused_computation.141 | convolution fusion | flops 805437440 | bytes 3145728 | tf_op jit(solution)/shard_map/...ij,...kj->...ik/dot_general | solution.py:17
  68.0 0.7 %copy.84 = f32[2,2,256,64]{2,3,1,0:T(8,128)} copy(f32[2,2,256,64]{2,3,0,1:T(8,128)S(1)} %pad_maximum_fusion.10) | data formatting | bytes 524288
  68.9 0.9 %subtract_reduce_fusion = (f32[4,2]{1,0:T(4,128)S(1)}, f32[4,2]{1,0:T(4,128)S(1)}) fusion(f32[2,256,256]{2,1,0:T(8,128)S(1)} %get-tuple-element.46, f32[4,256,256]{2,1,0:T(8,128)S(1)} %get-tuple-element.42, f32[2,256,256]{2,1,0:T(8,128)S(1)} %get-tuple-element.45, f32[4,256,256]{2,1,0:T(8,128)S(1)} %get-tuple-element.41), kind=kLoop, calls=%fused_computation.10 | loop fusion | flops 4194288 | bytes 3145792 | tf_op jit(solution)/shard_map/reduce_sum | solution.py:158
  69.8 1.2 %multiply_subtract_fusion = f32[4,2]{1,0:T(4,128)S(1)} fusion(f32[4,2]{1,0:T(4,128)S(1)} %get-tuple-element.33, f32[4,2]{1,0:T(4,128)S(1)} %get-tuple-element.32, f32[]{:T(128)} %get-tuple-element.35, f32[]{:T(128)} %get-tuple-element.34), kind=kLoop, calls=%fused_computation.151 | loop fusion | flops 24 | bytes 104 | tf_op jit(solution)/shard_map/sub | solution.py:159
  71.1 0.6 copy.83
  (61 shorter events, 5.3 us)
Async XLA Ops:
  1.4 2.4 %copy-start.5 = (f32[2,256,256]{2,1,0:T(8,128)S(1)}, f32[2,256,256]{2,1,0:T(8,128)}, u32[]{:S(2)}) copy-start(f32[2,256,256]{2,1,0:T(8,128)} %param.9) | copy-start | bytes 1572868
  17.6 4.6 %copy-start.4 = (f32[1,1,256,256]{3,2,0,1:T(8,128)}, f32[1,1,256,256]{3,2,0,1:T(8,128)S(1)}, u32[]{:S(2)}) copy-start(f32[1,1,256,256]{3,2,0,1:T(8,128)S(1)} %get-tuple-element.71) | copy-start | bytes 786436
  18.4 12.2 %collective-permute-start = (f32[2,128,256]{2,1,0:T(8,128)}, f32[2,128,256]{2,1,0:T(8,128)}, u32[]{:S(2)}, u32[]{:S(2)}) collective-permute-start(f32[2,128,256]{2,1,0:T(8,128)} %fusion.41), channel_id=1, source_target_pairs={{0,4},{4,8},{8,12},{12,0},{1,5},{5,9},{9,13},{13,1},{2,6},{6,10},{... | collective-permute-start | bytes 786440 | tf_op jit(solution)/shard_map/ppermute | solution.py:98
  19.7 22.1 %collective-permute-start.1 = (f32[2,128,256]{2,1,0:T(8,128)}, f32[2,128,256]{2,1,0:T(8,128)}, u32[]{:S(2)}, u32[]{:S(2)}) collective-permute-start(f32[2,128,256]{2,1,0:T(8,128)} %fusion.41), channel_id=1, source_target_pairs={{0,8},{4,12},{8,0},{12,4},{1,9},{5,13},{9,1},{13,5},{2,10},{6,14},... | collective-permute-start | bytes 786440 | tf_op jit(solution)/shard_map/ppermute | solution.py:98
  20.7 24.0 %collective-permute-start.2 = (f32[2,128,256]{2,1,0:T(8,128)}, f32[2,128,256]{2,1,0:T(8,128)}, u32[]{:S(2)}, u32[]{:S(2)}) collective-permute-start(f32[2,128,256]{2,1,0:T(8,128)} %fusion.41), channel_id=1, source_target_pairs={{0,12},{4,0},{8,4},{12,8},{1,13},{5,1},{9,5},{13,9},{2,14},{6,2},{... | collective-permute-start | bytes 786440 | tf_op jit(solution)/shard_map/ppermute | solution.py:98
  22.2 1.7 %copy-start = (f32[4,2,256,256]{3,2,1,0:T(8,128)S(1)}, f32[4,2,256,256]{3,2,1,0:T(8,128)}, u32[]{:S(2)}) copy-start(f32[4,2,256,256]{3,2,1,0:T(8,128)} %param.10) | copy-start | bytes 6291460
  30.5 16.9 %copy-start.2 = (f32[4,256,256]{1,2,0:T(8,128)S(1)}, f32[4,256,256]{1,2,0:T(8,128)}, u32[]{:S(2)}) copy-start(f32[4,256,256]{1,2,0:T(8,128)} %copy.80) | copy-start | bytes 3145732
  30.5 17.0 %copy-start.3 = (f32[4,1,256,256]{2,3,0,1:T(8,128)S(1)}, f32[4,1,256,256]{2,3,0,1:T(8,128)}, u32[]{:S(2)}) copy-start(f32[4,1,256,256]{2,3,0,1:T(8,128)} %copy.97) | copy-start | bytes 3145732
  45.9 2.5 %collective-permute-start.3 = (f32[3,2,128,256]{3,2,1,0:T(8,128)S(1)}, f32[3,2,128,256]{3,2,1,0:T(8,128)S(1)}, u32[]{:S(2)}, u32[]{:S(2)}) collective-permute-start(f32[3,2,128,256]{3,2,1,0:T(8,128)S(1)} %pad_maximum_fusion.7), channel_id=1, source_target_pairs={{0,1},{1,0},{2,3},{3,2},{4,5},{5,4},{6,7},{7,6},{8,9},{9,8},{10,11... | collective-permute-start | bytes 2359304 | tf_op jit(solution)/shard_map/ppermute | solution.py:101
  57.8 2.2 %copy-start.1 = (f32[2,256,256]{2,1,0:T(8,128)S(1)}, f32[2,256,256]{2,1,0:T(8,128)}, u32[]{:S(2)}) copy-start(f32[2,256,256]{2,1,0:T(8,128)} %param.11) | copy-start | bytes 1572868

commit v5 on v4

--- a/solution.py
+++ b/solution.py
@@ -100,9 +100,9 @@
         if split == 2:
             theirs = lax.ppermute(received, "col", [(i, i ^ 1) for i in range(col_count)])
             own_block = block_total
-            received = jnp.where(
-                part == 0, jnp.concatenate([received, theirs], 2), jnp.concatenate([theirs, received], 2)
-            )
+            joined = jnp.zeros(received.shape[:2] + (size,) + received.shape[3:], received.dtype)
+            joined = lax.dynamic_update_slice_in_dim(joined, received, part * rows, 2)
+            received = lax.dynamic_update_slice_in_dim(joined, theirs, (1 - part) * rows, 2)
         else:
             own_block = block_total
         slots = jnp.arange(tm_count)[:, None, None, None]

time: 72.1 us -> 71.1 us (0.986)
  other arithmetic: 14.7 us -> 12.4 us
  waiting for transfers between devices: 14.6 us -> 15.6 us
    select_n x1 -> x0, other arithmetic: 1.58 us -> none  [shards(): jnp.where(part == 0, jnp.concatenate([received, theirs], 2), jnp.concaten...]
    broadcast_in_dim x1, other arithmetic: 0.99 us -> 0.04 us  [shards(): jnp.where(slots == tm_index, own_block[None], jnp.zeros_like(own_block)[N...]
    ppermute x1, waiting for transfers between devices: 0.54 us -> 1.48 us  [shards(): lax.ppermute(received, 'col', [(i, i ^ 1) for i in range(col_count)])]
    unnamed x17 -> x19, local copies, waits for them, and re-layouts: 5.27 us -> 5.26 us
  transfers between devices with their start and end apart: 4 -> 4, of which waited for: 3 -> 3; matrix products, arithmetic and copies ran while one was open for 13% -> 12% of each run, Pallas kernels for 0% -> 0%
where the time goes in v5:
time: 71.1 us; the launch traced here: 70.7 us
  matrix products  24.6 us (35%)
  waiting for transfers between devices  15.6 us (22%)
  local copies, waits for them, and re-layouts  12.5 us (18%)
  other arithmetic  12.4 us (17%)
  starting transfers between devices  4.33 us (6%)
  between operations  1.31 us (2%)
    dot_general x18, matrix products, mm(): return jnp.matmul(left, right, precision=mode)  20.1 us
    ppermute x3, waiting for transfers between devices, shards(): received.append(lax.ppermute(mine, 'tm', pairs))  14.1 us
    unnamed x19, local copies, waits for them, and re-layouts  5.26 us
    ppermute x3, starting transfers between devices, shards(): received.append(lax.ppermute(mine, 'tm', pairs))  3.77 us
    squeeze x1, local copies, waits for them, and re-layouts, shards(): controls[:, 1] - jnp.swapaxes(controls[:, 1], 1, 2)  2.56 us
    dot_general x2, matrix products, mm_tn(): return jnp.einsum('...ji,...jk->...ik', left, right, precision=fast_mode)  2.27 us
    dot_general x2, matrix products, mm_nt(): return jnp.einsum('...ij,...kj->...ik', left, right, precision=fast_mode)  2.2 us
    reduce_sum x1, other arithmetic, shards(): jnp.sum(amplitudes[:, :, None, None, None] * controls[:, None], axis=0)  2.1 us
  transfers between devices with their start and end apart: 4, of which 3 were waited for; matrix products, arithmetic and copies ran while one was open for 12% of the time, Pallas kernels for 0%

profile of v5, /device:TPU:13, one launch (start us, length us, event | category | flops | bytes accessed | tf_op | source)
XLA Modules:
  0.0 70.7 jit_solution(14254296591417355645)
XLA Ops:
  0.6 0.8 %copy.55 = f32[4,2]{1,0:T(4,128)S(1)} copy(f32[4,2]{0,1:T(2,128)} %param.8) | data formatting | bytes 64 | tf_op args[0]
  1.4 2.1 %multiply_reduce_fusion = f32[2,2,256,256]{3,2,1,0:T(8,128)S(1)} fusion(f32[4,2,256,256]{3,2,1,0:T(8,128)} %param.10, f32[4,2]{1,0:T(4,128)S(1)} %copy.55), kind=kLoop, calls=%fused_computation | loop fusion | flops 1835008 | bytes 3145760 | tf_op jit(solution)/shard_map/reduce_sum | solution.py:80
  3.5 0.3 copy.56
  5.2 1.1 %fusion.54 = f32[2,512,256]{2,1,0:T(8,128)S(1)} fusion(f32[2,512,256]{2,1,0:T(8,128)S(1)} %bitcast.224, f32[2,256,256]{2,1,0:T(8,128)S(1)} %copy.57, f32[2,2,256,256]{2,3,0,1:T(8,128)S(1)} %broadcast_add_fusion), kind=kOutput, calls=%fused_computation.136 | convolution fusion | flops 805568512 | bytes 3145728 | tf_op jit(solution)/shard_map/dot_general | solution.py:13
  6.4 1.1 %fusion.38 = f32[2,512,256]{2,1,0:T(8,128)S(1)} fusion(f32[2,512,256]{2,1,0:T(8,128)S(1)} %bitcast.225, f32[2,256,256]{2,1,0:T(8,128)S(1)} %copy.59), kind=kOutput, calls=%fused_computation.104 | convolution fusion | flops 805568512 | bytes 2621440 | tf_op jit(solution)/shard_map/dot_general | solution.py:13
  7.8 2.0 %fusion.7 = f32[2,2,512,256]{3,2,1,0:T(8,128)S(1)} fusion(f32[1,2,2,256,256]{4,3,1,2,0:T(8,128)S(1)} %get-tuple-element.72, f32[1,2,512,256]{3,2,0,1:T(8,128)S(1)} %bitcast.238, f32[1,2,512,256]{3,2,0,1:T(8,128)S(1)} %bitcast.226), kind=kOutput, calls=%fused_computation.17 | convolution fusion | flops 1611137024 | bytes 4718592 | tf_op jit(solution)/shard_map/dot_general | solution.py:13
  9.8 2.0 %fusion.10 = f32[2,2,512,256]{3,2,1,0:T(8,128)S(1)} fusion(f32[1,2,2,256,256]{4,3,1,2,0:T(8,128)S(1)} %get-tuple-element.72, f32[1,2,512,256]{3,2,0,1:T(8,128)S(1)} %bitcast.239, f32[1,2,512,256]{3,2,0,1:T(8,128)S(1)} %bitcast.227), kind=kOutput, calls=%fused_computation.18 | convolution fusion | flops 1611137024 | bytes 4718592 | tf_op jit(solution)/shard_map/dot_general | solution.py:13
  11.8 0.3 fusion.15
  12.2 0.4 bitcast_add_fusion.1
  12.7 1.1 %fusion.27 = f32[2,512,256]{2,1,0:T(8,128)S(1)} fusion(f32[2,512,256]{2,1,0:T(8,128)S(1)} %bitcast.236, f32[2,2,256,256]{3,2,0,1:T(8,128)S(1)} %get-tuple-element.36), kind=kOutput, calls=%fused_computation.80 | convolution fusion | flops 805306368 | bytes 2621440 | tf_op jit(solution)/shard_map/dot_general | solution.py:13
  13.8 1.1 %fusion.29 = f32[2,512,256]{2,1,0:T(8,128)S(1)} fusion(f32[2,512,256]{2,1,0:T(8,128)S(1)} %bitcast.237, f32[2,2,256,256]{3,2,0,1:T(8,128)S(1)} %get-tuple-element.36, f32[256,256]{1,0:T(8,128)S(1)} %fusion.51), kind=kOutput, calls=%fused_computation.83 | convolution fusion | flops 805437440 | bytes 2883584 | tf_op jit(solution)/shard_map/dot_general | solution.py:13
  15.3 0.9 %fusion.76 = (f32[1,2,256,256]{3,2,0,1:T(8,128)}, f32[1,2,256,256]{3,2,0,1:T(8,128)S(1)}) fusion(f32[2,2,256,256]{3,2,0,1:T(8,128)S(1)} %maximum_add_fusion), kind=kLoop, calls=%fused_computation.168 | loop fusion | bytes 2097152 | tf_op jit(solution)/shard_map/slice | solution.py:86
  16.2 0.8 %convolution_bitcast_fusion.1 = f32[1,512,256]{2,1,0:T(8,128)S(1)} fusion(f32[512,256]{1,0:T(8,128)S(1)} %bitcast.245, f32[2,2,256,256]{3,2,0,1:T(8,128)S(1)} %maximum_add_fusion), kind=kOutput, calls=%fused_computation.20 | convolution fusion | flops 402653184 | bytes 1310720 | tf_op jit(solution)/shard_map/dot_general | solution.py:13
  16.9 0.6 convolution_bitcast_fusion
  17.6 0.8 %fusion.41 = f32[2,128,256]{2,1,0:T(8,128)} fusion(s32[]{:T(128)S(6)} %select_n.53, f32[1,1,256,256]{3,2,0,1:T(8,128)S(1)} %get-tuple-element.70, f32[1,1,256,256]{3,2,0,1:T(8,128)S(1)} %get-tuple-element.71), kind=kLoop, calls=%fused_computation.107 | loop fusion | flops 65536 | bytes 786436 | tf_op jit(solution)/shard_map/dynamic_slice | solution.py:93
  18.4 1.3 %collective-permute-start = (f32[2,128,256]{2,1,0:T(8,128)}, f32[2,128,256]{2,1,0:T(8,128)}, u32[]{:S(2)}, u32[]{:S(2)}) collective-permute-start(f32[2,128,256]{2,1,0:T(8,128)} %fusion.41), channel_id=1, source_target_pairs={{0,4},{4,8},{8,12},{12,0},{1,5},{5,9},{9,13},{13,1},{2,6},{6,10},{... | collective-permute-start | bytes 786440 | tf_op jit(solution)/shard_map/ppermute | solution.py:98
  19.7 1.0 %collective-permute-start.1 = (f32[2,128,256]{2,1,0:T(8,128)}, f32[2,128,256]{2,1,0:T(8,128)}, u32[]{:S(2)}, u32[]{:S(2)}) collective-permute-start(f32[2,128,256]{2,1,0:T(8,128)} %fusion.41), channel_id=1, source_target_pairs={{0,8},{4,12},{8,0},{12,4},{1,9},{5,13},{9,1},{13,5},{2,10},{6,14},... | collective-permute-start | bytes 786440 | tf_op jit(solution)/shard_map/ppermute | solution.py:98
  20.7 1.5 %collective-permute-start.2 = (f32[2,128,256]{2,1,0:T(8,128)}, f32[2,128,256]{2,1,0:T(8,128)}, u32[]{:S(2)}, u32[]{:S(2)}) collective-permute-start(f32[2,128,256]{2,1,0:T(8,128)} %fusion.41), channel_id=1, source_target_pairs={{0,12},{4,0},{8,4},{12,8},{1,13},{5,1},{9,5},{13,9},{2,14},{6,2},{... | collective-permute-start | bytes 786440 | tf_op jit(solution)/shard_map/ppermute | solution.py:98
  22.2 1.3 %maximum_maximum_fusion = f32[2,2,256,256]{3,2,0,1:T(8,128)S(1)} fusion(f32[1,1,256,256]{3,2,0,1:T(8,128)S(1)} %get-tuple-element.71, f32[1,1,256,256]{3,2,0,1:T(8,128)S(1)} %get-tuple-element.70, f32[1,2,256,256]{3,2,0,1:T(8,128)} %get-tuple-element.68), kind=kLoop, calls=%fused_computation.35 | loop fusion | flops 524288 | bytes 2097152 | tf_op jit(solution)/shard_map/stack | solution.py:149
  23.5 0.4 copy-done
  23.9 1.6 %fusion.73 = (f32[4,1,256,256]{3,2,1,0:T(8,128)}, f32[4,256,256]{2,1,0:T(8,128)}) fusion(f32[4,2,256,256]{3,2,1,0:T(8,128)S(1)} %copy-done), kind=kLoop, calls=%fused_computation.165 | loop fusion | bytes 4194304 | tf_op jit(solution)/shard_map/slice | solution.py:155
  25.5 2.6 %copy.80 = f32[4,256,256]{1,2,0:T(8,128)} copy(f32[4,256,256]{2,1,0:T(8,128)} %get-tuple-element.44) | data formatting | bytes 2097152 | tf_op jit(solution)/shard_map/squeeze | solution.py:156
  28.0 2.5 %copy.97 = f32[4,1,256,256]{2,3,0,1:T(8,128)} copy(f32[4,1,256,256]{3,2,1,0:T(8,128)} %get-tuple-element.43) | data formatting | bytes 2097152
  30.6 11.2 %collective-permute-done.1 = f32[2,128,256]{2,1,0:T(8,128)} collective-permute-done((f32[2,128,256]{2,1,0:T(8,128)}, f32[2,128,256]{2,1,0:T(8,128)}, u32[]{:S(2)}, u32[]{:S(2)}) %collective-permute-start.1) | collective-permute-done | bytes 262176 | tf_op jit(solution)/shard_map/ppermute | solution.py:98
  41.8 2.8 %collective-permute-done.2 = f32[2,128,256]{2,1,0:T(8,128)} collective-permute-done((f32[2,128,256]{2,1,0:T(8,128)}, f32[2,128,256]{2,1,0:T(8,128)}, u32[]{:S(2)}, u32[]{:S(2)}) %collective-permute-start.2) | collective-permute-done | bytes 262176 | tf_op jit(solution)/shard_map/ppermute | solution.py:98
  44.8 1.4 %pad_maximum_fusion.7 = (f32[3,2,128,256]{3,2,1,0:T(8,128)S(1)}, f32[3,2,256,256]{3,2,1,0:T(8,128)S(1)}) fusion(f32[1,2,128,256]{3,2,1,0:T(8,128)} %bitcast.42, f32[1,2,128,256]{3,2,1,0:T(8,128)} %bitcast.41, f32[1,2,128,256]{3,2,1,0:T(8,128)} %bitcast.40, f32[3,2,256,256]{3,2,1,0:T(8,128)S(1)} %broadcast_in_dim.92, s32[]{:T(128)S(6)} %select_n.53), kind=kLoop, calls=%fused_computation.48 | loop fusion | flops 393216 | bytes 2359300 | tf_op jit(solution)/shard_map/stack | solution.py:99
  46.2 0.6 collective-permute-start.3
  47.2 1.5 %collective-permute-done.3 = f32[3,2,128,256]{3,2,1,0:T(8,128)S(1)} collective-permute-done((f32[3,2,128,256]{3,2,1,0:T(8,128)S(1)}, f32[3,2,128,256]{3,2,1,0:T(8,128)S(1)}, u32[]{:S(2)}, u32[]{:S(2)}) %collective-permute-start.3) | collective-permute-done | bytes 786464 | tf_op jit(solution)/shard_map/ppermute | solution.py:101
  48.9 0.3 select_select_fusion
  49.5 1.1 %fusion.24 = f32[2,512,256]{2,1,0:T(8,128)S(1)} fusion(f32[2,512,256]{2,1,0:T(8,128)S(1)} %bitcast.232, f32[2,2,256,256]{3,2,0,1:T(8,128)S(1)} %get-tuple-element.57), kind=kOutput, calls=%fused_computation.71 | convolution fusion | flops 805306368 | bytes 2621440 | tf_op jit(solution)/shard_map/dot_general | solution.py:13
  50.6 1.1 %fusion.23 = f32[2,512,256]{2,1,0:T(8,128)S(1)} fusion(f32[2,512,256]{2,1,0:T(8,128)S(1)} %bitcast.233, f32[2,2,256,256]{3,2,0,1:T(8,128)S(1)} %get-tuple-element.57), kind=kOutput, calls=%fused_computation.69 | convolution fusion | flops 805306368 | bytes 2621440 | tf_op jit(solution)/shard_map/dot_general | solution.py:13
  52.2 1.0 %fusion.46 = f32[2,512,256]{2,1,0:T(8,128)S(1)} fusion(f32[2,512,256]{2,1,0:T(8,128)S(1)} %bitcast.234, f32[2,256,256]{2,1,0:T(8,128)S(1)} %get-tuple-element.56), kind=kOutput, calls=%fused_computation.117 | convolution fusion | flops 805306368 | bytes 2359296 | tf_op jit(solution)/shard_map/dot_general | solution.py:13
  53.2 1.0 %fusion.47 = f32[2,512,256]{2,1,0:T(8,128)S(1)} fusion(f32[2,512,256]{2,1,0:T(8,128)S(1)} %bitcast.235, f32[2,256,256]{2,1,0:T(8,128)S(1)} %get-tuple-element.55), kind=kOutput, calls=%fused_computation.119 | convolution fusion | flops 805306368 | bytes 2359296 | tf_op jit(solution)/shard_map/dot_general | solution.py:13
  54.6 1.0 %fusion.45 = f32[2,512,256]{2,1,0:T(8,128)S(1)} fusion(f32[2,512,256]{2,1,0:T(8,128)S(1)} %bitcast.220, f32[4,2,256,256]{3,2,0,1:T(8,128)S(1)} %fusion.1, s32[]{:T(128)S(6)} %select_n.61), kind=kOutput, calls=%fused_computation.115 | convolution fusion | flops 805306368 | bytes 2359300 | tf_op jit(solution)/shard_map/dot_general | solution.py:13
  55.6 1.2 %fusion.64 = f32[2,512,64]{1,2,0:T(8,128)S(1)} fusion(f32[2,512,256]{2,1,0:T(8,128)S(1)} %bitcast.221, f32[4,2,256,256]{3,2,0,1:T(8,128)S(1)} %fusion.1, s32[]{:T(128)S(6)} %select_n.62, s32[]{:T(128)S(6)} %select_n.64), kind=kOutput, calls=%fused_computation.149 | convolution fusion | flops 201326592 | bytes 1441800 | tf_op jit(solution)/shard_map/dot_general | solution.py:13
  56.7 1.2 %fusion.63 = f32[2,512,64]{1,2,0:T(8,128)S(1)} fusion(f32[2,512,256]{2,1,0:T(8,128)S(1)} %bitcast.222, f32[4,2,256,256]{3,2,0,1:T(8,128)S(1)} %fusion.1, s32[]{:T(128)S(6)} %select_n.62, s32[]{:T(128)S(6)} %add.149, s32[]{:T(128)S(6)} %select_n.64), kind=kOutput, calls=%fused_computation.147 | convolution fusion | flops 201326592 | bytes 1441804 | tf_op jit(solution)/shard_map/dot_general | solution.py:13
  57.9 1.0 %fusion.44 = f32[2,512,256]{2,1,0:T(8,128)S(1)} fusion(f32[2,512,256]{2,1,0:T(8,128)S(1)} %bitcast.223, f32[4,2,256,256]{3,2,0,1:T(8,128)S(1)} %fusion.1, s32[]{:T(128)S(6)} %select_n.61, s32[]{:T(128)S(6)} %add.149), kind=kOutput, calls=%fused_computation.113 | convolution fusion | flops 805306368 | bytes 2359304 | tf_op jit(solution)/shard_map/dot_general | solution.py:13
  58.9 0.7 %add_reduce_fusion.1 = (f32[]{:T(128)}, f32[]{:T(128)}, f32[1,256,256]{2,1,0:T(8,128)S(1)}, f32[1,256,256]{2,1,0:T(8,128)S(1)}) fusion(f32[2,256,256]{2,1,0:T(8,128)S(1)} %copy-done.1, f32[2,256,256]{2,1,0:T(8,128)S(1)} %get-tuple-element.54, f32[2,256,256]{2,1,0:T(8,128)S(1)} %get-tuple-element.53), kind=kLoop, calls=%fused_computation.129 | loop fusion | flops 589822 | bytes 1572872 | tf_op jit(solution)/shard_map/reduce_sum | solution.py:152
  60.0 1.2 %convolution_bitcast_fusion.2 = f32[1,256,256]{1,2,0:T(8,128)S(1)} fusion(f32[2,256,256]{2,1,0:T(8,128)S(1)} %copy-done.1, f32[1,256,256]{2,1,0:T(8,128)S(1)} %get-tuple-element.81, f32[1,256,256]{2,1,0:T(8,128)S(1)} %get-tuple-element.80), kind=kOutput, calls=%fused_computation.21 | convolution fusion | flops 402784256 | bytes 1310720 | tf_op jit(solution)/shard_map/...ji,...jk->...ik/dot_general | solution.py:21
  61.2 1.0 %convolution_bitcast_fusion.3 = f32[1,256,256]{1,2,0:T(8,128)S(1)} fusion(f32[512,256]{1,0:T(8,128)S(1)} %bitcast.249, f32[512,256]{1,0:T(8,128)S(1)} %bitcast.244), kind=kOutput, calls=%fused_computation.22 | convolution fusion | flops 402653184 | bytes 1310720 | tf_op jit(solution)/shard_map/...ji,...jk->...ik/dot_general | solution.py:21
  62.3 1.0 %fusion.43 = f32[2,512,256]{2,1,0:T(8,128)S(1)} fusion(f32[2,512,256]{2,1,0:T(8,128)S(1)} %bitcast.230, f32[1,2,256,256]{2,3,1,0:T(8,128)S(1)} %maximum_bitcast_fusion), kind=kOutput, calls=%fused_computation.111 | convolution fusion | flops 805306368 | bytes 2359296 | tf_op jit(solution)/shard_map/dot_general | solution.py:13
  63.3 1.0 %fusion.42 = f32[2,512,256]{2,1,0:T(8,128)S(1)} fusion(f32[2,512,256]{2,1,0:T(8,128)S(1)} %bitcast.231, f32[1,2,256,256]{2,3,1,0:T(8,128)S(1)} %maximum_bitcast_fusion), kind=kOutput, calls=%fused_computation.109 | convolution fusion | flops 805306368 | bytes 2359296 | tf_op jit(solution)/shard_map/dot_general | solution.py:13
  64.7 1.1 %fusion.57 = f32[2,512,256]{2,1,0:T(8,128)S(1)} fusion(f32[2,512,256]{2,1,0:T(8,128)S(1)} %bitcast.228, f32[2,512,256]{2,1,0:T(8,128)S(1)} %fusion.44, f32[2,512,256]{2,1,0:T(8,128)S(1)} %fusion.45), kind=kOutput, calls=%fused_computation.138 | convolution fusion | flops 805437440 | bytes 3145728 | tf_op jit(solution)/shard_map/...ij,...kj->...ik/dot_general | solution.py:17
  65.8 1.1 %fusion.59 = f32[2,512,256]{2,1,0:T(8,128)S(1)} fusion(f32[2,512,256]{2,1,0:T(8,128)S(1)} %bitcast.229, f32[2,512,256]{2,1,0:T(8,128)S(1)} %fusion.45, f32[2,512,256]{2,1,0:T(8,128)S(1)} %fusion.44), kind=kOutput, calls=%fused_computation.140 | convolution fusion | flops 805437440 | bytes 3145728 | tf_op jit(solution)/shard_map/...ij,...kj->...ik/dot_general | solution.py:17
  67.0 0.7 %copy.84 = f32[2,2,256,64]{2,3,1,0:T(8,128)} copy(f32[2,2,256,64]{2,3,0,1:T(8,128)S(1)} %pad_maximum_fusion.10) | data formatting | bytes 524288
  67.8 0.9 %subtract_reduce_fusion = (f32[4,2]{1,0:T(4,128)S(1)}, f32[4,2]{1,0:T(4,128)S(1)}) fusion(f32[2,256,256]{2,1,0:T(8,128)S(1)} %get-tuple-element.46, f32[4,256,256]{2,1,0:T(8,128)S(1)} %get-tuple-element.42, f32[2,256,256]{2,1,0:T(8,128)S(1)} %get-tuple-element.45, f32[4,256,256]{2,1,0:T(8,128)S(1)} %get-tuple-element.41), kind=kLoop, calls=%fused_computation.10 | loop fusion | flops 4194288 | bytes 3145792 | tf_op jit(solution)/shard_map/reduce_sum | solution.py:158
  68.8 1.3 %multiply_subtract_fusion = f32[4,2]{1,0:T(4,128)S(1)} fusion(f32[4,2]{1,0:T(4,128)S(1)} %get-tuple-element.33, f32[4,2]{1,0:T(4,128)S(1)} %get-tuple-element.32, f32[]{:T(128)} %get-tuple-element.35, f32[]{:T(128)} %get-tuple-element.34), kind=kLoop, calls=%fused_computation.156 | loop fusion | flops 24 | bytes 104 | tf_op jit(solution)/shard_map/sub | solution.py:159
  70.1 0.6 copy.83
  (64 shorter events, 4.9 us)
Async XLA Ops:
  1.4 2.4 %copy-start.6 = (f32[2,256,256]{2,1,0:T(8,128)S(1)}, f32[2,256,256]{2,1,0:T(8,128)}, u32[]{:S(2)}) copy-start(f32[2,256,256]{2,1,0:T(8,128)} %param.9) | copy-start | bytes 1572868
  17.6 4.6 %copy-start.4 = (f32[1,1,256,256]{3,2,0,1:T(8,128)}, f32[1,1,256,256]{3,2,0,1:T(8,128)S(1)}, u32[]{:S(2)}) copy-start(f32[1,1,256,256]{3,2,0,1:T(8,128)S(1)} %get-tuple-element.71) | copy-start | bytes 786436
  18.4 12.2 %collective-permute-start = (f32[2,128,256]{2,1,0:T(8,128)}, f32[2,128,256]{2,1,0:T(8,128)}, u32[]{:S(2)}, u32[]{:S(2)}) collective-permute-start(f32[2,128,256]{2,1,0:T(8,128)} %fusion.41), channel_id=1, source_target_pairs={{0,4},{4,8},{8,12},{12,0},{1,5},{5,9},{9,13},{13,1},{2,6},{6,10},{... | collective-permute-start | bytes 786440 | tf_op jit(solution)/shard_map/ppermute | solution.py:98
  19.7 22.1 %collective-permute-start.1 = (f32[2,128,256]{2,1,0:T(8,128)}, f32[2,128,256]{2,1,0:T(8,128)}, u32[]{:S(2)}, u32[]{:S(2)}) collective-permute-start(f32[2,128,256]{2,1,0:T(8,128)} %fusion.41), channel_id=1, source_target_pairs={{0,8},{4,12},{8,0},{12,4},{1,9},{5,13},{9,1},{13,5},{2,10},{6,14},... | collective-permute-start | bytes 786440 | tf_op jit(solution)/shard_map/ppermute | solution.py:98
  20.7 24.0 %collective-permute-start.2 = (f32[2,128,256]{2,1,0:T(8,128)}, f32[2,128,256]{2,1,0:T(8,128)}, u32[]{:S(2)}, u32[]{:S(2)}) collective-permute-start(f32[2,128,256]{2,1,0:T(8,128)} %fusion.41), channel_id=1, source_target_pairs={{0,12},{4,0},{8,4},{12,8},{1,13},{5,1},{9,5},{13,9},{2,14},{6,2},{... | collective-permute-start | bytes 786440 | tf_op jit(solution)/shard_map/ppermute | solution.py:98
  22.2 1.7 %copy-start = (f32[4,2,256,256]{3,2,1,0:T(8,128)S(1)}, f32[4,2,256,256]{3,2,1,0:T(8,128)}, u32[]{:S(2)}) copy-start(f32[4,2,256,256]{3,2,1,0:T(8,128)} %param.10) | copy-start | bytes 6291460
  30.6 16.3 %copy-start.5 = (f32[1,1,256,256]{3,2,0,1:T(8,128)S(1)}, f32[1,1,256,256]{3,2,0,1:T(8,128)}, u32[]{:S(2)}) copy-start(f32[1,1,256,256]{3,2,0,1:T(8,128)} %copy-done.4) | copy-start | bytes 786436
  44.8 2.1 %copy-start.2 = (f32[4,256,256]{1,2,0:T(8,128)S(1)}, f32[4,256,256]{1,2,0:T(8,128)}, u32[]{:S(2)}) copy-start(f32[4,256,256]{1,2,0:T(8,128)} %copy.80) | copy-start | bytes 3145732
  44.8 2.1 %copy-start.3 = (f32[4,1,256,256]{2,3,0,1:T(8,128)S(1)}, f32[4,1,256,256]{2,3,0,1:T(8,128)}, u32[]{:S(2)}) copy-start(f32[4,1,256,256]{2,3,0,1:T(8,128)} %copy.97) | copy-start | bytes 3145732
  46.2 2.5 %collective-permute-start.3 = (f32[3,2,128,256]{3,2,1,0:T(8,128)S(1)}, f32[3,2,128,256]{3,2,1,0:T(8,128)S(1)}, u32[]{:S(2)}, u32[]{:S(2)}) collective-permute-start(f32[3,2,128,256]{3,2,1,0:T(8,128)S(1)} %get-tuple-element.76), channel_id=1, source_target_pairs={{0,1},{1,0},{2,3},{3,2},{4,5},{5,4},{6,7},{7,6},{8,9},{9,8},{10,11... | collective-permute-start | bytes 2359304 | tf_op jit(solution)/shard_map/ppermute | solution.py:101
  56.7 2.2 %copy-start.1 = (f32[2,256,256]{2,1,0:T(8,128)S(1)}, f32[2,256,256]{2,1,0:T(8,128)}, u32[]{:S(2)}) copy-start(f32[2,256,256]{2,1,0:T(8,128)} %param.11) | copy-start | bytes 1572868

commit v6 on v5

--- a/solution.py
+++ b/solution.py
@@ -154,8 +154,11 @@
     weighted = cmul_adjoint_right(cmul(states, overlap[None]), states)
     control_real = (0.5 * (controls[:, 0] + jnp.swapaxes(controls[:, 0], 1, 2)))[:, None]
     control_imag = (0.5 * (controls[:, 1] - jnp.swapaxes(controls[:, 1], 1, 2)))[:, None]
-    trace_real = jnp.sum(control_real * weighted[None, :, 0] + control_imag * weighted[None, :, 1], axis=(2, 3))
-    trace_imag = jnp.sum(control_real * weighted[None, :, 1] - control_imag * weighted[None, :, 0], axis=(2, 3))
+    partial_real = jnp.sum(control_real * weighted[None, :, 0] + control_imag * weighted[None, :, 1], axis=2)
+    partial_imag = jnp.sum(control_real * weighted[None, :, 1] - control_imag * weighted[None, :, 0], axis=2)
+    partial_real, partial_imag = lax.optimization_barrier((partial_real, partial_imag))
+    trace_real = jnp.sum(partial_real, axis=-1)
+    trace_imag = jnp.sum(partial_imag, axis=-1)
     gradient = correlation_real * trace_imag - correlation_imag * trace_real
     propagators = cmul(jnp.stack(running, 0), lax.dynamic_slice_in_dim(prefix, col_start, col_width, 2)[None])
     return (gradient, propagators)

time: 71.1 us -> 70.9 us (level)
  no operation moved by 1% of the time
where the time goes in v6:
time: 70.9 us; the launch traced here: 70.5 us
  matrix products  24.6 us (35%)
  waiting for transfers between devices  15.6 us (22%)
  local copies, waits for them, and re-layouts  12.5 us (18%)
  other arithmetic  12.3 us (17%)
  starting transfers between devices  4.34 us (6%)
  between operations  1.31 us (2%)
    dot_general x18, matrix products, mm(): return jnp.matmul(left, right, precision=mode)  20.1 us
    ppermute x3, waiting for transfers between devices, shards(): received.append(lax.ppermute(mine, 'tm', pairs))  14.1 us
    unnamed x19, local copies, waits for them, and re-layouts  5.28 us
    ppermute x3, starting transfers between devices, shards(): received.append(lax.ppermute(mine, 'tm', pairs))  3.78 us
    squeeze x1, local copies, waits for them, and re-layouts, shards(): controls[:, 1] - jnp.swapaxes(controls[:, 1], 1, 2)  2.54 us
    dot_general x2, matrix products, mm_tn(): return jnp.einsum('...ji,...jk->...ik', left, right, precision=fast_mode)  2.27 us
    dot_general x2, matrix products, mm_nt(): return jnp.einsum('...ij,...kj->...ik', left, right, precision=fast_mode)  2.2 us
    reduce_sum x1, other arithmetic, shards(): jnp.sum(amplitudes[:, :, None, None, None] * controls[:, None], axis=0)  2.1 us
  transfers between devices with their start and end apart: 4, of which 3 were waited for; matrix products, arithmetic and copies ran while one was open for 12% of the time, Pallas kernels for 0%

profile of v6, /device:TPU:13, one launch (start us, length us, event | category | flops | bytes accessed | tf_op | source)
XLA Modules:
  0.0 70.5 jit_solution(18283029421999509500)
XLA Ops:
  0.6 0.8 %copy.85 = f32[4,2]{1,0:T(4,128)S(1)} copy(f32[4,2]{0,1:T(2,128)} %param.8) | data formatting | bytes 64 | tf_op args[0]
  1.4 2.1 %multiply_reduce_fusion = f32[2,2,256,256]{3,2,1,0:T(8,128)S(1)} fusion(f32[4,2,256,256]{3,2,1,0:T(8,128)} %param.10, f32[4,2]{1,0:T(4,128)S(1)} %copy.85), kind=kLoop, calls=%fused_computation | loop fusion | flops 1835008 | bytes 3145760 | tf_op jit(solution)/shard_map/reduce_sum | solution.py:80
  3.5 0.3 copy.86
  5.2 1.1 %fusion.54 = f32[2,512,256]{2,1,0:T(8,128)S(1)} fusion(f32[2,512,256]{2,1,0:T(8,128)S(1)} %bitcast.224, f32[2,256,256]{2,1,0:T(8,128)S(1)} %copy.87, f32[2,2,256,256]{2,3,0,1:T(8,128)S(1)} %broadcast_add_fusion), kind=kOutput, calls=%fused_computation.136 | convolution fusion | flops 805568512 | bytes 3145728 | tf_op jit(solution)/shard_map/dot_general | solution.py:13
  6.4 1.1 %fusion.38 = f32[2,512,256]{2,1,0:T(8,128)S(1)} fusion(f32[2,512,256]{2,1,0:T(8,128)S(1)} %bitcast.225, f32[2,256,256]{2,1,0:T(8,128)S(1)} %copy.89), kind=kOutput, calls=%fused_computation.104 | convolution fusion | flops 805568512 | bytes 2621440 | tf_op jit(solution)/shard_map/dot_general | solution.py:13
  7.8 2.0 %fusion.7 = f32[2,2,512,256]{3,2,1,0:T(8,128)S(1)} fusion(f32[1,2,2,256,256]{4,3,1,2,0:T(8,128)S(1)} %get-tuple-element.78, f32[1,2,512,256]{3,2,0,1:T(8,128)S(1)} %bitcast.238, f32[1,2,512,256]{3,2,0,1:T(8,128)S(1)} %bitcast.226), kind=kOutput, calls=%fused_computation.17 | convolution fusion | flops 1611137024 | bytes 4718592 | tf_op jit(solution)/shard_map/dot_general | solution.py:13
  9.8 2.0 %fusion.10 = f32[2,2,512,256]{3,2,1,0:T(8,128)S(1)} fusion(f32[1,2,2,256,256]{4,3,1,2,0:T(8,128)S(1)} %get-tuple-element.78, f32[1,2,512,256]{3,2,0,1:T(8,128)S(1)} %bitcast.239, f32[1,2,512,256]{3,2,0,1:T(8,128)S(1)} %bitcast.227), kind=kOutput, calls=%fused_computation.18 | convolution fusion | flops 1611137024 | bytes 4718592 | tf_op jit(solution)/shard_map/dot_general | solution.py:13
  11.8 0.3 fusion.15
  12.2 0.4 bitcast_add_fusion.1
  12.7 1.1 %fusion.27 = f32[2,512,256]{2,1,0:T(8,128)S(1)} fusion(f32[2,512,256]{2,1,0:T(8,128)S(1)} %bitcast.236, f32[2,2,256,256]{3,2,0,1:T(8,128)S(1)} %get-tuple-element.42), kind=kOutput, calls=%fused_computation.80 | convolution fusion | flops 805306368 | bytes 2621440 | tf_op jit(solution)/shard_map/dot_general | solution.py:13
  13.8 1.1 %fusion.29 = f32[2,512,256]{2,1,0:T(8,128)S(1)} fusion(f32[2,512,256]{2,1,0:T(8,128)S(1)} %bitcast.237, f32[2,2,256,256]{3,2,0,1:T(8,128)S(1)} %get-tuple-element.42, f32[256,256]{1,0:T(8,128)S(1)} %fusion.51), kind=kOutput, calls=%fused_computation.83 | convolution fusion | flops 805437440 | bytes 2883584 | tf_op jit(solution)/shard_map/dot_general | solution.py:13
  15.3 0.9 %fusion.76 = (f32[1,2,256,256]{3,2,0,1:T(8,128)}, f32[1,2,256,256]{3,2,0,1:T(8,128)S(1)}) fusion(f32[2,2,256,256]{3,2,0,1:T(8,128)S(1)} %maximum_add_fusion), kind=kLoop, calls=%fused_computation.168 | loop fusion | bytes 2097152 | tf_op jit(solution)/shard_map/slice | solution.py:86
  16.1 0.8 %convolution_bitcast_fusion.1 = f32[1,512,256]{2,1,0:T(8,128)S(1)} fusion(f32[512,256]{1,0:T(8,128)S(1)} %bitcast.245, f32[2,2,256,256]{3,2,0,1:T(8,128)S(1)} %maximum_add_fusion), kind=kOutput, calls=%fused_computation.20 | convolution fusion | flops 402653184 | bytes 1310720 | tf_op jit(solution)/shard_map/dot_general | solution.py:13
  16.9 0.6 convolution_bitcast_fusion
  17.6 0.8 %fusion.41 = f32[2,128,256]{2,1,0:T(8,128)} fusion(s32[]{:T(128)S(6)} %select_n.53, f32[1,1,256,256]{3,2,0,1:T(8,128)S(1)} %get-tuple-element.76, f32[1,1,256,256]{3,2,0,1:T(8,128)S(1)} %get-tuple-element.77), kind=kLoop, calls=%fused_computation.107 | loop fusion | flops 65536 | bytes 786436 | tf_op jit(solution)/shard_map/dynamic_slice | solution.py:93
  18.4 1.3 %collective-permute-start = (f32[2,128,256]{2,1,0:T(8,128)}, f32[2,128,256]{2,1,0:T(8,128)}, u32[]{:S(2)}, u32[]{:S(2)}) collective-permute-start(f32[2,128,256]{2,1,0:T(8,128)} %fusion.41), channel_id=1, source_target_pairs={{0,4},{4,8},{8,12},{12,0},{1,5},{5,9},{9,13},{13,1},{2,6},{6,10},{... | collective-permute-start | bytes 786440 | tf_op jit(solution)/shard_map/ppermute | solution.py:98
  19.7 1.0 %collective-permute-start.1 = (f32[2,128,256]{2,1,0:T(8,128)}, f32[2,128,256]{2,1,0:T(8,128)}, u32[]{:S(2)}, u32[]{:S(2)}) collective-permute-start(f32[2,128,256]{2,1,0:T(8,128)} %fusion.41), channel_id=1, source_target_pairs={{0,8},{4,12},{8,0},{12,4},{1,9},{5,13},{9,1},{13,5},{2,10},{6,14},... | collective-permute-start | bytes 786440 | tf_op jit(solution)/shard_map/ppermute | solution.py:98
  20.7 1.5 %collective-permute-start.2 = (f32[2,128,256]{2,1,0:T(8,128)}, f32[2,128,256]{2,1,0:T(8,128)}, u32[]{:S(2)}, u32[]{:S(2)}) collective-permute-start(f32[2,128,256]{2,1,0:T(8,128)} %fusion.41), channel_id=1, source_target_pairs={{0,12},{4,0},{8,4},{12,8},{1,13},{5,1},{9,5},{13,9},{2,14},{6,2},{... | collective-permute-start | bytes 786440 | tf_op jit(solution)/shard_map/ppermute | solution.py:98
  22.2 1.3 %maximum_maximum_fusion = f32[2,2,256,256]{3,2,0,1:T(8,128)S(1)} fusion(f32[1,1,256,256]{3,2,0,1:T(8,128)S(1)} %get-tuple-element.77, f32[1,1,256,256]{3,2,0,1:T(8,128)S(1)} %get-tuple-element.76, f32[1,2,256,256]{3,2,0,1:T(8,128)} %get-tuple-element.74), kind=kLoop, calls=%fused_computation.35 | loop fusion | flops 524288 | bytes 2097152 | tf_op jit(solution)/shard_map/stack | solution.py:149
  23.5 0.4 copy-done
  23.9 1.6 %fusion.73 = (f32[4,1,256,256]{3,2,1,0:T(8,128)}, f32[4,256,256]{2,1,0:T(8,128)}) fusion(f32[4,2,256,256]{3,2,1,0:T(8,128)S(1)} %copy-done), kind=kLoop, calls=%fused_computation.165 | loop fusion | bytes 4194304 | tf_op jit(solution)/shard_map/slice | solution.py:155
  25.5 2.5 %copy.110 = f32[4,256,256]{1,2,0:T(8,128)} copy(f32[4,256,256]{2,1,0:T(8,128)} %get-tuple-element.50) | data formatting | bytes 2097152 | tf_op jit(solution)/shard_map/squeeze | solution.py:156
  28.0 2.5 %copy.127 = f32[4,1,256,256]{2,3,0,1:T(8,128)} copy(f32[4,1,256,256]{3,2,1,0:T(8,128)} %get-tuple-element.49) | data formatting | bytes 2097152
  30.6 11.2 %collective-permute-done.1 = f32[2,128,256]{2,1,0:T(8,128)} collective-permute-done((f32[2,128,256]{2,1,0:T(8,128)}, f32[2,128,256]{2,1,0:T(8,128)}, u32[]{:S(2)}, u32[]{:S(2)}) %collective-permute-start.1) | collective-permute-done | bytes 262176 | tf_op jit(solution)/shard_map/ppermute | solution.py:98
  41.8 2.9 %collective-permute-done.2 = f32[2,128,256]{2,1,0:T(8,128)} collective-permute-done((f32[2,128,256]{2,1,0:T(8,128)}, f32[2,128,256]{2,1,0:T(8,128)}, u32[]{:S(2)}, u32[]{:S(2)}) %collective-permute-start.2) | collective-permute-done | bytes 262176 | tf_op jit(solution)/shard_map/ppermute | solution.py:98
  44.8 1.4 %pad_maximum_fusion.7 = (f32[3,2,128,256]{3,2,1,0:T(8,128)S(1)}, f32[3,2,256,256]{3,2,1,0:T(8,128)S(1)}) fusion(f32[1,2,128,256]{3,2,1,0:T(8,128)} %bitcast.42, f32[1,2,128,256]{3,2,1,0:T(8,128)} %bitcast.41, f32[1,2,128,256]{3,2,1,0:T(8,128)} %bitcast.40, f32[3,2,256,256]{3,2,1,0:T(8,128)S(1)} %broadcast_in_dim.92, s32[]{:T(128)S(6)} %select_n.53), kind=kLoop, calls=%fused_computation.48 | loop fusion | flops 393216 | bytes 2359300 | tf_op jit(solution)/shard_map/stack | solution.py:99
  46.2 0.6 collective-permute-start.3
  47.2 1.5 %collective-permute-done.3 = f32[3,2,128,256]{3,2,1,0:T(8,128)S(1)} collective-permute-done((f32[3,2,128,256]{3,2,1,0:T(8,128)S(1)}, f32[3,2,128,256]{3,2,1,0:T(8,128)S(1)}, u32[]{:S(2)}, u32[]{:S(2)}) %collective-permute-start.3) | collective-permute-done | bytes 786464 | tf_op jit(solution)/shard_map/ppermute | solution.py:101
  48.9 0.3 select_select_fusion
  49.5 1.1 %fusion.24 = f32[2,512,256]{2,1,0:T(8,128)S(1)} fusion(f32[2,512,256]{2,1,0:T(8,128)S(1)} %bitcast.232, f32[2,2,256,256]{3,2,0,1:T(8,128)S(1)} %get-tuple-element.63), kind=kOutput, calls=%fused_computation.71 | convolution fusion | flops 805306368 | bytes 2621440 | tf_op jit(solution)/shard_map/dot_general | solution.py:13
  50.6 1.1 %fusion.23 = f32[2,512,256]{2,1,0:T(8,128)S(1)} fusion(f32[2,512,256]{2,1,0:T(8,128)S(1)} %bitcast.233, f32[2,2,256,256]{3,2,0,1:T(8,128)S(1)} %get-tuple-element.63), kind=kOutput, calls=%fused_computation.69 | convolution fusion | flops 805306368 | bytes 2621440 | tf_op jit(solution)/shard_map/dot_general | solution.py:13
  52.2 1.0 %fusion.46 = f32[2,512,256]{2,1,0:T(8,128)S(1)} fusion(f32[2,512,256]{2,1,0:T(8,128)S(1)} %bitcast.234, f32[2,256,256]{2,1,0:T(8,128)S(1)} %get-tuple-element.62), kind=kOutput, calls=%fused_computation.117 | convolution fusion | flops 805306368 | bytes 2359296 | tf_op jit(solution)/shard_map/dot_general | solution.py:13
  53.2 1.0 %fusion.47 = f32[2,512,256]{2,1,0:T(8,128)S(1)} fusion(f32[2,512,256]{2,1,0:T(8,128)S(1)} %bitcast.235, f32[2,256,256]{2,1,0:T(8,128)S(1)} %get-tuple-element.61), kind=kOutput, calls=%fused_computation.119 | convolution fusion | flops 805306368 | bytes 2359296 | tf_op jit(solution)/shard_map/dot_general | solution.py:13
  54.6 1.0 %fusion.45 = f32[2,512,256]{2,1,0:T(8,128)S(1)} fusion(f32[2,512,256]{2,1,0:T(8,128)S(1)} %bitcast.220, f32[4,2,256,256]{3,2,0,1:T(8,128)S(1)} %fusion.1, s32[]{:T(128)S(6)} %select_n.61), kind=kOutput, calls=%fused_computation.115 | convolution fusion | flops 805306368 | bytes 2359300 | tf_op jit(solution)/shard_map/dot_general | solution.py:13
  55.6 1.2 %fusion.64 = f32[2,512,64]{1,2,0:T(8,128)S(1)} fusion(f32[2,512,256]{2,1,0:T(8,128)S(1)} %bitcast.221, f32[4,2,256,256]{3,2,0,1:T(8,128)S(1)} %fusion.1, s32[]{:T(128)S(6)} %select_n.62, s32[]{:T(128)S(6)} %select_n.64), kind=kOutput, calls=%fused_computation.149 | convolution fusion | flops 201326592 | bytes 1441800 | tf_op jit(solution)/shard_map/dot_general | solution.py:13
  56.7 1.2 %fusion.63 = f32[2,512,64]{1,2,0:T(8,128)S(1)} fusion(f32[2,512,256]{2,1,0:T(8,128)S(1)} %bitcast.222, f32[4,2,256,256]{3,2,0,1:T(8,128)S(1)} %fusion.1, s32[]{:T(128)S(6)} %select_n.62, s32[]{:T(128)S(6)} %add.149, s32[]{:T(128)S(6)} %select_n.64), kind=kOutput, calls=%fused_computation.147 | convolution fusion | flops 201326592 | bytes 1441804 | tf_op jit(solution)/shard_map/dot_general | solution.py:13
  57.9 1.0 %fusion.44 = f32[2,512,256]{2,1,0:T(8,128)S(1)} fusion(f32[2,512,256]{2,1,0:T(8,128)S(1)} %bitcast.223, f32[4,2,256,256]{3,2,0,1:T(8,128)S(1)} %fusion.1, s32[]{:T(128)S(6)} %select_n.61, s32[]{:T(128)S(6)} %add.149), kind=kOutput, calls=%fused_computation.113 | convolution fusion | flops 805306368 | bytes 2359304 | tf_op jit(solution)/shard_map/dot_general | solution.py:13
  58.9 0.7 %add_reduce_fusion.1 = (f32[]{:T(128)}, f32[]{:T(128)}, f32[1,256,256]{2,1,0:T(8,128)S(1)}, f32[1,256,256]{2,1,0:T(8,128)S(1)}) fusion(f32[2,256,256]{2,1,0:T(8,128)S(1)} %copy-done.1, f32[2,256,256]{2,1,0:T(8,128)S(1)} %get-tuple-element.60, f32[2,256,256]{2,1,0:T(8,128)S(1)} %get-tuple-element.59), kind=kLoop, calls=%fused_computation.129 | loop fusion | flops 589822 | bytes 1572872 | tf_op jit(solution)/shard_map/reduce_sum | solution.py:152
  60.0 1.2 %convolution_bitcast_fusion.2 = f32[1,256,256]{1,2,0:T(8,128)S(1)} fusion(f32[2,256,256]{2,1,0:T(8,128)S(1)} %copy-done.1, f32[1,256,256]{2,1,0:T(8,128)S(1)} %get-tuple-element.87, f32[1,256,256]{2,1,0:T(8,128)S(1)} %get-tuple-element.86), kind=kOutput, calls=%fused_computation.21 | convolution fusion | flops 402784256 | bytes 1310720 | tf_op jit(solution)/shard_map/...ji,...jk->...ik/dot_general | solution.py:21
  61.2 1.0 %convolution_bitcast_fusion.3 = f32[1,256,256]{1,2,0:T(8,128)S(1)} fusion(f32[512,256]{1,0:T(8,128)S(1)} %bitcast.249, f32[512,256]{1,0:T(8,128)S(1)} %bitcast.244), kind=kOutput, calls=%fused_computation.22 | convolution fusion | flops 402653184 | bytes 1310720 | tf_op jit(solution)/shard_map/...ji,...jk->...ik/dot_general | solution.py:21
  62.3 1.0 %fusion.43 = f32[2,512,256]{2,1,0:T(8,128)S(1)} fusion(f32[2,512,256]{2,1,0:T(8,128)S(1)} %bitcast.230, f32[1,2,256,256]{2,3,1,0:T(8,128)S(1)} %maximum_bitcast_fusion), kind=kOutput, calls=%fused_computation.111 | convolution fusion | flops 805306368 | bytes 2359296 | tf_op jit(solution)/shard_map/dot_general | solution.py:13
  63.3 1.0 %fusion.42 = f32[2,512,256]{2,1,0:T(8,128)S(1)} fusion(f32[2,512,256]{2,1,0:T(8,128)S(1)} %bitcast.231, f32[1,2,256,256]{2,3,1,0:T(8,128)S(1)} %maximum_bitcast_fusion), kind=kOutput, calls=%fused_computation.109 | convolution fusion | flops 805306368 | bytes 2359296 | tf_op jit(solution)/shard_map/dot_general | solution.py:13
  64.7 1.1 %fusion.57 = f32[2,512,256]{2,1,0:T(8,128)S(1)} fusion(f32[2,512,256]{2,1,0:T(8,128)S(1)} %bitcast.228, f32[2,512,256]{2,1,0:T(8,128)S(1)} %fusion.44, f32[2,512,256]{2,1,0:T(8,128)S(1)} %fusion.45), kind=kOutput, calls=%fused_computation.138 | convolution fusion | flops 805437440 | bytes 3145728 | tf_op jit(solution)/shard_map/...ij,...kj->...ik/dot_general | solution.py:17
  65.8 1.1 %fusion.59 = f32[2,512,256]{2,1,0:T(8,128)S(1)} fusion(f32[2,512,256]{2,1,0:T(8,128)S(1)} %bitcast.229, f32[2,512,256]{2,1,0:T(8,128)S(1)} %fusion.45, f32[2,512,256]{2,1,0:T(8,128)S(1)} %fusion.44), kind=kOutput, calls=%fused_computation.140 | convolution fusion | flops 805437440 | bytes 3145728 | tf_op jit(solution)/shard_map/...ij,...kj->...ik/dot_general | solution.py:17
  67.0 0.7 %copy.114 = f32[2,2,256,64]{2,3,1,0:T(8,128)} copy(f32[2,2,256,64]{2,3,0,1:T(8,128)S(1)} %pad_maximum_fusion.10) | data formatting | bytes 524288
  67.8 0.6 subtract_reduce_fusion
  68.6 1.3 %multiply_subtract_fusion = f32[4,2]{1,0:T(4,128)S(1)} fusion(f32[4,2]{1,0:T(4,128)S(1)} %reduce_sum.69, f32[4,2]{1,0:T(4,128)S(1)} %reduce_sum.67, f32[]{:T(128)} %get-tuple-element.41, f32[]{:T(128)} %get-tuple-element.40), kind=kLoop, calls=%fused_computation.156 | loop fusion | flops 24 | bytes 104 | tf_op jit(solution)/shard_map/sub | solution.py:162
  69.9 0.6 copy.113
  (66 shorter events, 5.1 us)
Async XLA Ops:
  1.4 2.4 %copy-start.6 = (f32[2,256,256]{2,1,0:T(8,128)S(1)}, f32[2,256,256]{2,1,0:T(8,128)}, u32[]{:S(2)}) copy-start(f32[2,256,256]{2,1,0:T(8,128)} %param.9) | copy-start | bytes 1572868
  17.6 4.6 %copy-start.4 = (f32[1,1,256,256]{3,2,0,1:T(8,128)}, f32[1,1,256,256]{3,2,0,1:T(8,128)S(1)}, u32[]{:S(2)}) copy-start(f32[1,1,256,256]{3,2,0,1:T(8,128)S(1)} %get-tuple-element.77) | copy-start | bytes 786436
  18.4 12.2 %collective-permute-start = (f32[2,128,256]{2,1,0:T(8,128)}, f32[2,128,256]{2,1,0:T(8,128)}, u32[]{:S(2)}, u32[]{:S(2)}) collective-permute-start(f32[2,128,256]{2,1,0:T(8,128)} %fusion.41), channel_id=1, source_target_pairs={{0,4},{4,8},{8,12},{12,0},{1,5},{5,9},{9,13},{13,1},{2,6},{6,10},{... | collective-permute-start | bytes 786440 | tf_op jit(solution)/shard_map/ppermute | solution.py:98
  19.7 22.1 %collective-permute-start.1 = (f32[2,128,256]{2,1,0:T(8,128)}, f32[2,128,256]{2,1,0:T(8,128)}, u32[]{:S(2)}, u32[]{:S(2)}) collective-permute-start(f32[2,128,256]{2,1,0:T(8,128)} %fusion.41), channel_id=1, source_target_pairs={{0,8},{4,12},{8,0},{12,4},{1,9},{5,13},{9,1},{13,5},{2,10},{6,14},... | collective-permute-start | bytes 786440 | tf_op jit(solution)/shard_map/ppermute | solution.py:98
  20.7 24.0 %collective-permute-start.2 = (f32[2,128,256]{2,1,0:T(8,128)}, f32[2,128,256]{2,1,0:T(8,128)}, u32[]{:S(2)}, u32[]{:S(2)}) collective-permute-start(f32[2,128,256]{2,1,0:T(8,128)} %fusion.41), channel_id=1, source_target_pairs={{0,12},{4,0},{8,4},{12,8},{1,13},{5,1},{9,5},{13,9},{2,14},{6,2},{... | collective-permute-start | bytes 786440 | tf_op jit(solution)/shard_map/ppermute | solution.py:98
  22.2 1.7 %copy-start = (f32[4,2,256,256]{3,2,1,0:T(8,128)S(1)}, f32[4,2,256,256]{3,2,1,0:T(8,128)}, u32[]{:S(2)}) copy-start(f32[4,2,256,256]{3,2,1,0:T(8,128)} %param.10) | copy-start | bytes 6291460
  30.6 16.3 %copy-start.5 = (f32[1,1,256,256]{3,2,0,1:T(8,128)S(1)}, f32[1,1,256,256]{3,2,0,1:T(8,128)}, u32[]{:S(2)}) copy-start(f32[1,1,256,256]{3,2,0,1:T(8,128)} %copy-done.4) | copy-start | bytes 786436
  44.8 2.1 %copy-start.2 = (f32[4,256,256]{1,2,0:T(8,128)S(1)}, f32[4,256,256]{1,2,0:T(8,128)}, u32[]{:S(2)}) copy-start(f32[4,256,256]{1,2,0:T(8,128)} %copy.110) | copy-start | bytes 3145732
  44.8 2.1 %copy-start.3 = (f32[4,1,256,256]{2,3,0,1:T(8,128)S(1)}, f32[4,1,256,256]{2,3,0,1:T(8,128)}, u32[]{:S(2)}) copy-start(f32[4,1,256,256]{2,3,0,1:T(8,128)} %copy.127) | copy-start | bytes 3145732
  46.2 2.5 %collective-permute-start.3 = (f32[3,2,128,256]{3,2,1,0:T(8,128)S(1)}, f32[3,2,128,256]{3,2,1,0:T(8,128)S(1)}, u32[]{:S(2)}, u32[]{:S(2)}) collective-permute-start(f32[3,2,128,256]{3,2,1,0:T(8,128)S(1)} %get-tuple-element.82), channel_id=1, source_target_pairs={{0,1},{1,0},{2,3},{3,2},{4,5},{5,4},{6,7},{7,6},{8,9},{9,8},{10,11... | collective-permute-start | bytes 2359304 | tf_op jit(solution)/shard_map/ppermute | solution.py:101
  56.7 2.2 %copy-start.1 = (f32[2,256,256]{2,1,0:T(8,128)S(1)}, f32[2,256,256]{2,1,0:T(8,128)}, u32[]{:S(2)}) copy-start(f32[2,256,256]{2,1,0:T(8,128)} %param.11) | copy-start | bytes 1572868
